TPU v7x, 256 devices: a whole 4x4x8 slice. The times are simulated.
256 devices in a mesh: nodes: 64 (over z, y, core), mp: 4 (over x).
Axes of the slice: x: 4, y: 4, z: 8, core: 2. Of those that a mesh axis runs over, the one named last changes fastest.
Arguments:
- event_feats: bfloat16 [65536, 512], P('nodes'), may hold values from -6 to 6
- event_owner: int32 [65536, 1], P('nodes'), may hold values from 0 to 63; in each aligned block of 1024 rows (0 to 1023, 1024 to 2047, ...) at most 32 rows name the same one
- event_slot: int32 [65536], P('nodes'), may hold values from 0 to 255
- memory: bfloat16 [16384, 1024], P('nodes'), may hold values from -6 to 6
- w_msg_event: bfloat16 [512, 2048], P(None, 'mp'), may hold values from -0.25 to 0.25
- w_msg_state: bfloat16 [1024, 2048], P(None, 'mp'), may hold values from -0.1875 to 0.1875
- b_msg: float32 [2048], P('mp'), may hold values from -3 to 3
- w_msg_out: bfloat16 [2048, 1024], P('mp'), may hold values from -0.125 to 0.125
- b_out: float32 [1024], replicated, may hold values from -3 to 3
- w_input: bfloat16 [3, 1024, 1024], P(None, None, 'mp'), may hold values from -0.1875 to 0.1875
- w_hidden: bfloat16 [3, 1024, 1024], P(None, None, 'mp'), may hold values from -0.1875 to 0.1875
- b_input: float32 [3, 1024], P(None, 'mp'), may hold values from -3 to 3
- b_hidden: float32 [3, 1024], P(None, 'mp'), may hold values from -3 to 3
- state_slots: int32 [4096, 32], P('nodes'), may hold values from 0 to 255
- neighbours: int32 [16384, 10], P('nodes'), may hold values from 0 to 2047
- query_slots: int32 [16384], P('nodes'), may hold values from 0 to 255
- w_neigh: bfloat16 [1024, 1024], P('mp'), may hold values from -0.1875 to 0.1875
- w_self: bfloat16 [1024, 1024], P('mp'), may hold values from -0.1875 to 0.1875
- b_embed: float32 [1024], replicated, may hold values from -3 to 3
Outputs:
- new_memory: bfloat16 [16384, 1024], P('nodes', 'mp')
- embedding: bfloat16 [16384, 1024], P(('nodes', 'mp'))
Inputs may be any that keep to these rules, and one draw needn't show every extreme that they name: `event_owner`: among the 1024 events of one block of events, at most 32 name the same owner, and in every draw some owner is named exactly 32 times by some block.
All inputs are finite; a program needn't handle non-finite values.
Results may differ from a plain program's by a relative error of at most 0.014.
Values may be sent and summed in bfloat16 or wider, within the bound.
No kernel may reach another device: no remote copies, remote signals or barrier semaphores. Data moves between devices by JAX's collectives and lax.ppermute only.
A program may use at most 64 MiB of HBM per device.

v0:
```python
import jax
import jax.numpy as jnp
from jax import lax
from jax.sharding import PartitionSpec as P


def per_device(
    event_feats,
    event_owner,
    event_slot,
    memory,
    w_msg_event,
    w_msg_state,
    b_msg,
    w_msg_out,
    b_out,
    w_input,
    w_hidden,
    b_input,
    b_hidden,
    state_slots,
    neighbours,
    query_slots,
    w_neigh,
    w_self,
    b_embed,
):
    owner_count = lax.axis_size("nodes")
    share_count = lax.axis_size("mp")
    mp_index = lax.axis_index("mp")
    event_rows = event_feats.shape[0]
    feat_width = event_feats.shape[1]
    mem_rows = memory.shape[0]
    mem_width = memory.shape[1]
    col_share = mem_width // share_count
    capacity = 2 * event_rows // owner_count
    owner = event_owner[:, 0]
    match = (owner[:, None] == lax.broadcasted_iota(jnp.int32, (1, owner_count), 1)).astype(
        jnp.int32
    )
    before = jnp.cumsum(match, axis=0) - match
    place = jnp.sum(before * match, axis=1)
    target = owner * capacity + place
    id_buffer = jnp.full((owner_count * capacity,), -1, jnp.int32).at[target].set(event_slot)
    id_buffer = id_buffer.reshape(owner_count, capacity)
    feat_buffer = (
        jnp.zeros((owner_count * capacity, feat_width), jnp.bfloat16).at[target].set(event_feats)
    )
    feat_buffer = feat_buffer.reshape(owner_count, capacity, feat_width)
    arrived = lax.all_to_all(feat_buffer, "nodes", split_axis=0, concat_axis=0, tiled=True)
    arrived_ids = lax.all_to_all(id_buffer, "nodes", split_axis=0, concat_axis=0, tiled=True)
    recv_rows = owner_count * capacity
    arrived = arrived.reshape(recv_rows, feat_width)
    arrived_ids = arrived_ids.reshape(recv_rows)
    valid = arrived_ids >= 0
    safe_ids = jnp.where(valid, arrived_ids, 0)
    segment_ids = jnp.where(valid, arrived_ids, mem_rows)
    state_proj = jnp.dot(memory, w_msg_state, preferred_element_type=jnp.float32)
    pre = (
        jnp.dot(arrived, w_msg_event, preferred_element_type=jnp.float32)
        + jnp.take(state_proj, safe_ids, axis=0)
        + b_msg
    )
    hidden_msg = jax.nn.relu(pre).astype(jnp.bfloat16)
    partial_msg = jnp.dot(hidden_msg, w_msg_out, preferred_element_type=jnp.float32)
    partial_total = jax.ops.segment_sum(partial_msg, segment_ids, num_segments=mem_rows + 1)[
        :mem_rows
    ]
    counts = jax.ops.segment_sum(valid.astype(jnp.float32), segment_ids, num_segments=mem_rows + 1)[
        :mem_rows
    ]
    divisor = jnp.maximum(counts, 1.0)[:, None]
    msg_total = lax.psum(partial_total.astype(jnp.bfloat16), "mp").astype(jnp.float32)
    aggregate = (msg_total / divisor + b_out).astype(jnp.bfloat16)
    gates_in = (
        jnp.einsum("nd,gdc->gnc", aggregate, w_input, preferred_element_type=jnp.float32)
        + b_input[:, None, :]
    )
    gates_st = (
        jnp.einsum("nd,gdc->gnc", memory, w_hidden, preferred_element_type=jnp.float32)
        + b_hidden[:, None, :]
    )
    reset_gate = jax.nn.sigmoid(gates_in[0] + gates_st[0])
    update_gate = jax.nn.sigmoid(gates_in[1] + gates_st[1])
    candidate = jnp.tanh(gates_in[2] + reset_gate * gates_st[2])
    old_state = lax.dynamic_slice_in_dim(memory, mp_index * col_share, col_share, 1).astype(
        jnp.float32
    )
    updated = (1.0 - update_gate) * candidate + update_gate * old_state
    new_memory = jnp.where((counts > 0.0)[:, None], updated, old_state).astype(jnp.bfloat16)
    outgoing = jnp.take(new_memory, state_slots, axis=0)
    relayed = lax.all_to_all(outgoing, "nodes", split_axis=0, concat_axis=0, tiled=True)
    relayed = relayed.reshape(relayed.shape[0] * relayed.shape[1], col_share)
    neigh_rows = jnp.take(relayed, neighbours, axis=0).astype(jnp.float32)
    neigh_mean = (jnp.sum(neigh_rows, axis=1) / neighbours.shape[1]).astype(jnp.bfloat16)
    self_state = jnp.take(new_memory, query_slots, axis=0)
    summed = lax.psum_scatter(
        (
            jnp.dot(neigh_mean, w_neigh, preferred_element_type=jnp.float32)
            + jnp.dot(self_state, w_self, preferred_element_type=jnp.float32)
        ).astype(jnp.bfloat16),
        "mp",
        scatter_dimension=0,
        tiled=True,
    ).astype(jnp.float32)
    embedding = jax.nn.relu(summed + b_embed).astype(jnp.bfloat16)
    return (new_memory, embedding)


def solution(mesh):
    in_specs = (
        P("nodes", None),
        P("nodes", None),
        P("nodes"),
        P("nodes", None),
        P(None, "mp"),
        P(None, "mp"),
        P("mp"),
        P("mp", None),
        P(),
        P(None, None, "mp"),
        P(None, None, "mp"),
        P(None, "mp"),
        P(None, "mp"),
        P("nodes", None),
        P("nodes", None),
        P("nodes"),
        P("mp", None),
        P("mp", None),
        P(),
    )
    out_specs = (P("nodes", "mp"), P(("nodes", "mp"), None))
    return jax.shard_map(
        per_device, mesh=mesh, in_specs=in_specs, out_specs=out_specs, check_vma=False
    )
```

profile of v0, /device:TPU:1, one launch (start us, length us, event | category | flops | bytes accessed | tf_op | source)
XLA Modules:
  0.0 280.0 jit_solution(5040244256541828532)
XLA Ops:
  8.0 18.0 %reduce-window.6 = s32[64,8,128]{2,1,0:T(8,128)S(1)} reduce-window(s32[64,8,128]{2,1,0:T(8,128)S(1)} %fusion.31, s32[]{:T(128)} %constant.48.clone.1), window={size=1x1x128 pad=0_0x0_0x127_0}, to_apply=%region_0.0 | reduce-window | flops 8323072 | bytes 524292 | tf_op jit(solution)/shard_map/reduce-window
  26.7 4.5 %scatter_custom_fusion = s32[2048]{0:T(1024)S(1)} fusion(s32[1024]{0:T(1024)S(1)} %bitcast.71, s32[1024]{0:T(1024)} %param.21, s32[]{:T(128)} %constant.46.clone.1), kind=kCustom, calls=%fused_computation.79 | custom fusion | bytes 8704 | tf_op jit(solution)/shard_map/scatter | solution.py:44
  31.9 13.1 %all-to-all-start = ((s32[64,1,32]{2,1,0:T(1,128)}), s32[64,1,32]{2,1,0:T(1,128)S(1)}, u32[]{:S(2)}, u32[]{:S(2)}) async-start(s32[64,1,32]{2,1,0:T(1,128)} %bitcast.6), calls=%async_computation | async-start | bytes 65536 | tf_op jit(solution)/shard_map/all_to_all | solution.py:51
  45.0 7.2 %scatter_custom_fusion.2 = bf16[2048,512]{1,0:T(8,128)(2,1)} fusion(s32[1024]{0:T(1024)S(1)} %bitcast.72, bf16[1024,512]{1,0:T(8,128)(2,1)} %param.19, bf16[]{:T(256)} %constant.58.clone.1), kind=kCustom, calls=%fused_computation.18 | custom fusion | bytes 2097664 | tf_op jit(solution)/shard_map/scatter | solution.py:47
  52.2 2.1 all-to-all-done
  54.3 8.5 %all-to-all-start.1 = ((bf16[64,32,512]{2,1,0:T(8,128)(2,1)}), bf16[64,32,512]{2,1,0:T(8,128)(2,1)}, u32[]{:S(2)}, u32[]{:S(2)}) async-start(bf16[64,32,512]{2,1,0:T(8,128)(2,1)} %bitcast.60), calls=%async_computation.1 | async-start | bytes 4194304 | tf_op jit(solution)/shard_map/all_to_all | solution.py:50
  63.3 1.5 fusion.45
  64.8 1.6 fusion.1
  67.9 9.0 %gather_fusion = f32[2048,512]{1,0:T(8,128)} fusion(f32[256,512]{1,0:T(8,128)S(1)} %fusion.45, s32[2048]{0:T(1024)S(1)} %broadcast_clamp_fusion.1), kind=kCustom, calls=%fused_computation | custom fusion | bytes 8396800 | tf_op jit(solution)/shard_map/jit(_take)/gather | solution.py:61
  76.8 35.6 %all-to-all-done.1 = bf16[64,32,512]{2,1,0:T(8,128)(2,1)} async-done(((bf16[64,32,512]{2,1,0:T(8,128)(2,1)}), bf16[64,32,512]{2,1,0:T(8,128)(2,1)}, u32[]{:S(2)}, u32[]{:S(2)}) %all-to-all-start.1) | async-done | bytes 2097184 | tf_op jit(solution)/shard_map/all_to_all | solution.py:50
  112.5 7.9 %fusion.5 = f32[2048,1024]{1,0:T(8,128)} fusion(bf16[512,1024]{1,0:T(8,128)(2,1)} %param.26, f32[2048,512]{1,0:T(8,128)} %gather_fusion, bf16[2048,512]{1,0:T(8,128)(2,1)} %bitcast.9, bf16[512,512]{1,0:T(8,128)(2,1)S(1)} %copy-done.10, f32[512]{0:T(512)S(1)} %copy-done.14, pred[2048]{0:T(1024)(128)(4,1)S(1)} %get-tuple-element.3), kind=kOutput, calls=%fused_computation.21 | convolution fusion | flops 3226468352 | bytes 16257024 | tf_op jit(solution)/shard_map/dot_general | solution.py:65
  120.3 19.2 %scatter_custom_fusion.3 = f32[257,1024]{1,0:T(8,128)S(1)} fusion(s32[2048]{0:T(1024)S(1)} %bitcast.69, f32[2048,1024]{1,0:T(8,128)} %fusion.5, f32[]{:T(128)} %constant.39.clone.1), kind=kCustom, calls=%fused_computation.22 | custom fusion | flops 2097152 | bytes 1053184 | tf_op jit(solution)/shard_map/scatter-add | solution.py:66
  140.6 14.7 %scatter_custom_fusion.1 = f32[257]{0:T(512)S(1)} fusion(s32[2048]{0:T(1024)S(1)} %bitcast.70, f32[2048]{0:T(1024)S(1)} %get-tuple-element.2, f32[]{:T(128)} %constant.39.clone.1), kind=kCustom, calls=%fused_computation.83 | custom fusion | flops 2048 | bytes 1032 | tf_op jit(solution)/shard_map/scatter-add | solution.py:69
  155.3 29.0 %all-reduce.2.cloned.1.call-done = bf16[256,1024]{1,0:T(8,128)(2,1)} async-done(((bf16[256,1024]{1,0:T(8,128)(2,1)}), bf16[256,1024]{1,0:T(8,128)(2,1)}) %all-reduce.2.cloned.1.call-update) | async-done | bytes 524304 | tf_op jit(solution)/shard_map/psum | solution.py:73
  184.3 2.2 fusion.2
  187.6 7.5 %gather_fusion.1 = bf16[2048,256]{1,0:T(8,128)(2,1)S(1)} fusion(bf16[256,256]{1,0:T(8,128)(2,1)S(1)} %fusion.14, s32[2048]{0:T(1024)S(1)} %broadcast_clamp_fusion), kind=kCustom, calls=%fused_computation.1 | custom fusion | bytes 2105344 | tf_op jit(solution)/shard_map/jit(_take)/gather | solution.py:91
  195.1 1.3 broadcast_select_fusion
  196.4 12.9 %all-to-all-start.2 = ((bf16[64,32,256]{2,1,0:T(8,128)(2,1)}), bf16[64,32,256]{2,1,0:T(8,128)(2,1)S(1)}, u32[]{:S(2)}, u32[]{:S(2)}) async-start(bf16[64,32,256]{2,1,0:T(8,128)(2,1)} %broadcast_select_fusion), calls=%async_computation.2 | async-start | bytes 2097152 | tf_op jit(solution)/shard_map/all_to_all | solution.py:92
  211.2 26.2 %all-to-all-done.2 = bf16[64,32,256]{2,1,0:T(8,128)(2,1)S(1)} async-done(((bf16[64,32,256]{2,1,0:T(8,128)(2,1)}), bf16[64,32,256]{2,1,0:T(8,128)(2,1)S(1)}, u32[]{:S(2)}, u32[]{:S(2)}) %all-to-all-start.2) | async-done | bytes 1048608 | tf_op jit(solution)/shard_map/all_to_all | solution.py:92
  237.5 8.1 %gather_fusion.2 = bf16[2560,256]{1,0:T(8,128)(2,1)} fusion(bf16[2048,256]{1,0:T(8,128)(2,1)S(1)} %bitcast.59, s32[3072]{0:T(1024)S(1)} %pad_clamp_fusion), kind=kCustom, calls=%fused_computation.2 | custom fusion | bytes 2631680 | tf_op jit(solution)/shard_map/jit(_take)/gather | solution.py:94
  245.6 3.6 %reshape.152 = bf16[256,10,256]{2,1,0:T(8,128)(2,1)} reshape(bf16[2560,256]{1,0:T(8,128)(2,1)} %gather_fusion.2) | data formatting | bytes 2621440 | tf_op jit(solution)/shard_map/jit(_take)/gather | solution.py:94
  249.2 2.7 convert_reduce_fusion
  253.5 18.1 %reduce-scatter.2.cloned.1.call-done = bf16[64,1024]{1,0:T(8,128)(2,1)} async-done(((bf16[256,1024]{1,0:T(8,128)(2,1)}), bf16[64,1024]{1,0:T(8,128)(2,1)}) %reduce-scatter.2.cloned.1.call-update) | async-done | bytes 131088 | tf_op jit(solution)/shard_map/reduce_scatter | solution.py:97
  271.6 1.6 maximum_convert_fusion.1
  (73 shorter events, 9.5 us)
Async XLA Ops:
  7.2 57.6 %copy-start = (bf16[3,1024,256]{2,1,0:T(8,128)(2,1)S(1)}, bf16[3,1024,256]{2,1,0:T(8,128)(2,1)}, u32[]{:S(2)}) copy-start(bf16[3,1024,256]{2,1,0:T(8,128)(2,1)} %param.29) | copy-start | bytes 4718596
  7.2 19.4 %copy-start.7 = (s32[1024,1]{0,1:T(1,128)S(1)}, s32[1024,1]{0,1:T(1,128)}, u32[]{:S(2)}) copy-start(s32[1024,1]{0,1:T(1,128)} %param.20) | copy-start | bytes 12292
  31.9 22.5 %all-to-all-start = ((s32[64,1,32]{2,1,0:T(1,128)}), s32[64,1,32]{2,1,0:T(1,128)S(1)}, u32[]{:S(2)}, u32[]{:S(2)}) async-start(s32[64,1,32]{2,1,0:T(1,128)} %bitcast.6), calls=%async_computation | async-start | bytes 65536 | tf_op jit(solution)/shard_map/all_to_all | solution.py:51
  54.3 8.7 %copy-start.5 = (s32[64,32]{0,1:T(8,128)S(1)}, s32[64,32]{0,1:T(8,128)}, u32[]{:S(2)}) copy-start(s32[64,32]{0,1:T(8,128)} %param.32) | copy-start | bytes 24580
  54.3 8.9 %copy-start.2 = (bf16[1024,512]{1,0:T(8,128)(2,1)S(1)}, bf16[1024,512]{1,0:T(8,128)(2,1)}, u32[]{:S(2)}) copy-start(bf16[1024,512]{1,0:T(8,128)(2,1)} %param.24) | copy-start | bytes 3145732
  54.3 58.1 %all-to-all-start.1 = ((bf16[64,32,512]{2,1,0:T(8,128)(2,1)}), bf16[64,32,512]{2,1,0:T(8,128)(2,1)}, u32[]{:S(2)}, u32[]{:S(2)}) async-start(bf16[64,32,512]{2,1,0:T(8,128)(2,1)} %bitcast.60), calls=%async_computation.1 | async-start | bytes 4194304 | tf_op jit(solution)/shard_map/all_to_all | solution.py:50
  62.8 1.9 copy-start.11
  62.8 121.4 %all-reduce.2.cloned.1.call-start = ((), (), s32[]{:S(2)}) async-start(), calls=%async_computation.4 | async-start | bytes 1048576 | tf_op jit(solution)/shard_map/psum | solution.py:73
  67.8 44.6 %copy-start.10 = (bf16[512,512]{1,0:T(8,128)(2,1)S(1)}, bf16[512,512]{1,0:T(8,128)(2,1)}, u32[]{:S(2)}) copy-start(bf16[512,512]{1,0:T(8,128)(2,1)} %param.23) | copy-start | bytes 1572868
  67.9 44.6 %copy-start.14 = (f32[512]{0:T(512)S(1)}, f32[512]{0:T(512)}, u32[]{:S(2)}) copy-start(f32[512]{0:T(512)} %param.25) | copy-start | bytes 6148
  120.3 63.9 %copy-start.12 = (f32[1024]{0:T(1024)S(1)}, f32[1024]{0:T(1024)}, u32[]{:S(2)}) copy-start(f32[1024]{0:T(1024)} %param.27) | copy-start | bytes 12292
  120.3 63.9 %copy-start.13 = (f32[3,256]{1,0:T(4,128)S(1)}, f32[3,256]{1,0:T(4,128)}, u32[]{:S(2)}) copy-start(f32[3,256]{1,0:T(4,128)} %param.30) | copy-start | bytes 9220
  187.6 22.5 %copy-start.1 = (bf16[256,256]{1,0:T(8,128)(2,1)}, bf16[256,256]{1,0:T(8,128)(2,1)S(1)}, u32[]{:S(2)}) copy-start(bf16[256,256]{1,0:T(8,128)(2,1)S(1)} %fusion.14) | copy-start | bytes 393220
  195.1 14.4 %copy-start.6 = (s32[256,10]{0,1:T(8,128)S(1)}, s32[256,10]{0,1:T(8,128)}, u32[]{:S(2)}) copy-start(s32[256,10]{0,1:T(8,128)} %param.33) | copy-start | bytes 30724
  195.1 14.9 %copy-start.9 = (s32[256]{0:T(256)S(1)}, s32[256]{0:T(256)}, u32[]{:S(2)}) copy-start(s32[256]{0:T(256)} %param.34) | copy-start | bytes 3076
  196.4 41.1 %all-to-all-start.2 = ((bf16[64,32,256]{2,1,0:T(8,128)(2,1)}), bf16[64,32,256]{2,1,0:T(8,128)(2,1)S(1)}, u32[]{:S(2)}, u32[]{:S(2)}) async-start(bf16[64,32,256]{2,1,0:T(8,128)(2,1)} %broadcast_select_fusion), calls=%async_computation.2 | async-start | bytes 2097152 | tf_op jit(solution)/shard_map/all_to_all | solution.py:92
  209.3 62.3 %reduce-scatter.2.cloned.1.call-start = ((), (), s32[]{:S(2)}) async-start(), calls=%async_computation.5 | async-start | bytes 655360 | tf_op jit(solution)/shard_map/reduce_scatter | solution.py:97
  245.6 6.4 %copy-start.3 = (bf16[256,1024]{1,0:T(8,128)(2,1)S(1)}, bf16[256,1024]{1,0:T(8,128)(2,1)}, u32[]{:S(2)}) copy-start(bf16[256,1024]{1,0:T(8,128)(2,1)} %param.35) | copy-start | bytes 1572868
  249.2 3.1 %copy-start.4 = (bf16[256,1024]{1,0:T(8,128)(2,1)S(1)}, bf16[256,1024]{1,0:T(8,128)(2,1)}, u32[]{:S(2)}) copy-start(bf16[256,1024]{1,0:T(8,128)(2,1)} %param.36) | copy-start | bytes 1572868
  252.0 19.6 %copy-start.8 = (f32[1024]{0:T(1024)S(1)}, f32[1024]{0:T(1024)}, u32[]{:S(2)}) copy-start(f32[1024]{0:T(1024)} %param.37) | copy-start | bytes 12292
Sparse Core Ops, SparseCore 0:
  140.6 43.6 all-reduce.1
  253.6 17.9 reduce-scatter.1
where the time goes:
time: 282 us; the launch traced here: 280 us
  waiting for transfers between devices  111 us (39%)
  other arithmetic  60.5 us (21%)
  local copies, waits for them, and re-layouts  44.4 us (16%)
  starting transfers between devices  35 us (12%)
  matrix products  14.6 us (5%)
  between operations  14.5 us (5%)
    all_to_all x1, waiting for transfers between devices, per_device(): lax.all_to_all(feat_buffer, 'nodes', split_axis=0, concat_axis=0, tiled=T...  35.6 us
    psum x1, waiting for transfers between devices, per_device(): lax.psum(partial_total.astype(jnp.bfloat16), 'mp').astype(jnp.float32)  29 us
    all_to_all x1, waiting for transfers between devices, per_device(): lax.all_to_all(outgoing, 'nodes', split_axis=0, concat_axis=0, tiled=True)  26.2 us
    scatter-add x1, other arithmetic, per_device(): jax.ops.segment_sum(partial_msg, segment_ids, num_segments=mem_rows + 1)  19.2 us
    another operation x3, other arithmetic  18.2 us
    reduce_scatter x1, waiting for transfers between devices, per_device(): lax.psum_scatter((jnp.dot(neigh_mean, w_neigh, preferred_element_type=jnp...  18.1 us
    scatter-add x1, other arithmetic, per_device(): jax.ops.segment_sum(valid.astype(jnp.float32), segment_ids, num_segments=...  14.7 us
    all_to_all x1, starting transfers between devices, per_device(): lax.all_to_all(id_buffer, 'nodes', split_axis=0, concat_axis=0, tiled=True)  13.1 us
  transfers between devices with their start and end apart: 5, of which 5 were waited for; matrix products, arithmetic and copies ran while one was open for 13% of the time, Pallas kernels for 0%

commit v1 on v0

v1 whole, which is shorter than its diff:
```python
import jax
import jax.numpy as jnp
from jax import lax
from jax.sharding import PartitionSpec as P

F32 = jnp.float32
BF16 = jnp.bfloat16


def one_hot(index, size, dtype=BF16):
    return (index[:, None] == lax.broadcasted_iota(jnp.int32, (1, size), 1)).astype(dtype)


def one_hot_t(index, size, dtype=BF16):
    return (lax.broadcasted_iota(jnp.int32, (size, 1), 0) == index[None, :]).astype(dtype)


def split_dot(x32, w):
    hi = x32.astype(BF16)
    lo = (x32 - hi.astype(F32)).astype(BF16)
    return jnp.dot(hi, w, preferred_element_type=F32) + jnp.dot(lo, w, preferred_element_type=F32)


def per_device(
    event_feats,
    event_owner,
    event_slot,
    memory,
    w_msg_event,
    w_msg_state,
    b_msg,
    w_msg_out,
    b_out,
    w_input,
    w_hidden,
    b_input,
    b_hidden,
    state_slots,
    neighbours,
    query_slots,
    w_neigh,
    w_self,
    b_embed,
):
    owner_count = lax.axis_size("nodes")
    share_count = lax.axis_size("mp")
    mp_index = lax.axis_index("mp")
    event_rows = event_feats.shape[0]
    mem_rows = memory.shape[0]
    mem_width = memory.shape[1]
    col_share = mem_width // share_count
    capacity = 2 * event_rows // owner_count
    send_rows = owner_count * capacity

    owner = event_owner[:, 0]
    match = owner[:, None] == lax.broadcasted_iota(jnp.int32, (1, owner_count), 1)
    earlier = (
        lax.broadcasted_iota(jnp.int32, (event_rows, event_rows), 1)
        < lax.broadcasted_iota(jnp.int32, (event_rows, event_rows), 0)
    ).astype(BF16)
    before = jnp.dot(earlier, match.astype(BF16), preferred_element_type=F32)
    place = jnp.sum(jnp.where(match, before, 0.0), axis=1).astype(jnp.int32)
    target = owner * capacity + place

    route = one_hot_t(target, send_rows)
    feat_buffer = jnp.dot(route, event_feats, preferred_element_type=F32).astype(BF16)
    slot_col = jnp.broadcast_to((event_slot + 1).astype(BF16)[:, None], (event_rows, 128))
    id_buffer = (
        jnp.dot(route, slot_col, preferred_element_type=F32)[:, 0].astype(jnp.int32) - 1
    )
    feat_buffer = feat_buffer.reshape(owner_count, capacity, event_feats.shape[1])
    id_buffer = id_buffer.reshape(owner_count, capacity)
    arrived = lax.all_to_all(feat_buffer, "nodes", split_axis=0, concat_axis=0, tiled=True)
    arrived_ids = lax.all_to_all(id_buffer, "nodes", split_axis=0, concat_axis=0, tiled=True)
    arrived = arrived.reshape(send_rows, event_feats.shape[1])
    arrived_ids = arrived_ids.reshape(send_rows)

    seg = one_hot_t(arrived_ids, mem_rows)
    seg_t = one_hot(arrived_ids, mem_rows)
    counts = jnp.sum(seg.astype(F32), axis=1)

    state_proj = jnp.dot(memory, w_msg_state, preferred_element_type=F32)
    sp_hi = state_proj.astype(BF16)
    sp_lo = (state_proj - sp_hi.astype(F32)).astype(BF16)
    gathered = jnp.dot(seg_t, sp_hi, preferred_element_type=F32) + jnp.dot(
        seg_t, sp_lo, preferred_element_type=F32
    )
    pre = jnp.dot(arrived, w_msg_event, preferred_element_type=F32) + gathered + b_msg
    hidden_msg = jax.nn.relu(pre).astype(BF16)
    hidden_sum = jnp.dot(seg, hidden_msg, preferred_element_type=F32)
    partial_total = split_dot(hidden_sum, w_msg_out)

    divisor = jnp.maximum(counts, 1.0)[:, None]
    msg_total = lax.psum(partial_total.astype(BF16), "mp").astype(F32)
    aggregate = (msg_total / divisor + b_out).astype(BF16)
    gates_in = (
        jnp.einsum("nd,gdc->gnc", aggregate, w_input, preferred_element_type=F32)
        + b_input[:, None, :]
    )
    gates_st = (
        jnp.einsum("nd,gdc->gnc", memory, w_hidden, preferred_element_type=F32)
        + b_hidden[:, None, :]
    )
    reset_gate = jax.nn.sigmoid(gates_in[0] + gates_st[0])
    update_gate = jax.nn.sigmoid(gates_in[1] + gates_st[1])
    candidate = jnp.tanh(gates_in[2] + reset_gate * gates_st[2])
    old_state = lax.dynamic_slice_in_dim(memory, mp_index * col_share, col_share, 1).astype(F32)
    updated = (1.0 - update_gate) * candidate + update_gate * old_state
    new_memory = jnp.where((counts > 0.0)[:, None], updated, old_state).astype(BF16)

    pick = one_hot(state_slots.reshape(-1), mem_rows)
    outgoing = jnp.dot(pick, new_memory, preferred_element_type=F32).astype(BF16)
    outgoing = outgoing.reshape(state_slots.shape[0], state_slots.shape[1], col_share)
    relayed = lax.all_to_all(outgoing, "nodes", split_axis=0, concat_axis=0, tiled=True)
    relayed = relayed.reshape(relayed.shape[0] * relayed.shape[1], col_share)
    recv_rows = relayed.shape[0]
    neigh_count = one_hot(neighbours[:, 0], recv_rows, F32)
    for k in range(1, neighbours.shape[1]):
        neigh_count = neigh_count + one_hot(neighbours[:, k], recv_rows, F32)
    neigh_total = jnp.dot(neigh_count.astype(BF16), relayed, preferred_element_type=F32)
    neigh_mean = (neigh_total / neighbours.shape[1]).astype(BF16)
    self_state = jnp.dot(
        one_hot(query_slots, mem_rows), new_memory, preferred_element_type=F32
    ).astype(BF16)
    summed = lax.psum_scatter(
        (
            jnp.dot(neigh_mean, w_neigh, preferred_element_type=F32)
            + jnp.dot(self_state, w_self, preferred_element_type=F32)
        ).astype(BF16),
        "mp",
        scatter_dimension=0,
        tiled=True,
    ).astype(F32)
    embedding = jax.nn.relu(summed + b_embed).astype(BF16)
    return (new_memory, embedding)


def solution(mesh):
    in_specs = (
        P("nodes", None),
        P("nodes", None),
        P("nodes"),
        P("nodes", None),
        P(None, "mp"),
        P(None, "mp"),
        P("mp"),
        P("mp", None),
        P(),
        P(None, None, "mp"),
        P(None, None, "mp"),
        P(None, "mp"),
        P(None, "mp"),
        P("nodes", None),
        P("nodes", None),
        P("nodes"),
        P("mp", None),
        P("mp", None),
        P(),
    )
    out_specs = (P("nodes", "mp"), P(("nodes", "mp"), None))
    return jax.shard_map(
        per_device, mesh=mesh, in_specs=in_specs, out_specs=out_specs, check_vma=False
    )
```

time: 282 us -> 230 us (0.82)
  other arithmetic: 60.5 us -> 5.33 us
  local copies, waits for them, and re-layouts: 44.4 us -> 1.72 us
  waiting for transfers between devices: 111 us -> 137 us
  matrix products: 14.6 us -> 38.1 us
  starting transfers between devices: 35 us -> 32 us
    scatter-add x2 -> x0, other arithmetic: 33.9 us -> none  [the longest x1 19.2 us: per_device(): jax.ops.segment_sum(partial_msg, segment_ids, num_segments=mem_rows + 1)]
    gather x5 -> x0, local copies, waits for them, and re-layouts: 29.4 us -> none  [the longest x2 11.8 us: per_device(): neigh_rows = jnp.take(relayed, neighbours, axis=0).astype(jnp.float32)]
    dot_general x6 -> x14, matrix products: 14.6 us -> 38.1 us  [the longest x1 5.98 us: per_device(): hidden_sum = jnp.dot(seg, hidden_msg, preferred_element_type=F32)]
    another operation x3 -> x0, other arithmetic: 18.2 us -> none
    psum x1, waiting for transfers between devices: 29 us -> 43.3 us  [per_device(): msg_total = lax.psum(partial_total.astype(BF16), 'mp').astype(F32)]
    scatter x2 -> x0, local copies, waits for them, and re-layouts: 11.7 us -> none  [the longest x1 7.19 us: per_device(): jnp.zeros((owner_count * capacity, feat_width), jnp.bfloat16).at[target]]
    all_to_all x1, waiting for transfers between devices: 35.6 us -> 41.7 us  [per_device(): lax.all_to_all(feat_buffer, 'nodes', split_axis=0, concat_axis=0, tiled=T...]
    all_to_all x1, waiting for transfers between devices: 2.14 us -> 5.65 us  [per_device(): lax.all_to_all(id_buffer, 'nodes', split_axis=0, concat_axis=0, tiled=True)]
  transfers between devices with their start and end apart: 5 -> 5, of which waited for: 5 -> 5; matrix products, arithmetic and copies ran while one was open for 13% -> 5% of each run, Pallas kernels for 0% -> 0%
where the time goes in v1:
time: 230 us; the launch traced here: 228 us
  waiting for transfers between devices  137 us (60%)
  matrix products  38.1 us (17%)
  starting transfers between devices  32 us (14%)
  between operations  14.3 us (6%)
  other arithmetic  5.33 us (2%)
    psum x1, waiting for transfers between devices, per_device(): msg_total = lax.psum(partial_total.astype(BF16), 'mp').astype(F32)  43.3 us
    all_to_all x1, waiting for transfers between devices, per_device(): lax.all_to_all(feat_buffer, 'nodes', split_axis=0, concat_axis=0, tiled=T...  41.7 us
    all_to_all x1, waiting for transfers between devices, per_device(): lax.all_to_all(outgoing, 'nodes', split_axis=0, concat_axis=0, tiled=True)  28.1 us
    reduce_scatter x1, waiting for transfers between devices, per_device(): lax.psum_scatter((jnp.dot(neigh_mean, w_neigh, preferred_element_type=F32...  18.1 us
    all_to_all x1, starting transfers between devices, per_device(): lax.all_to_all(id_buffer, 'nodes', split_axis=0, concat_axis=0, tiled=True)  13.1 us
    all_to_all x1, starting transfers between devices, per_device(): lax.all_to_all(outgoing, 'nodes', split_axis=0, concat_axis=0, tiled=True)  12.9 us
    dot_general x1, matrix products, per_device(): hidden_sum = jnp.dot(seg, hidden_msg, preferred_element_type=F32)  5.98 us
    all_to_all x1, starting transfers between devices, per_device(): lax.all_to_all(feat_buffer, 'nodes', split_axis=0, concat_axis=0, tiled=T...  5.74 us
  transfers between devices with their start and end apart: 5, of which 5 were waited for; matrix products, arithmetic and copies ran while one was open for 5% of the time, Pallas kernels for 0%

profile of v1, /device:TPU:1, one launch (start us, length us, event | category | flops | bytes accessed | tf_op | source)
XLA Modules:
  0.0 228.4 jit_solution(13765049817450807412)
XLA Ops:
  8.2 1.4 fusion.17
  10.4 1.6 fusion.19
  12.6 13.1 %all-to-all-start = ((s32[64,1,32]{2,1,0:T(1,128)}), s32[64,1,32]{2,1,0:T(1,128)S(1)}, u32[]{:S(2)}, u32[]{:S(2)}) async-start(s32[64,1,32]{2,1,0:T(1,128)} %bitcast.1), calls=%async_computation | async-start | bytes 65536 | tf_op jit(solution)/shard_map/all_to_all | solution.py:74
  25.8 3.7 %fusion.5 = bf16[2048,512]{1,0:T(8,128)(2,1)} fusion(bf16[1024,512]{1,0:T(8,128)(2,1)S(1)} %copy-done.12, s32[1024]{0:T(1024)S(1)} %convert_add_fusion), kind=kOutput, calls=%fused_computation.8 | convolution fusion | flops 2150629376 | bytes 3149824 | tf_op jit(solution)/shard_map/dot_general | solution.py:66
  29.5 5.7 %all-to-all-done = s32[64,1,32]{2,1,0:T(1,128)S(1)} async-done(((s32[64,1,32]{2,1,0:T(1,128)}), s32[64,1,32]{2,1,0:T(1,128)S(1)}, u32[]{:S(2)}, u32[]{:S(2)}) %all-to-all-start) | async-done | bytes 8224 | tf_op jit(solution)/shard_map/all_to_all | solution.py:74
  35.1 5.7 %all-to-all-start.1 = ((bf16[64,32,512]{2,1,0:T(8,128)(2,1)}), bf16[64,32,512]{2,1,0:T(8,128)(2,1)}, u32[]{:S(2)}, u32[]{:S(2)}) async-start(bf16[64,32,512]{2,1,0:T(8,128)(2,1)} %bitcast.51), calls=%async_computation.1 | async-start | bytes 4194304 | tf_op jit(solution)/shard_map/all_to_all | solution.py:73
  41.3 1.5 fusion.78
  42.8 2.5 %fusion.13 = f32[3,256,256]{2,1,0:T(8,128)} fusion(bf16[3,1024,256]{2,1,0:T(8,128)(2,1)S(1)} %copy-done, bf16[256,1024]{1,0:T(8,128)(2,1)} %param.22, f32[3,256]{1,0:T(4,128)S(1)} %copy-done.13), kind=kOutput, calls=%fused_computation.35 | convolution fusion | flops 402849792 | bytes 2886656 | tf_op jit(solution)/shard_map/nd,gdc->gnc/dot_general | solution.py:101
  46.6 2.4 %fusion.8 = f32[2048,512]{1,0:T(8,128)} fusion(s32[2048]{0:T(1024)S(1)} %eq.239, f32[256,512]{1,0:T(8,128)S(1)} %fusion.78), kind=kOutput, calls=%fused_computation.25 | convolution fusion | flops 537526272 | bytes 4726784 | tf_op jit(solution)/shard_map/dot_general | solution.py:85
  49.1 41.7 %all-to-all-done.1 = bf16[64,32,512]{2,1,0:T(8,128)(2,1)} async-done(((bf16[64,32,512]{2,1,0:T(8,128)(2,1)}), bf16[64,32,512]{2,1,0:T(8,128)(2,1)}, u32[]{:S(2)}, u32[]{:S(2)}) %all-to-all-start.1) | async-done | bytes 2097184 | tf_op jit(solution)/shard_map/all_to_all | solution.py:73
  90.8 4.8 %fusion.77 = f32[2048,512]{1,0:T(8,128)} fusion(bf16[2048,512]{1,0:T(8,128)(2,1)} %bitcast.3, bf16[512,512]{1,0:T(8,128)(2,1)S(1)} %copy-done.5), kind=kOutput, calls=%fused_computation.104 | convolution fusion | flops 1073741824 | bytes 6815744 | tf_op jit(solution)/shard_map/dot_general | solution.py:88
  95.6 6.0 %fusion.9 = f32[256,512]{1,0:T(8,128)} fusion(s32[2048]{0:T(1024)S(1)} %eq.239, f32[2048,512]{1,0:T(8,128)} %fusion.77, f32[2048,512]{1,0:T(8,128)} %fusion.8, f32[512]{0:T(512)S(1)} %copy-done.16, f32[256,512]{1,0:T(8,128)S(1)} %fusion.78), kind=kOutput, calls=%fused_computation.28 | convolution fusion | flops 1080557568 | bytes 9447424 | tf_op jit(solution)/shard_map/dot_general | solution.py:90
  101.6 1.5 fusion.68
  103.2 1.2 fusion.11
  104.8 43.3 %all-reduce.2.cloned.1.call-done = bf16[256,1024]{1,0:T(8,128)(2,1)} async-done(((bf16[256,1024]{1,0:T(8,128)(2,1)}), bf16[256,1024]{1,0:T(8,128)(2,1)}) %all-reduce.2.cloned.1.call-update) | async-done | bytes 524304 | tf_op jit(solution)/shard_map/psum | solution.py:94
  148.1 2.2 fusion.14
  150.3 1.1 fusion.50
  151.5 1.5 convolution_convert_fusion
  153.0 12.9 %all-to-all-start.2 = ((bf16[64,32,256]{2,1,0:T(8,128)(2,1)}), bf16[64,32,256]{2,1,0:T(8,128)(2,1)S(1)}, u32[]{:S(2)}, u32[]{:S(2)}) async-start(bf16[64,32,256]{2,1,0:T(8,128)(2,1)} %bitcast.53), calls=%async_computation.2 | async-start | bytes 2097152 | tf_op jit(solution)/shard_map/all_to_all | solution.py:114
  166.0 28.1 %all-to-all-done.2 = bf16[64,32,256]{2,1,0:T(8,128)(2,1)S(1)} async-done(((bf16[64,32,256]{2,1,0:T(8,128)(2,1)}), bf16[64,32,256]{2,1,0:T(8,128)(2,1)S(1)}, u32[]{:S(2)}, u32[]{:S(2)}) %all-to-all-start.2) | async-done | bytes 1048608 | tf_op jit(solution)/shard_map/all_to_all | solution.py:114
  194.1 5.2 %fusion.18 = f32[256,1024]{1,0:T(8,128)} fusion(bf16[256,1024]{1,0:T(8,128)(2,1)} %param.35, bf16[2048,256]{1,0:T(8,128)(2,1)S(1)} %bitcast.52, s32[256]{0:T(256)S(1)} %bitcast.64, s32[256]{0:T(256)S(1)} %bitcast.65, s32[256]{0:T(256)S(1)} %bitcast.57, s32[256]{0:T(256)S(1)} %bitcast.58, s32[256]{0:T(256)S(1)} %bitcast.59, s32[256]{0:T(256)S(1)} %bitcast.60, ...), kind=kOutput, calls=%fused_computation.43 | convolution fusion | flops 418512896 | bytes 2631680 | tf_op jit(solution)/shard_map/dot_general | solution.py:127
  199.3 2.5 %fusion.12 = bf16[256,1024]{1,0:T(8,128)(2,1)} fusion(f32[256,1024]{1,0:T(8,128)} %fusion.18, bf16[256,1024]{1,0:T(8,128)(2,1)S(1)} %copy-done.7, bf16[256,256]{1,0:T(8,128)(2,1)S(1)} %fusion.50, s32[256]{0:T(256)S(1)} %copy-done.11), kind=kOutput, calls=%fused_computation.33 | convolution fusion | flops 168427520 | bytes 2229248 | tf_op jit(solution)/shard_map/dot_general | solution.py:128
  201.8 18.1 %reduce-scatter.2.cloned.1.call-done = bf16[64,1024]{1,0:T(8,128)(2,1)} async-done(((bf16[256,1024]{1,0:T(8,128)(2,1)}), bf16[64,1024]{1,0:T(8,128)(2,1)}) %reduce-scatter.2.cloned.1.call-update) | async-done | bytes 131088 | tf_op jit(solution)/shard_map/reduce_scatter | solution.py:125
  219.9 1.6 maximum_convert_fusion.1
  (51 shorter events, 4.6 us)
Async XLA Ops:
  7.2 35.6 %copy-start = (bf16[3,1024,256]{2,1,0:T(8,128)(2,1)S(1)}, bf16[3,1024,256]{2,1,0:T(8,128)(2,1)}, u32[]{:S(2)}) copy-start(bf16[3,1024,256]{2,1,0:T(8,128)(2,1)} %param.29) | copy-start | bytes 4718596
  9.6 16.2 %copy-start.12 = (bf16[1024,512]{1,0:T(8,128)(2,1)S(1)}, bf16[1024,512]{1,0:T(8,128)(2,1)}, u32[]{:S(2)}) copy-start(bf16[1024,512]{1,0:T(8,128)(2,1)} %param.19) | copy-start | bytes 3145732
  12.6 22.5 %all-to-all-start = ((s32[64,1,32]{2,1,0:T(1,128)}), s32[64,1,32]{2,1,0:T(1,128)S(1)}, u32[]{:S(2)}, u32[]{:S(2)}) async-start(s32[64,1,32]{2,1,0:T(1,128)} %bitcast.1), calls=%async_computation | async-start | bytes 65536 | tf_op jit(solution)/shard_map/all_to_all | solution.py:74
  35.1 6.0 %copy-start.8 = (s32[64,32]{0,1:T(8,128)S(1)}, s32[64,32]{0,1:T(8,128)}, u32[]{:S(2)}) copy-start(s32[64,32]{0,1:T(8,128)} %param.32) | copy-start | bytes 24580
  35.1 6.2 %copy-start.3 = (bf16[1024,512]{1,0:T(8,128)(2,1)S(1)}, bf16[1024,512]{1,0:T(8,128)(2,1)}, u32[]{:S(2)}) copy-start(bf16[1024,512]{1,0:T(8,128)(2,1)} %param.24) | copy-start | bytes 3145732
  35.1 55.7 %all-to-all-start.1 = ((bf16[64,32,512]{2,1,0:T(8,128)(2,1)}), bf16[64,32,512]{2,1,0:T(8,128)(2,1)}, u32[]{:S(2)}, u32[]{:S(2)}) async-start(bf16[64,32,512]{2,1,0:T(8,128)(2,1)} %bitcast.51), calls=%async_computation.1 | async-start | bytes 4194304 | tf_op jit(solution)/shard_map/all_to_all | solution.py:73
  40.9 1.9 copy-start.13
  40.9 107.2 %all-reduce.2.cloned.1.call-start = ((), (), s32[]{:S(2)}) async-start(), calls=%async_computation.4 | async-start | bytes 1048576 | tf_op jit(solution)/shard_map/psum | solution.py:94
  46.6 44.2 %copy-start.5 = (bf16[512,512]{1,0:T(8,128)(2,1)S(1)}, bf16[512,512]{1,0:T(8,128)(2,1)}, u32[]{:S(2)}) copy-start(bf16[512,512]{1,0:T(8,128)(2,1)} %param.23) | copy-start | bytes 1572868
  90.8 4.8 %copy-start.16 = (f32[512]{0:T(512)S(1)}, f32[512]{0:T(512)}, u32[]{:S(2)}) copy-start(f32[512]{0:T(512)} %param.25) | copy-start | bytes 6148
  95.6 6.0 %copy-start.1 = (bf16[512,1024]{1,0:T(8,128)(2,1)S(1)}, bf16[512,1024]{1,0:T(8,128)(2,1)}, u32[]{:S(2)}) copy-start(bf16[512,1024]{1,0:T(8,128)(2,1)} %param.26) | copy-start | bytes 3145732
  101.6 1.6 copy-start.2
  103.2 44.9 %copy-start.14 = (f32[1024]{0:T(1024)S(1)}, f32[1024]{0:T(1024)}, u32[]{:S(2)}) copy-start(f32[1024]{0:T(1024)} %param.27) | copy-start | bytes 12292
  103.2 44.9 %copy-start.15 = (f32[3,256]{1,0:T(4,128)S(1)}, f32[3,256]{1,0:T(4,128)}, u32[]{:S(2)}) copy-start(f32[3,256]{1,0:T(4,128)} %param.30) | copy-start | bytes 9220
  104.8 45.6 %copy-start.4 = (f32[3,256,256]{2,1,0:T(8,128)S(1)}, f32[3,256,256]{2,1,0:T(8,128)}, u32[]{:S(2)}) copy-start(f32[3,256,256]{2,1,0:T(8,128)} %fusion.13) | copy-start | bytes 2359300
  151.4 47.8 %copy-start.6 = (bf16[256,256]{1,0:T(8,128)(2,1)}, bf16[256,256]{1,0:T(8,128)(2,1)S(1)}, u32[]{:S(2)}) copy-start(bf16[256,256]{1,0:T(8,128)(2,1)S(1)} %fusion.50) | copy-start | bytes 393220
  151.5 14.5 %copy-start.9 = (s32[256,10]{0,1:T(8,128)S(1)}, s32[256,10]{0,1:T(8,128)}, u32[]{:S(2)}) copy-start(s32[256,10]{0,1:T(8,128)} %param.33) | copy-start | bytes 30724
  153.0 41.1 %all-to-all-start.2 = ((bf16[64,32,256]{2,1,0:T(8,128)(2,1)}), bf16[64,32,256]{2,1,0:T(8,128)(2,1)S(1)}, u32[]{:S(2)}, u32[]{:S(2)}) async-start(bf16[64,32,256]{2,1,0:T(8,128)(2,1)} %bitcast.53), calls=%async_computation.2 | async-start | bytes 2097152 | tf_op jit(solution)/shard_map/all_to_all | solution.py:114
  165.9 54.0 %reduce-scatter.2.cloned.1.call-start = ((), (), s32[]{:S(2)}) async-start(), calls=%async_computation.5 | async-start | bytes 655360 | tf_op jit(solution)/shard_map/reduce_scatter | solution.py:125
  194.1 5.2 %copy-start.7 = (bf16[256,1024]{1,0:T(8,128)(2,1)S(1)}, bf16[256,1024]{1,0:T(8,128)(2,1)}, u32[]{:S(2)}) copy-start(bf16[256,1024]{1,0:T(8,128)(2,1)} %param.36) | copy-start | bytes 1572868
  194.1 5.2 %copy-start.11 = (s32[256]{0:T(256)S(1)}, s32[256]{0:T(256)}, u32[]{:S(2)}) copy-start(s32[256]{0:T(256)} %param.34) | copy-start | bytes 3076
  199.3 20.7 %copy-start.10 = (f32[1024]{0:T(1024)S(1)}, f32[1024]{0:T(1024)}, u32[]{:S(2)}) copy-start(f32[1024]{0:T(1024)} %param.37) | copy-start | bytes 12292
Sparse Core Ops, SparseCore 0:
  104.6 43.4 all-reduce.1
  201.9 17.9 reduce-scatter.1

commit v2 on v1

--- a/solution.py
+++ b/solution.py
@@ -19,6 +19,27 @@
     hi = x32.astype(BF16)
     lo = (x32 - hi.astype(F32)).astype(BF16)
     return jnp.dot(hi, w, preferred_element_type=F32) + jnp.dot(lo, w, preferred_element_type=F32)
+
+
+def mp_reduce_scatter(x, axis, n, me):
+    rows = x.shape[0] // n
+    chunks = x.reshape(n, rows, x.shape[1])
+    doubled = jnp.concatenate([chunks, chunks], axis=0)
+    ahead = lax.dynamic_slice_in_dim(doubled, me, n, 0)
+    total = ahead[0].astype(F32)
+    for t in range(1, n):
+        got = lax.ppermute(ahead[t], axis, [(i, (i + t) % n) for i in range(n)])
+        total = total + got.astype(F32)
+    return total
+
+
+def mp_all_gather(piece, axis, n, me):
+    rel = [piece]
+    for t in range(1, n):
+        rel.append(lax.ppermute(piece, axis, [(i, (i - t) % n) for i in range(n)]))
+    rel = jnp.stack(rel + rel, axis=0)
+    full = lax.dynamic_slice_in_dim(rel, (n - me) % n, n, 0)
+    return full.reshape(n * piece.shape[0], piece.shape[1])
 
 
 def per_device(
@@ -91,7 +112,8 @@
     partial_total = split_dot(hidden_sum, w_msg_out)
 
     divisor = jnp.maximum(counts, 1.0)[:, None]
-    msg_total = lax.psum(partial_total.astype(BF16), "mp").astype(F32)
+    reduced = mp_reduce_scatter(partial_total.astype(BF16), "mp", share_count, mp_index)
+    msg_total = mp_all_gather(reduced.astype(BF16), "mp", share_count, mp_index).astype(F32)
     aggregate = (msg_total / divisor + b_out).astype(BF16)
     gates_in = (
         jnp.einsum("nd,gdc->gnc", aggregate, w_input, preferred_element_type=F32)
@@ -122,15 +144,15 @@
     self_state = jnp.dot(
         one_hot(query_slots, mem_rows), new_memory, preferred_element_type=F32
     ).astype(BF16)
-    summed = lax.psum_scatter(
+    summed = mp_reduce_scatter(
         (
             jnp.dot(neigh_mean, w_neigh, preferred_element_type=F32)
             + jnp.dot(self_state, w_self, preferred_element_type=F32)
         ).astype(BF16),
         "mp",
-        scatter_dimension=0,
-        tiled=True,
-    ).astype(F32)
+        share_count,
+        mp_index,
+    )
     embedding = jax.nn.relu(summed + b_embed).astype(BF16)
     return (new_memory, embedding)
 

time: 230 us -> 177 us (0.77)
  waiting for transfers between devices: 137 us -> 95.5 us
  between operations: 14.3 us -> 1.02 us
  starting transfers between devices: 32 us -> 37.8 us
  matrix products: 38.1 us -> 35 us
    psum x1 -> x0, waiting for transfers between devices: 43.3 us -> none  [per_device(): msg_total = lax.psum(partial_total.astype(BF16), 'mp').astype(F32)]
    ppermute x0 -> x9, waiting for transfers between devices: none -> 20.1 us  [the longest x6 14.7 us: mp_reduce_scatter(): got = lax.ppermute(ahead[t], axis, [(i, (i + t) % n) for i in range(n)])]
    reduce_scatter x1 -> x0, waiting for transfers between devices: 18.1 us -> none  [per_device(): lax.psum_scatter((jnp.dot(neigh_mean, w_neigh, preferred_element_type=F32...]
    ppermute x0 -> x9, starting transfers between devices: none -> 7.03 us  [the longest x6 5.41 us: mp_reduce_scatter(): got = lax.ppermute(ahead[t], axis, [(i, (i + t) % n) for i in range(n)])]
  transfers between devices with their start and end apart: 5 -> 12, of which waited for: 5 -> 12; matrix products, arithmetic and copies ran while one was open for 5% -> 7% of each run, Pallas kernels for 0% -> 0%
where the time goes in v2:
time: 177 us
  waiting for transfers between devices  95.5 us (54%)
  starting transfers between devices  37.8 us (21%)
  matrix products  35 us (20%)
  other arithmetic  4.95 us (3%)
  local copies, waits for them, and re-layouts  2.39 us (1%)
    all_to_all x1, waiting for transfers between devices, per_device(): lax.all_to_all(feat_buffer, 'nodes', split_axis=0, concat_axis=0, tiled=T...  41.6 us
    all_to_all x1, waiting for transfers between devices, per_device(): lax.all_to_all(outgoing, 'nodes', split_axis=0, concat_axis=0, tiled=True)  28.1 us
    ppermute x6, waiting for transfers between devices, mp_reduce_scatter(): got = lax.ppermute(ahead[t], axis, [(i, (i + t) % n) for i in range(n)])  14.7 us
    all_to_all x1, starting transfers between devices, per_device(): lax.all_to_all(id_buffer, 'nodes', split_axis=0, concat_axis=0, tiled=True)  13.1 us
    all_to_all x1, starting transfers between devices, per_device(): lax.all_to_all(outgoing, 'nodes', split_axis=0, concat_axis=0, tiled=True)  11.9 us
    dot_general x1, matrix products, per_device(): hidden_sum = jnp.dot(seg, hidden_msg, preferred_element_type=F32)  6.03 us
    all_to_all x1, starting transfers between devices, per_device(): lax.all_to_all(feat_buffer, 'nodes', split_axis=0, concat_axis=0, tiled=T...  5.73 us
    all_to_all x1, waiting for transfers between devices, per_device(): lax.all_to_all(id_buffer, 'nodes', split_axis=0, concat_axis=0, tiled=True)  5.62 us
  transfers between devices with their start and end apart: 12, of which 12 were waited for; matrix products, arithmetic and copies ran while one was open for 7% of the time, Pallas kernels for 0%

profile of v2, /device:TPU:1, one launch (start us, length us, event | category | flops | bytes accessed | tf_op | source)
XLA Modules:
  0.0 176.7 jit_solution(12860992149401192293)
XLA Ops:
  3.8 1.6 fusion.19
  6.1 13.1 %all-to-all-start = ((s32[64,1,32]{2,1,0:T(1,128)}), s32[64,1,32]{2,1,0:T(1,128)S(1)}, u32[]{:S(2)}, u32[]{:S(2)}) async-start(s32[64,1,32]{2,1,0:T(1,128)} %bitcast.1), calls=%async_computation | async-start | bytes 65536 | tf_op jit(solution)/shard_map/all_to_all | solution.py:95
  19.3 3.7 %fusion.5 = bf16[2048,512]{1,0:T(8,128)(2,1)} fusion(bf16[1024,512]{1,0:T(8,128)(2,1)S(1)} %copy-done.13, s32[1024]{0:T(1024)S(1)} %convert_add_fusion.2), kind=kOutput, calls=%fused_computation.8 | convolution fusion | flops 2150629376 | bytes 3149824 | tf_op jit(solution)/shard_map/dot_general | solution.py:87
  23.0 5.6 %all-to-all-done = s32[64,1,32]{2,1,0:T(1,128)S(1)} async-done(((s32[64,1,32]{2,1,0:T(1,128)}), s32[64,1,32]{2,1,0:T(1,128)S(1)}, u32[]{:S(2)}, u32[]{:S(2)}) %all-to-all-start) | async-done | bytes 8224 | tf_op jit(solution)/shard_map/all_to_all | solution.py:95
  28.6 5.7 %all-to-all-start.1 = ((bf16[64,32,512]{2,1,0:T(8,128)(2,1)}), bf16[64,32,512]{2,1,0:T(8,128)(2,1)}, u32[]{:S(2)}, u32[]{:S(2)}) async-start(bf16[64,32,512]{2,1,0:T(8,128)(2,1)} %bitcast.90), calls=%async_computation.1 | async-start | bytes 4194304 | tf_op jit(solution)/shard_map/all_to_all | solution.py:94
  36.0 2.5 %fusion.13 = f32[3,256,256]{2,1,0:T(8,128)} fusion(bf16[3,1024,256]{2,1,0:T(8,128)(2,1)S(1)} %copy-done, bf16[256,1024]{1,0:T(8,128)(2,1)} %param.22, f32[3,256]{1,0:T(4,128)S(1)} %copy-done.14), kind=kOutput, calls=%fused_computation.35 | convolution fusion | flops 402849792 | bytes 2886656 | tf_op jit(solution)/shard_map/nd,gdc->gnc/dot_general | solution.py:123
  40.2 2.5 %fusion.8 = f32[2048,512]{1,0:T(8,128)} fusion(s32[2048]{0:T(1024)S(1)} %eq.241, f32[256,512]{1,0:T(8,128)S(1)} %fusion.91), kind=kOutput, calls=%fused_computation.25 | convolution fusion | flops 537526272 | bytes 4726784 | tf_op jit(solution)/shard_map/dot_general | solution.py:106
  42.6 41.6 %all-to-all-done.1 = bf16[64,32,512]{2,1,0:T(8,128)(2,1)} async-done(((bf16[64,32,512]{2,1,0:T(8,128)(2,1)}), bf16[64,32,512]{2,1,0:T(8,128)(2,1)}, u32[]{:S(2)}, u32[]{:S(2)}) %all-to-all-start.1) | async-done | bytes 2097184 | tf_op jit(solution)/shard_map/all_to_all | solution.py:94
  84.2 4.9 %fusion.90 = f32[2048,512]{1,0:T(8,128)} fusion(bf16[2048,512]{1,0:T(8,128)(2,1)} %bitcast.3, bf16[512,512]{1,0:T(8,128)(2,1)S(1)} %copy-done.5), kind=kOutput, calls=%fused_computation.138 | convolution fusion | flops 1073741824 | bytes 6815744 | tf_op jit(solution)/shard_map/dot_general | solution.py:109
  89.1 6.0 %fusion.9 = f32[256,512]{1,0:T(8,128)} fusion(s32[2048]{0:T(1024)S(1)} %eq.241, f32[2048,512]{1,0:T(8,128)} %fusion.90, f32[2048,512]{1,0:T(8,128)} %fusion.8, f32[512]{0:T(512)S(1)} %copy-done.17, f32[256,512]{1,0:T(8,128)S(1)} %fusion.91), kind=kOutput, calls=%fused_computation.28 | convolution fusion | flops 1080557568 | bytes 9447424 | tf_op jit(solution)/shard_map/dot_general | solution.py:111
  95.1 1.5 fusion.80
  97.4 2.7 %collective-permute-start.2 = (bf16[64,1024]{1,0:T(8,128)(2,1)S(1)}, bf16[64,1024]{1,0:T(8,128)(2,1)S(1)}, u32[]{:S(2)}, u32[]{:S(2)}) collective-permute-start(bf16[64,1024]{1,0:T(8,128)(2,1)S(1)} %get-tuple-element.9), channel_id=1, source_target_pairs={{0,3},{1,0},{2,1},{3,2},{4,7},{5,4},{6,5},{7,6},{8,11},{9,8},{10,9... | collective-permute-start | bytes 393224 | tf_op jit(solution)/shard_map/ppermute | solution.py:31
  102.7 2.9 %collective-permute-done.1 = bf16[64,1024]{1,0:T(8,128)(2,1)S(1)} collective-permute-done((bf16[64,1024]{1,0:T(8,128)(2,1)S(1)}, bf16[64,1024]{1,0:T(8,128)(2,1)S(1)}, u32[]{:S(2)}, u32[]{:S(2)}) %collective-permute-start.1) | collective-permute-done | bytes 131104 | tf_op jit(solution)/shard_map/ppermute | solution.py:31
  105.6 1.8 collective-permute-done
  109.0 2.3 %collective-permute-done.3 = bf16[64,1024]{1,0:T(8,128)(2,1)S(1)} collective-permute-done((bf16[64,1024]{1,0:T(8,128)(2,1)S(1)}, bf16[64,1024]{1,0:T(8,128)(2,1)S(1)}, u32[]{:S(2)}, u32[]{:S(2)}) %collective-permute-start.3) | collective-permute-done | bytes 131104 | tf_op jit(solution)/shard_map/ppermute | solution.py:39
  111.3 1.9 %collective-permute-done.4 = bf16[64,1024]{1,0:T(8,128)(2,1)S(1)} collective-permute-done((bf16[64,1024]{1,0:T(8,128)(2,1)S(1)}, bf16[64,1024]{1,0:T(8,128)(2,1)S(1)}, u32[]{:S(2)}, u32[]{:S(2)}) %collective-permute-start.4) | collective-permute-done | bytes 131104 | tf_op jit(solution)/shard_map/ppermute | solution.py:39
  116.9 1.5 convolution_convert_fusion
  118.5 11.9 %all-to-all-start.2 = ((bf16[64,32,256]{2,1,0:T(8,128)(2,1)}), bf16[64,32,256]{2,1,0:T(8,128)(2,1)S(1)}, u32[]{:S(2)}, u32[]{:S(2)}) async-start(bf16[64,32,256]{2,1,0:T(8,128)(2,1)} %bitcast.94), calls=%async_computation.2 | async-start | bytes 2097152 | tf_op jit(solution)/shard_map/all_to_all | solution.py:136
  130.4 28.1 %all-to-all-done.2 = bf16[64,32,256]{2,1,0:T(8,128)(2,1)S(1)} async-done(((bf16[64,32,256]{2,1,0:T(8,128)(2,1)}), bf16[64,32,256]{2,1,0:T(8,128)(2,1)S(1)}, u32[]{:S(2)}, u32[]{:S(2)}) %all-to-all-start.2) | async-done | bytes 1048608 | tf_op jit(solution)/shard_map/all_to_all | solution.py:136
  158.5 5.2 %fusion.18 = f32[256,1024]{1,0:T(8,128)} fusion(bf16[256,1024]{1,0:T(8,128)(2,1)} %param.35, bf16[2048,256]{1,0:T(8,128)(2,1)S(1)} %bitcast.93, s32[256]{0:T(256)S(1)} %bitcast.106, s32[256]{0:T(256)S(1)} %bitcast.107, s32[256]{0:T(256)S(1)} %bitcast.99, s32[256]{0:T(256)S(1)} %bitcast.100, s32[256]{0:T(256)S(1)} %bitcast.101, s32[256]{0:T(256)S(1)} %bitcast.102, ...), kind=kOutput, calls=%fused_computation.43 | convolution fusion | flops 418512896 | bytes 2631680 | tf_op jit(solution)/shard_map/dot_general | solution.py:149
  163.8 1.7 fusion.12
  167.3 2.3 %collective-permute-done.8 = bf16[64,1024]{1,0:T(8,128)(2,1)S(1)} collective-permute-done((bf16[64,1024]{1,0:T(8,128)(2,1)S(1)}, bf16[64,1024]{1,0:T(8,128)(2,1)S(1)}, u32[]{:S(2)}, u32[]{:S(2)}) %collective-permute-start.8) | collective-permute-done | bytes 131104 | tf_op jit(solution)/shard_map/ppermute | solution.py:31
  169.6 2.4 %collective-permute-done.7 = bf16[64,1024]{1,0:T(8,128)(2,1)S(1)} collective-permute-done((bf16[64,1024]{1,0:T(8,128)(2,1)S(1)}, bf16[64,1024]{1,0:T(8,128)(2,1)S(1)}, u32[]{:S(2)}, u32[]{:S(2)}) %collective-permute-start.7) | collective-permute-done | bytes 131104 | tf_op jit(solution)/shard_map/ppermute | solution.py:31
  172.0 3.9 %collective-permute-done.6 = bf16[64,1024]{1,0:T(8,128)(2,1)S(1)} collective-permute-done((bf16[64,1024]{1,0:T(8,128)(2,1)S(1)}, bf16[64,1024]{1,0:T(8,128)(2,1)S(1)}, u32[]{:S(2)}, u32[]{:S(2)}) %collective-permute-start.6) | collective-permute-done | bytes 131104 | tf_op jit(solution)/shard_map/ppermute | solution.py:31
  (78 shorter events, 18.3 us)
Async XLA Ops:
  0.6 35.4 %copy-start = (bf16[3,1024,256]{2,1,0:T(8,128)(2,1)S(1)}, bf16[3,1024,256]{2,1,0:T(8,128)(2,1)}, u32[]{:S(2)}) copy-start(bf16[3,1024,256]{2,1,0:T(8,128)(2,1)} %param.29) | copy-start | bytes 4718596
  3.0 16.2 %copy-start.13 = (bf16[1024,512]{1,0:T(8,128)(2,1)S(1)}, bf16[1024,512]{1,0:T(8,128)(2,1)}, u32[]{:S(2)}) copy-start(bf16[1024,512]{1,0:T(8,128)(2,1)} %param.19) | copy-start | bytes 3145732
  6.1 22.5 %all-to-all-start = ((s32[64,1,32]{2,1,0:T(1,128)}), s32[64,1,32]{2,1,0:T(1,128)S(1)}, u32[]{:S(2)}, u32[]{:S(2)}) async-start(s32[64,1,32]{2,1,0:T(1,128)} %bitcast.1), calls=%async_computation | async-start | bytes 65536 | tf_op jit(solution)/shard_map/all_to_all | solution.py:95
  28.6 5.8 %copy-start.8 = (s32[64,32]{0,1:T(8,128)S(1)}, s32[64,32]{0,1:T(8,128)}, u32[]{:S(2)}) copy-start(s32[64,32]{0,1:T(8,128)} %param.32) | copy-start | bytes 24580
  28.6 5.9 %copy-start.3 = (bf16[1024,512]{1,0:T(8,128)(2,1)S(1)}, bf16[1024,512]{1,0:T(8,128)(2,1)}, u32[]{:S(2)}) copy-start(bf16[1024,512]{1,0:T(8,128)(2,1)} %param.24) | copy-start | bytes 3145732
  28.6 55.6 %all-to-all-start.1 = ((bf16[64,32,512]{2,1,0:T(8,128)(2,1)}), bf16[64,32,512]{2,1,0:T(8,128)(2,1)}, u32[]{:S(2)}, u32[]{:S(2)}) async-start(bf16[64,32,512]{2,1,0:T(8,128)(2,1)} %bitcast.90), calls=%async_computation.1 | async-start | bytes 4194304 | tf_op jit(solution)/shard_map/all_to_all | solution.py:94
  40.1 44.1 %copy-start.5 = (bf16[512,512]{1,0:T(8,128)(2,1)S(1)}, bf16[512,512]{1,0:T(8,128)(2,1)}, u32[]{:S(2)}) copy-start(bf16[512,512]{1,0:T(8,128)(2,1)} %param.23) | copy-start | bytes 1572868
  89.1 6.0 %copy-start.1 = (bf16[512,1024]{1,0:T(8,128)(2,1)S(1)}, bf16[512,1024]{1,0:T(8,128)(2,1)}, u32[]{:S(2)}) copy-start(bf16[512,1024]{1,0:T(8,128)(2,1)} %param.26) | copy-start | bytes 3145732
  97.4 17.3 %copy-start.12 = (bf16[3,1024,256]{2,1,0:T(8,128)(2,1)S(1)}, bf16[3,1024,256]{2,1,0:T(8,128)(2,1)}, u32[]{:S(2)}) copy-start(bf16[3,1024,256]{2,1,0:T(8,128)(2,1)} %param.28) | copy-start | bytes 4718596
  97.4 17.3 %copy-start.15 = (f32[1024]{0:T(1024)S(1)}, f32[1024]{0:T(1024)}, u32[]{:S(2)}) copy-start(f32[1024]{0:T(1024)} %param.27) | copy-start | bytes 12292
  97.4 17.3 %copy-start.16 = (f32[3,256]{1,0:T(4,128)S(1)}, f32[3,256]{1,0:T(4,128)}, u32[]{:S(2)}) copy-start(f32[3,256]{1,0:T(4,128)} %param.30) | copy-start | bytes 9220
  97.4 5.3 %collective-permute-start.2 = (bf16[64,1024]{1,0:T(8,128)(2,1)S(1)}, bf16[64,1024]{1,0:T(8,128)(2,1)S(1)}, u32[]{:S(2)}, u32[]{:S(2)}) collective-permute-start(bf16[64,1024]{1,0:T(8,128)(2,1)S(1)} %get-tuple-element.9), channel_id=1, source_target_pairs={{0,3},{1,0},{2,1},{3,2},{4,7},{5,4},{6,5},{7,6},{8,11},{9,8},{10,9... | collective-permute-start | bytes 393224 | tf_op jit(solution)/shard_map/ppermute | solution.py:31
  100.2 5.4 %collective-permute-start.1 = (bf16[64,1024]{1,0:T(8,128)(2,1)S(1)}, bf16[64,1024]{1,0:T(8,128)(2,1)S(1)}, u32[]{:S(2)}, u32[]{:S(2)}) collective-permute-start(bf16[64,1024]{1,0:T(8,128)(2,1)S(1)} %get-tuple-element.8), channel_id=1, source_target_pairs={{0,2},{1,3},{2,0},{3,1},{4,6},{5,7},{6,4},{7,5},{8,10},{9,11},{10,... | collective-permute-start | bytes 393224 | tf_op jit(solution)/shard_map/ppermute | solution.py:31
  100.7 6.6 %collective-permute-start = (bf16[64,1024]{1,0:T(8,128)(2,1)S(1)}, bf16[64,1024]{1,0:T(8,128)(2,1)S(1)}, u32[]{:S(2)}, u32[]{:S(2)}) collective-permute-start(bf16[64,1024]{1,0:T(8,128)(2,1)S(1)} %get-tuple-element.7), channel_id=1, source_target_pairs={{0,1},{1,2},{2,3},{3,0},{4,5},{5,6},{6,7},{7,4},{8,9},{9,10},{10,1... | collective-permute-start | bytes 393224 | tf_op jit(solution)/shard_map/ppermute | solution.py:31
  107.4 3.9 %collective-permute-start.3 = (bf16[64,1024]{1,0:T(8,128)(2,1)S(1)}, bf16[64,1024]{1,0:T(8,128)(2,1)S(1)}, u32[]{:S(2)}, u32[]{:S(2)}) collective-permute-start(bf16[64,1024]{1,0:T(8,128)(2,1)S(1)} %get-tuple-element.3), channel_id=1, source_target_pairs={{0,3},{1,0},{2,1},{3,2},{4,7},{5,4},{6,5},{7,6},{8,11},{9,8},{10,9... | collective-permute-start | bytes 393224 | tf_op jit(solution)/shard_map/ppermute | solution.py:39
  107.8 5.4 %collective-permute-start.4 = (bf16[64,1024]{1,0:T(8,128)(2,1)S(1)}, bf16[64,1024]{1,0:T(8,128)(2,1)S(1)}, u32[]{:S(2)}, u32[]{:S(2)}) collective-permute-start(bf16[64,1024]{1,0:T(8,128)(2,1)S(1)} %get-tuple-element.3), channel_id=1, source_target_pairs={{0,2},{1,3},{2,0},{3,1},{4,6},{5,7},{6,4},{7,5},{8,10},{9,11},{10,... | collective-permute-start | bytes 393224 | tf_op jit(solution)/shard_map/ppermute | solution.py:39
  108.3 6.2 %collective-permute-start.5 = (bf16[64,1024]{1,0:T(8,128)(2,1)S(1)}, bf16[64,1024]{1,0:T(8,128)(2,1)S(1)}, u32[]{:S(2)}, u32[]{:S(2)}) collective-permute-start(bf16[64,1024]{1,0:T(8,128)(2,1)S(1)} %get-tuple-element.3), channel_id=1, source_target_pairs={{0,1},{1,2},{2,3},{3,0},{4,5},{5,6},{6,7},{7,4},{8,9},{9,10},{10,1... | collective-permute-start | bytes 393224 | tf_op jit(solution)/shard_map/ppermute | solution.py:39
  116.9 46.8 %copy-start.6 = (bf16[256,256]{1,0:T(8,128)(2,1)}, bf16[256,256]{1,0:T(8,128)(2,1)S(1)}, u32[]{:S(2)}) copy-start(bf16[256,256]{1,0:T(8,128)(2,1)S(1)} %fusion.54) | copy-start | bytes 393220
  116.9 13.4 %copy-start.9 = (s32[256,10]{0,1:T(8,128)S(1)}, s32[256,10]{0,1:T(8,128)}, u32[]{:S(2)}) copy-start(s32[256,10]{0,1:T(8,128)} %param.33) | copy-start | bytes 30724
  118.5 40.0 %all-to-all-start.2 = ((bf16[64,32,256]{2,1,0:T(8,128)(2,1)}), bf16[64,32,256]{2,1,0:T(8,128)(2,1)S(1)}, u32[]{:S(2)}, u32[]{:S(2)}) async-start(bf16[64,32,256]{2,1,0:T(8,128)(2,1)} %bitcast.94), calls=%async_computation.2 | async-start | bytes 2097152 | tf_op jit(solution)/shard_map/all_to_all | solution.py:136
  163.8 12.1 %copy-start.10 = (f32[1024]{0:T(1024)S(1)}, f32[1024]{0:T(1024)}, u32[]{:S(2)}) copy-start(f32[1024]{0:T(1024)} %param.37) | copy-start | bytes 12292
  165.7 3.9 %collective-permute-start.8 = (bf16[64,1024]{1,0:T(8,128)(2,1)S(1)}, bf16[64,1024]{1,0:T(8,128)(2,1)S(1)}, u32[]{:S(2)}, u32[]{:S(2)}) collective-permute-start(bf16[64,1024]{1,0:T(8,128)(2,1)S(1)} %get-tuple-element.6), channel_id=1, source_target_pairs={{0,3},{1,0},{2,1},{3,2},{4,7},{5,4},{6,5},{7,6},{8,11},{9,8},{10,9... | collective-permute-start | bytes 393224 | tf_op jit(solution)/shard_map/ppermute | solution.py:31
  166.6 5.4 %collective-permute-start.7 = (bf16[64,1024]{1,0:T(8,128)(2,1)S(1)}, bf16[64,1024]{1,0:T(8,128)(2,1)S(1)}, u32[]{:S(2)}, u32[]{:S(2)}) collective-permute-start(bf16[64,1024]{1,0:T(8,128)(2,1)S(1)} %get-tuple-element.5), channel_id=1, source_target_pairs={{0,2},{1,3},{2,0},{3,1},{4,6},{5,7},{6,4},{7,5},{8,10},{9,11},{10,... | collective-permute-start | bytes 393224 | tf_op jit(solution)/shard_map/ppermute | solution.py:31
  166.6 9.3 %collective-permute-start.6 = (bf16[64,1024]{1,0:T(8,128)(2,1)S(1)}, bf16[64,1024]{1,0:T(8,128)(2,1)S(1)}, u32[]{:S(2)}, u32[]{:S(2)}) collective-permute-start(bf16[64,1024]{1,0:T(8,128)(2,1)S(1)} %get-tuple-element.4), channel_id=1, source_target_pairs={{0,1},{1,2},{2,3},{3,0},{4,5},{5,6},{6,7},{7,4},{8,9},{9,10},{10,1... | collective-permute-start | bytes 393224 | tf_op jit(solution)/shard_map/ppermute | solution.py:31
  (6 other events, 19.7 us)

commit v3 on v2

--- a/solution.py
+++ b/solution.py
@@ -81,20 +81,32 @@
     ).astype(BF16)
     before = jnp.dot(earlier, match.astype(BF16), preferred_element_type=F32)
     place = jnp.sum(jnp.where(match, before, 0.0), axis=1).astype(jnp.int32)
-    target = owner * capacity + place
-
-    route = one_hot_t(target, send_rows)
-    feat_buffer = jnp.dot(route, event_feats, preferred_element_type=F32).astype(BF16)
+    per = capacity // share_count
+    low = mp_index * per
+    in_range = (place >= low) & (place < low + per)
+    local = jnp.where(in_range, owner * per + (place - low), -1)
+    route = one_hot_t(local, owner_count * per)
+    feat_part = jnp.dot(route, event_feats, preferred_element_type=F32).astype(BF16)
     slot_col = jnp.broadcast_to((event_slot + 1).astype(BF16)[:, None], (event_rows, 128))
-    id_buffer = (
-        jnp.dot(route, slot_col, preferred_element_type=F32)[:, 0].astype(jnp.int32) - 1
+    id_part = jnp.dot(route, slot_col, preferred_element_type=F32)[:, 0] - 1.0
+    feat_width = event_feats.shape[1]
+    id_block = jnp.pad(id_part.reshape(owner_count, per), ((0, 0), (0, 128 - per)))
+    payload = jnp.concatenate(
+        [feat_part.reshape(owner_count, per * feat_width), id_block.astype(BF16)], axis=1
     )
-    feat_buffer = feat_buffer.reshape(owner_count, capacity, event_feats.shape[1])
-    id_buffer = id_buffer.reshape(owner_count, capacity)
-    arrived = lax.all_to_all(feat_buffer, "nodes", split_axis=0, concat_axis=0, tiled=True)
-    arrived_ids = lax.all_to_all(id_buffer, "nodes", split_axis=0, concat_axis=0, tiled=True)
-    arrived = arrived.reshape(send_rows, event_feats.shape[1])
-    arrived_ids = arrived_ids.reshape(send_rows)
+    landed = lax.all_to_all(payload, "nodes", split_axis=0, concat_axis=0, tiled=True)
+    pieces = [landed]
+    for t in range(1, share_count):
+        pieces.append(
+            lax.ppermute(landed, "mp", [(i, (i - t) % share_count) for i in range(share_count)])
+        )
+    arrived = jnp.concatenate(
+        [p[:, : per * feat_width].reshape(owner_count * per, feat_width) for p in pieces], axis=0
+    )
+    arrived_ids = jnp.concatenate(
+        [p[:, per * feat_width : per * feat_width + per].reshape(owner_count * per) for p in pieces],
+        axis=0,
+    ).astype(jnp.int32)
 
     seg = one_hot_t(arrived_ids, mem_rows)
     seg_t = one_hot(arrived_ids, mem_rows)

time: 177 us -> 168 us (0.949)
  local copies, waits for them, and re-layouts: 2.39 us -> 13.8 us
  waiting for transfers between devices: 95.5 us -> 88.5 us
  starting transfers between devices: 37.8 us -> 30.8 us
  matrix products: 35 us -> 28.6 us
    all_to_all x2 -> x1, waiting for transfers between devices: 47.2 us -> 18.2 us  [per_device(): lax.all_to_all(payload, 'nodes', split_axis=0, concat_axis=0, tiled=True)]
    ppermute x0 -> x3, waiting for transfers between devices: none -> 20.1 us  [per_device(): lax.ppermute(landed, 'mp', [(i, (i - t) % share_count) for i in range(sha...]
    all_to_all x1, starting transfers between devices: 11.9 us -> 5.67 us  [per_device(): lax.all_to_all(outgoing, 'nodes', split_axis=0, concat_axis=0, tiled=True)]
    all_to_all x2 -> x1, starting transfers between devices: 18.9 us -> 13.1 us  [per_device(): lax.all_to_all(payload, 'nodes', split_axis=0, concat_axis=0, tiled=True)]
    slice x1 -> x9, local copies, waits for them, and re-layouts: 0.2 us -> 5.63 us  [the longest x4 3.28 us: per_device(): p[:, :per * feat_width].reshape(owner_count * per, feat_width)]
    reshape x0 -> x5, local copies, waits for them, and re-layouts: none -> 4.39 us  [the longest x4 4.14 us: per_device(): p[:, :per * feat_width].reshape(owner_count * per, feat_width)]
    ppermute x0 -> x3, starting transfers between devices: none -> 3.68 us  [per_device(): lax.ppermute(landed, 'mp', [(i, (i - t) % share_count) for i in range(sha...]
    dot_general x2, matrix products: 6.45 us -> 3 us  [the longest x1 2.51 us: per_device(): jnp.dot(seg_t, sp_lo, preferred_element_type=F32)]
  transfers between devices with their start and end apart: 12 -> 14, of which waited for: 12 -> 12; matrix products, arithmetic and copies ran while one was open for 7% -> 4% of each run, Pallas kernels for 0% -> 0%
where the time goes in v3:
time: 168 us; the launch traced here: 167 us
  waiting for transfers between devices  88.5 us (53%)
  starting transfers between devices  30.8 us (18%)
  matrix products  28.6 us (17%)
  local copies, waits for them, and re-layouts  13.8 us (8%)
  other arithmetic  4.36 us (3%)
    all_to_all x1, waiting for transfers between devices, per_device(): lax.all_to_all(outgoing, 'nodes', split_axis=0, concat_axis=0, tiled=True)  28.1 us
    ppermute x3, waiting for transfers between devices, per_device(): lax.ppermute(landed, 'mp', [(i, (i - t) % share_count) for i in range(sha...  20.1 us
    all_to_all x1, waiting for transfers between devices, per_device(): lax.all_to_all(payload, 'nodes', split_axis=0, concat_axis=0, tiled=True)  18.2 us
    ppermute x6, waiting for transfers between devices, mp_reduce_scatter(): got = lax.ppermute(ahead[t], axis, [(i, (i + t) % n) for i in range(n)])  13.5 us
    all_to_all x1, starting transfers between devices, per_device(): lax.all_to_all(payload, 'nodes', split_axis=0, concat_axis=0, tiled=True)  13.1 us
    ppermute x3, waiting for transfers between devices, mp_all_gather(): rel.append(lax.ppermute(piece, axis, [(i, (i - t) % n) for i in range(n)]))  8.58 us
    dot_general x1, matrix products, per_device(): hidden_sum = jnp.dot(seg, hidden_msg, preferred_element_type=F32)  6.45 us
    all_to_all x1, starting transfers between devices, per_device(): lax.all_to_all(outgoing, 'nodes', split_axis=0, concat_axis=0, tiled=True)  5.67 us
  transfers between devices with their start and end apart: 14, of which 12 were waited for; matrix products, arithmetic and copies ran while one was open for 4% of the time, Pallas kernels for 0%

profile of v3, /device:TPU:1, one launch (start us, length us, event | category | flops | bytes accessed | tf_op | source)
XLA Modules:
  0.0 167.1 jit_solution(14716996972449985297)
XLA Ops:
  2.8 2.0 %fusion.14 = bf16[512,512]{1,0:T(8,128)(2,1)S(1)} fusion(bf16[1024,512]{1,0:T(8,128)(2,1)} %param.19, s32[1024]{0:T(1024)S(1)} %add_select_fusion), kind=kOutput, calls=%fused_computation.35 | convolution fusion | flops 537657344 | bytes 1576960 | tf_op jit(solution)/shard_map/dot_general | solution.py:89
  8.5 13.1 %all-to-all-start = ((bf16[64,2,2112]{2,1,0:T(2,128)(2,1)}), bf16[64,2,2112]{2,1,0:T(2,128)(2,1)S(1)}, u32[]{:S(2)}, u32[]{:S(2)}) async-start(bf16[64,2,2112]{2,1,0:T(2,128)(2,1)} %reshape.176), calls=%async_computation | async-start | bytes 1114112 | tf_op jit(solution)/shard_map/all_to_all | solution.py:97
  21.9 18.2 %all-to-all-done = bf16[64,2,2112]{2,1,0:T(2,128)(2,1)S(1)} async-done(((bf16[64,2,2112]{2,1,0:T(2,128)(2,1)}), bf16[64,2,2112]{2,1,0:T(2,128)(2,1)S(1)}, u32[]{:S(2)}, u32[]{:S(2)}) %all-to-all-start) | async-done | bytes 540704 | tf_op jit(solution)/shard_map/all_to_all | solution.py:97
  40.8 2.6 %collective-permute-start = (bf16[64,4224]{1,0:T(8,128)(2,1)S(1)}, bf16[64,4224]{1,0:T(8,128)(2,1)}, u32[]{:S(2)}, u32[]{:S(2)}) collective-permute-start(bf16[64,4224]{1,0:T(8,128)(2,1)S(1)} %bitcast.91), channel_id=1, source_target_pairs={{0,3},{1,0},{2,1},{3,2},{4,7},{5,4},{6,5},{7,6},{8,11},{9,8},{10,9... | collective-permute-start | bytes 1622024 | tf_op jit(solution)/shard_map/ppermute | solution.py:101
  44.4 1.8 %fusion.105 = f32[256,512]{1,0:T(8,128)S(1)} fusion(bf16[256,1024]{1,0:T(8,128)(2,1)} %param.22, bf16[1024,512]{1,0:T(8,128)(2,1)} %param.24), kind=kOutput, calls=%fused_computation.156 | convolution fusion | flops 268435456 | bytes 2097152 | tf_op jit(solution)/shard_map/dot_general | solution.py:115
  49.0 6.3 %collective-permute-done = bf16[64,4224]{1,0:T(8,128)(2,1)} collective-permute-done((bf16[64,4224]{1,0:T(8,128)(2,1)S(1)}, bf16[64,4224]{1,0:T(8,128)(2,1)}, u32[]{:S(2)}, u32[]{:S(2)}) %collective-permute-start) | collective-permute-done | bytes 540704 | tf_op jit(solution)/shard_map/ppermute | solution.py:101
  56.1 2.0 %collective-permute-done.1 = bf16[64,4224]{1,0:T(8,128)(2,1)} collective-permute-done((bf16[64,4224]{1,0:T(8,128)(2,1)S(1)}, bf16[64,4224]{1,0:T(8,128)(2,1)}, u32[]{:S(2)}, u32[]{:S(2)}) %collective-permute-start.1) | collective-permute-done | bytes 540704 | tf_op jit(solution)/shard_map/ppermute | solution.py:101
  58.9 11.8 %collective-permute-done.2 = bf16[64,4224]{1,0:T(8,128)(2,1)} collective-permute-done((bf16[64,4224]{1,0:T(8,128)(2,1)S(1)}, bf16[64,4224]{1,0:T(8,128)(2,1)}, u32[]{:S(2)}, u32[]{:S(2)}) %collective-permute-start.2) | collective-permute-done | bytes 540704 | tf_op jit(solution)/shard_map/ppermute | solution.py:101
  71.5 2.5 %fusion.8 = f32[2048,512]{1,0:T(8,128)} fusion(s32[2048]{0:T(1024)S(1)} %maximum_convert_fusion.1, f32[256,512]{1,0:T(8,128)S(1)} %fusion.105), kind=kOutput, calls=%fused_computation.24 | convolution fusion | flops 537919488 | bytes 4726784 | tf_op jit(solution)/shard_map/dot_general | solution.py:118
  74.0 2.4 %fusion.9 = f32[2048,512]{1,0:T(8,128)} fusion(s32[2048]{0:T(1024)S(1)} %maximum_convert_fusion.1, f32[256,512]{1,0:T(8,128)S(1)} %fusion.105), kind=kOutput, calls=%fused_computation.25 | convolution fusion | flops 537526272 | bytes 4726784 | tf_op jit(solution)/shard_map/dot_general | solution.py:118
  83.2 6.4 %fusion.12 = f32[256,512]{1,0:T(8,128)S(1)} fusion(f32[2048,512]{1,0:T(8,128)} %fusion.9, f32[2048,512]{1,0:T(8,128)} %fusion.8, bf16[512,512]{1,0:T(8,128)(2,1)} %param.23, bf16[512,512]{1,0:T(8,128)(2,1)} %reshape.157, bf16[512,512]{1,0:T(8,128)(2,1)} %reshape.156, bf16[512,512]{1,0:T(8,128)(2,1)} %reshape.155, bf16[512,512]{1,0:T(8,128)(2,1)} %reshape.154, ...), kind=kOutput, calls=%fused_computation.31 | convolution fusion | flops 1624768512 | bytes 11544576 | tf_op jit(solution)/shard_map/dot_general | solution.py:123
  91.1 1.7 %collective-permute-start.4 = (bf16[64,1024]{1,0:T(8,128)(2,1)S(1)}, bf16[64,1024]{1,0:T(8,128)(2,1)S(1)}, u32[]{:S(2)}, u32[]{:S(2)}) collective-permute-start(bf16[64,1024]{1,0:T(8,128)(2,1)S(1)} %get-tuple-element.8), channel_id=1, source_target_pairs={{0,2},{1,3},{2,0},{3,1},{4,6},{5,7},{6,4},{7,5},{8,10},{9,11},{10,... | collective-permute-start | bytes 393224 | tf_op jit(solution)/shard_map/ppermute | solution.py:31
  93.7 6.3 %collective-permute-done.3 = bf16[64,1024]{1,0:T(8,128)(2,1)S(1)} collective-permute-done((bf16[64,1024]{1,0:T(8,128)(2,1)S(1)}, bf16[64,1024]{1,0:T(8,128)(2,1)S(1)}, u32[]{:S(2)}, u32[]{:S(2)}) %collective-permute-start.3) | collective-permute-done | bytes 131104 | tf_op jit(solution)/shard_map/ppermute | solution.py:31
  100.1 2.9 %collective-permute-start.6 = (bf16[64,1024]{1,0:T(8,128)(2,1)S(1)}, bf16[64,1024]{1,0:T(8,128)(2,1)S(1)}, u32[]{:S(2)}, u32[]{:S(2)}) collective-permute-start(bf16[64,1024]{1,0:T(8,128)(2,1)S(1)} %get-tuple-element.3), channel_id=1, source_target_pairs={{0,3},{1,0},{2,1},{3,2},{4,7},{5,4},{6,5},{7,6},{8,11},{9,8},{10,9... | collective-permute-start | bytes 393224 | tf_op jit(solution)/shard_map/ppermute | solution.py:39
  103.7 2.9 %collective-permute-done.6 = bf16[64,1024]{1,0:T(8,128)(2,1)S(1)} collective-permute-done((bf16[64,1024]{1,0:T(8,128)(2,1)S(1)}, bf16[64,1024]{1,0:T(8,128)(2,1)S(1)}, u32[]{:S(2)}, u32[]{:S(2)}) %collective-permute-start.6) | collective-permute-done | bytes 131104 | tf_op jit(solution)/shard_map/ppermute | solution.py:39
  106.6 1.9 %collective-permute-done.7 = bf16[64,1024]{1,0:T(8,128)(2,1)S(1)} collective-permute-done((bf16[64,1024]{1,0:T(8,128)(2,1)S(1)}, bf16[64,1024]{1,0:T(8,128)(2,1)S(1)}, u32[]{:S(2)}, u32[]{:S(2)}) %collective-permute-start.7) | collective-permute-done | bytes 131104 | tf_op jit(solution)/shard_map/ppermute | solution.py:39
  108.5 3.9 %collective-permute-done.8 = bf16[64,1024]{1,0:T(8,128)(2,1)S(1)} collective-permute-done((bf16[64,1024]{1,0:T(8,128)(2,1)S(1)}, bf16[64,1024]{1,0:T(8,128)(2,1)S(1)}, u32[]{:S(2)}, u32[]{:S(2)}) %collective-permute-start.8) | collective-permute-done | bytes 131104 | tf_op jit(solution)/shard_map/ppermute | solution.py:39
  114.8 1.6 convolution_convert_fusion
  116.3 5.7 %all-to-all-start.1 = ((bf16[64,32,256]{2,1,0:T(8,128)(2,1)}), bf16[64,32,256]{2,1,0:T(8,128)(2,1)S(1)}, u32[]{:S(2)}, u32[]{:S(2)}) async-start(bf16[64,32,256]{2,1,0:T(8,128)(2,1)} %bitcast.99), calls=%async_computation.1 | async-start | bytes 2097152 | tf_op jit(solution)/shard_map/all_to_all | solution.py:148
  122.0 28.1 %all-to-all-done.1 = bf16[64,32,256]{2,1,0:T(8,128)(2,1)S(1)} async-done(((bf16[64,32,256]{2,1,0:T(8,128)(2,1)}), bf16[64,32,256]{2,1,0:T(8,128)(2,1)S(1)}, u32[]{:S(2)}, u32[]{:S(2)}) %all-to-all-start.1) | async-done | bytes 1048608 | tf_op jit(solution)/shard_map/all_to_all | solution.py:148
  150.2 5.2 %fusion.24 = f32[256,1024]{1,0:T(8,128)} fusion(bf16[256,1024]{1,0:T(8,128)(2,1)} %param.35, bf16[2048,256]{1,0:T(8,128)(2,1)S(1)} %bitcast.98, s32[256]{0:T(256)S(1)} %bitcast.111, s32[256]{0:T(256)S(1)} %bitcast.112, s32[256]{0:T(256)S(1)} %bitcast.104, s32[256]{0:T(256)S(1)} %bitcast.105, s32[256]{0:T(256)S(1)} %bitcast.106, s32[256]{0:T(256)S(1)} %bitcast.107, ...), kind=kOutput, calls=%fused_computation.47 | convolution fusion | flops 418512896 | bytes 2631680 | tf_op jit(solution)/shard_map/dot_general | solution.py:161
  155.4 1.7 %fusion.16 = bf16[256,1024]{1,0:T(8,128)(2,1)S(1)} fusion(f32[256,1024]{1,0:T(8,128)} %fusion.24, bf16[256,1024]{1,0:T(8,128)(2,1)S(1)} %copy-done.5, bf16[256,256]{1,0:T(8,128)(2,1)S(1)} %fusion.67, s32[256]{0:T(256)S(1)} %copy-done.10), kind=kOutput, calls=%fused_computation.37 | convolution fusion | flops 168427520 | bytes 2229248 | tf_op jit(solution)/shard_map/dot_general | solution.py:162
  159.1 3.7 %collective-permute-done.10 = bf16[64,1024]{1,0:T(8,128)(2,1)S(1)} collective-permute-done((bf16[64,1024]{1,0:T(8,128)(2,1)S(1)}, bf16[64,1024]{1,0:T(8,128)(2,1)S(1)}, u32[]{:S(2)}, u32[]{:S(2)}) %collective-permute-start.10) | collective-permute-done | bytes 131104 | tf_op jit(solution)/shard_map/ppermute | solution.py:31
  163.8 2.6 %collective-permute-done.9 = bf16[64,1024]{1,0:T(8,128)(2,1)S(1)} collective-permute-done((bf16[64,1024]{1,0:T(8,128)(2,1)S(1)}, bf16[64,1024]{1,0:T(8,128)(2,1)S(1)}, u32[]{:S(2)}, u32[]{:S(2)}) %collective-permute-start.9) | collective-permute-done | bytes 131104 | tf_op jit(solution)/shard_map/ppermute | solution.py:31
  (99 shorter events, 28.9 us)
Async XLA Ops:
  0.6 45.6 %copy-start = (bf16[3,1024,256]{2,1,0:T(8,128)(2,1)S(1)}, bf16[3,1024,256]{2,1,0:T(8,128)(2,1)}, u32[]{:S(2)}) copy-start(bf16[3,1024,256]{2,1,0:T(8,128)(2,1)} %param.29) | copy-start | bytes 4718596
  5.8 15.9 %copy-start.6 = (s32[64,32]{0,1:T(8,128)S(1)}, s32[64,32]{0,1:T(8,128)}, u32[]{:S(2)}) copy-start(s32[64,32]{0,1:T(8,128)} %param.32) | copy-start | bytes 24580
  8.5 31.5 %all-to-all-start = ((bf16[64,2,2112]{2,1,0:T(2,128)(2,1)}), bf16[64,2,2112]{2,1,0:T(2,128)(2,1)S(1)}, u32[]{:S(2)}, u32[]{:S(2)}) async-start(bf16[64,2,2112]{2,1,0:T(2,128)(2,1)} %reshape.176), calls=%async_computation | async-start | bytes 1114112 | tf_op jit(solution)/shard_map/all_to_all | solution.py:97
  40.7 5.6 %copy-start.2 = (bf16[256,1024]{1,0:T(8,128)(2,1)S(1)}, bf16[256,1024]{1,0:T(8,128)(2,1)}, u32[]{:S(2)}) copy-start(bf16[256,1024]{1,0:T(8,128)(2,1)} %param.22) | copy-start | bytes 1572868
  40.8 14.5 %collective-permute-start = (bf16[64,4224]{1,0:T(8,128)(2,1)S(1)}, bf16[64,4224]{1,0:T(8,128)(2,1)}, u32[]{:S(2)}, u32[]{:S(2)}) collective-permute-start(bf16[64,4224]{1,0:T(8,128)(2,1)S(1)} %bitcast.91), channel_id=1, source_target_pairs={{0,3},{1,0},{2,1},{3,2},{4,7},{5,4},{6,5},{7,6},{8,11},{9,8},{10,9... | collective-permute-start | bytes 1622024 | tf_op jit(solution)/shard_map/ppermute | solution.py:101
  43.3 14.8 %collective-permute-start.1 = (bf16[64,4224]{1,0:T(8,128)(2,1)S(1)}, bf16[64,4224]{1,0:T(8,128)(2,1)}, u32[]{:S(2)}, u32[]{:S(2)}) collective-permute-start(bf16[64,4224]{1,0:T(8,128)(2,1)S(1)} %bitcast.92), channel_id=1, source_target_pairs={{0,2},{1,3},{2,0},{3,1},{4,6},{5,7},{6,4},{7,5},{8,10},{9,11},{10,... | collective-permute-start | bytes 1622024 | tf_op jit(solution)/shard_map/ppermute | solution.py:101
  43.8 26.9 %collective-permute-start.2 = (bf16[64,4224]{1,0:T(8,128)(2,1)S(1)}, bf16[64,4224]{1,0:T(8,128)(2,1)}, u32[]{:S(2)}, u32[]{:S(2)}) collective-permute-start(bf16[64,4224]{1,0:T(8,128)(2,1)S(1)} %bitcast.93), channel_id=1, source_target_pairs={{0,1},{1,2},{2,3},{3,0},{4,5},{5,6},{6,7},{7,4},{8,9},{9,10},{10,1... | collective-permute-start | bytes 1622024 | tf_op jit(solution)/shard_map/ppermute | solution.py:101
  83.1 6.5 %copy-start.1 = (bf16[512,1024]{1,0:T(8,128)(2,1)S(1)}, bf16[512,1024]{1,0:T(8,128)(2,1)}, u32[]{:S(2)}) copy-start(bf16[512,1024]{1,0:T(8,128)(2,1)} %param.26) | copy-start | bytes 3145732
  90.7 21.8 %copy-start.11 = (bf16[3,1024,256]{2,1,0:T(8,128)(2,1)S(1)}, bf16[3,1024,256]{2,1,0:T(8,128)(2,1)}, u32[]{:S(2)}) copy-start(bf16[3,1024,256]{2,1,0:T(8,128)(2,1)} %param.28) | copy-start | bytes 4718596
  90.7 21.8 %copy-start.13 = (f32[1024]{0:T(1024)S(1)}, f32[1024]{0:T(1024)}, u32[]{:S(2)}) copy-start(f32[1024]{0:T(1024)} %param.27) | copy-start | bytes 12292
  90.7 21.7 %copy-start.14 = (f32[3,256]{1,0:T(4,128)S(1)}, f32[3,256]{1,0:T(4,128)}, u32[]{:S(2)}) copy-start(f32[3,256]{1,0:T(4,128)} %param.30) | copy-start | bytes 9220
  90.8 9.2 %collective-permute-start.3 = (bf16[64,1024]{1,0:T(8,128)(2,1)S(1)}, bf16[64,1024]{1,0:T(8,128)(2,1)S(1)}, u32[]{:S(2)}, u32[]{:S(2)}) collective-permute-start(bf16[64,1024]{1,0:T(8,128)(2,1)S(1)} %get-tuple-element.7), channel_id=1, source_target_pairs={{0,1},{1,2},{2,3},{3,0},{4,5},{5,6},{6,7},{7,4},{8,9},{9,10},{10,1... | collective-permute-start | bytes 393224 | tf_op jit(solution)/shard_map/ppermute | solution.py:31
  91.1 8.9 %collective-permute-start.4 = (bf16[64,1024]{1,0:T(8,128)(2,1)S(1)}, bf16[64,1024]{1,0:T(8,128)(2,1)S(1)}, u32[]{:S(2)}, u32[]{:S(2)}) collective-permute-start(bf16[64,1024]{1,0:T(8,128)(2,1)S(1)} %get-tuple-element.8), channel_id=1, source_target_pairs={{0,2},{1,3},{2,0},{3,1},{4,6},{5,7},{6,4},{7,5},{8,10},{9,11},{10,... | collective-permute-start | bytes 393224 | tf_op jit(solution)/shard_map/ppermute | solution.py:31
  92.8 7.2 %collective-permute-start.5 = (bf16[64,1024]{1,0:T(8,128)(2,1)S(1)}, bf16[64,1024]{1,0:T(8,128)(2,1)S(1)}, u32[]{:S(2)}, u32[]{:S(2)}) collective-permute-start(bf16[64,1024]{1,0:T(8,128)(2,1)S(1)} %get-tuple-element.9), channel_id=1, source_target_pairs={{0,3},{1,0},{2,1},{3,2},{4,7},{5,4},{6,5},{7,6},{8,11},{9,8},{10,9... | collective-permute-start | bytes 393224 | tf_op jit(solution)/shard_map/ppermute | solution.py:31
  100.1 6.5 %collective-permute-start.6 = (bf16[64,1024]{1,0:T(8,128)(2,1)S(1)}, bf16[64,1024]{1,0:T(8,128)(2,1)S(1)}, u32[]{:S(2)}, u32[]{:S(2)}) collective-permute-start(bf16[64,1024]{1,0:T(8,128)(2,1)S(1)} %get-tuple-element.3), channel_id=1, source_target_pairs={{0,3},{1,0},{2,1},{3,2},{4,7},{5,4},{6,5},{7,6},{8,11},{9,8},{10,9... | collective-permute-start | bytes 393224 | tf_op jit(solution)/shard_map/ppermute | solution.py:39
  103.0 5.4 %collective-permute-start.7 = (bf16[64,1024]{1,0:T(8,128)(2,1)S(1)}, bf16[64,1024]{1,0:T(8,128)(2,1)S(1)}, u32[]{:S(2)}, u32[]{:S(2)}) collective-permute-start(bf16[64,1024]{1,0:T(8,128)(2,1)S(1)} %get-tuple-element.3), channel_id=1, source_target_pairs={{0,2},{1,3},{2,0},{3,1},{4,6},{5,7},{6,4},{7,5},{8,10},{9,11},{10,... | collective-permute-start | bytes 393224 | tf_op jit(solution)/shard_map/ppermute | solution.py:39
  103.0 9.3 %collective-permute-start.8 = (bf16[64,1024]{1,0:T(8,128)(2,1)S(1)}, bf16[64,1024]{1,0:T(8,128)(2,1)S(1)}, u32[]{:S(2)}, u32[]{:S(2)}) collective-permute-start(bf16[64,1024]{1,0:T(8,128)(2,1)S(1)} %get-tuple-element.3), channel_id=1, source_target_pairs={{0,1},{1,2},{2,3},{3,0},{4,5},{5,6},{6,7},{7,4},{8,9},{9,10},{10,1... | collective-permute-start | bytes 393224 | tf_op jit(solution)/shard_map/ppermute | solution.py:39
  114.7 40.6 %copy-start.4 = (bf16[256,256]{1,0:T(8,128)(2,1)}, bf16[256,256]{1,0:T(8,128)(2,1)S(1)}, u32[]{:S(2)}) copy-start(bf16[256,256]{1,0:T(8,128)(2,1)S(1)} %fusion.67) | copy-start | bytes 393220
  114.8 7.2 %copy-start.7 = (s32[256,10]{0,1:T(8,128)S(1)}, s32[256,10]{0,1:T(8,128)}, u32[]{:S(2)}) copy-start(s32[256,10]{0,1:T(8,128)} %param.33) | copy-start | bytes 30724
  116.3 33.8 %all-to-all-start.1 = ((bf16[64,32,256]{2,1,0:T(8,128)(2,1)}), bf16[64,32,256]{2,1,0:T(8,128)(2,1)S(1)}, u32[]{:S(2)}, u32[]{:S(2)}) async-start(bf16[64,32,256]{2,1,0:T(8,128)(2,1)} %bitcast.99), calls=%async_computation.1 | async-start | bytes 2097152 | tf_op jit(solution)/shard_map/all_to_all | solution.py:148
  155.4 11.0 %copy-start.8 = (f32[1024]{0:T(1024)S(1)}, f32[1024]{0:T(1024)}, u32[]{:S(2)}) copy-start(f32[1024]{0:T(1024)} %param.37) | copy-start | bytes 12292
  157.3 5.5 %collective-permute-start.10 = (bf16[64,1024]{1,0:T(8,128)(2,1)S(1)}, bf16[64,1024]{1,0:T(8,128)(2,1)S(1)}, u32[]{:S(2)}, u32[]{:S(2)}) collective-permute-start(bf16[64,1024]{1,0:T(8,128)(2,1)S(1)} %get-tuple-element.5), channel_id=1, source_target_pairs={{0,2},{1,3},{2,0},{3,1},{4,6},{5,7},{6,4},{7,5},{8,10},{9,11},{10,... | collective-permute-start | bytes 393224 | tf_op jit(solution)/shard_map/ppermute | solution.py:31
  157.7 6.2 %collective-permute-start.11 = (bf16[64,1024]{1,0:T(8,128)(2,1)S(1)}, bf16[64,1024]{1,0:T(8,128)(2,1)S(1)}, u32[]{:S(2)}, u32[]{:S(2)}) collective-permute-start(bf16[64,1024]{1,0:T(8,128)(2,1)S(1)} %get-tuple-element.6), channel_id=1, source_target_pairs={{0,3},{1,0},{2,1},{3,2},{4,7},{5,4},{6,5},{7,6},{8,11},{9,8},{10,9... | collective-permute-start | bytes 393224 | tf_op jit(solution)/shard_map/ppermute | solution.py:31
  158.5 7.8 %collective-permute-start.9 = (bf16[64,1024]{1,0:T(8,128)(2,1)S(1)}, bf16[64,1024]{1,0:T(8,128)(2,1)S(1)}, u32[]{:S(2)}, u32[]{:S(2)}) collective-permute-start(bf16[64,1024]{1,0:T(8,128)(2,1)S(1)} %get-tuple-element.4), channel_id=1, source_target_pairs={{0,1},{1,2},{2,3},{3,0},{4,5},{5,6},{6,7},{7,4},{8,9},{9,10},{10,1... | collective-permute-start | bytes 393224 | tf_op jit(solution)/shard_map/ppermute | solution.py:31
  (6 other events, 23.6 us)

commit v4 on v3

--- a/solution.py
+++ b/solution.py
@@ -84,41 +84,44 @@
     per = capacity // share_count
     low = mp_index * per
     in_range = (place >= low) & (place < low + per)
-    local = jnp.where(in_range, owner * per + (place - low), -1)
-    route = one_hot_t(local, owner_count * per)
+    local = jnp.where(in_range, (place - low) * owner_count + owner, -1)
+    route = one_hot_t(local, per * owner_count)
+    feat_width = event_feats.shape[1]
     feat_part = jnp.dot(route, event_feats, preferred_element_type=F32).astype(BF16)
     slot_col = jnp.broadcast_to((event_slot + 1).astype(BF16)[:, None], (event_rows, 128))
     id_part = jnp.dot(route, slot_col, preferred_element_type=F32)[:, 0] - 1.0
-    feat_width = event_feats.shape[1]
-    id_block = jnp.pad(id_part.reshape(owner_count, per), ((0, 0), (0, 128 - per)))
+    id_plane = jnp.pad(id_part.reshape(per, owner_count).T, ((0, 0), (0, feat_width - per)))
     payload = jnp.concatenate(
-        [feat_part.reshape(owner_count, per * feat_width), id_block.astype(BF16)], axis=1
+        [feat_part.reshape(per, owner_count, feat_width), id_plane.astype(BF16)[None]], axis=0
     )
-    landed = lax.all_to_all(payload, "nodes", split_axis=0, concat_axis=0, tiled=True)
+    landed = lax.all_to_all(payload, "nodes", split_axis=1, concat_axis=1, tiled=True)
     pieces = [landed]
     for t in range(1, share_count):
         pieces.append(
             lax.ppermute(landed, "mp", [(i, (i - t) % share_count) for i in range(share_count)])
         )
     arrived = jnp.concatenate(
-        [p[:, : per * feat_width].reshape(owner_count * per, feat_width) for p in pieces], axis=0
+        [p[:per].reshape(per * owner_count, feat_width) for p in pieces], axis=0
     )
     arrived_ids = jnp.concatenate(
-        [p[:, per * feat_width : per * feat_width + per].reshape(owner_count * per) for p in pieces],
-        axis=0,
+        [p[per, :, :per].T.reshape(per * owner_count) for p in pieces], axis=0
     ).astype(jnp.int32)
 
     seg = one_hot_t(arrived_ids, mem_rows)
     seg_t = one_hot(arrived_ids, mem_rows)
     counts = jnp.sum(seg.astype(F32), axis=1)
 
+    recv_rows = state_slots.shape[0] * state_slots.shape[1]
+    neigh_count = one_hot(neighbours[:, 0], recv_rows, F32)
+    for k in range(1, neighbours.shape[1]):
+        neigh_count = neigh_count + one_hot(neighbours[:, k], recv_rows, F32)
+    neigh_count = lax.optimization_barrier(neigh_count.astype(BF16))
     state_proj = jnp.dot(memory, w_msg_state, preferred_element_type=F32)
     sp_hi = state_proj.astype(BF16)
     sp_lo = (state_proj - sp_hi.astype(F32)).astype(BF16)
-    gathered = jnp.dot(seg_t, sp_hi, preferred_element_type=F32) + jnp.dot(
-        seg_t, sp_lo, preferred_element_type=F32
-    )
-    pre = jnp.dot(arrived, w_msg_event, preferred_element_type=F32) + gathered + b_msg
+    lhs = jnp.concatenate([arrived, seg_t, seg_t], axis=1)
+    rhs = jnp.concatenate([w_msg_event, sp_hi, sp_lo], axis=0)
+    pre = jnp.dot(lhs, rhs, preferred_element_type=F32) + b_msg
     hidden_msg = jax.nn.relu(pre).astype(BF16)
     hidden_sum = jnp.dot(seg, hidden_msg, preferred_element_type=F32)
     partial_total = split_dot(hidden_sum, w_msg_out)
@@ -147,11 +150,7 @@
     outgoing = outgoing.reshape(state_slots.shape[0], state_slots.shape[1], col_share)
     relayed = lax.all_to_all(outgoing, "nodes", split_axis=0, concat_axis=0, tiled=True)
     relayed = relayed.reshape(relayed.shape[0] * relayed.shape[1], col_share)
-    recv_rows = relayed.shape[0]
-    neigh_count = one_hot(neighbours[:, 0], recv_rows, F32)
-    for k in range(1, neighbours.shape[1]):
-        neigh_count = neigh_count + one_hot(neighbours[:, k], recv_rows, F32)
-    neigh_total = jnp.dot(neigh_count.astype(BF16), relayed, preferred_element_type=F32)
+    neigh_total = jnp.dot(neigh_count, relayed, preferred_element_type=F32)
     neigh_mean = (neigh_total / neighbours.shape[1]).astype(BF16)
     self_state = jnp.dot(
         one_hot(query_slots, mem_rows), new_memory, preferred_element_type=F32

time: 168 us -> 168 us (level)
  blocking collectives: 0 us -> 41.2 us
  waiting for transfers between devices: 88.5 us -> 67.8 us
  starting transfers between devices: 30.8 us -> 18.1 us
  matrix products: 28.6 us -> 20 us
  other arithmetic: 4.36 us -> 8.02 us
  local copies, waits for them, and re-layouts: 13.8 us -> 11.4 us
    all_to_all x0 -> x1, blocking collectives: none -> 41.2 us  [per_device(): lax.all_to_all(payload, 'nodes', split_axis=1, concat_axis=1, tiled=True)]
    all_to_all x1 -> x0, waiting for transfers between devices: 18.2 us -> none  [per_device(): lax.all_to_all(payload, 'nodes', split_axis=0, concat_axis=0, tiled=True)]
    all_to_all x1 -> x0, starting transfers between devices: 13.1 us -> none  [per_device(): lax.all_to_all(payload, 'nodes', split_axis=0, concat_axis=0, tiled=True)]
    convert_element_type x1 -> x3, other arithmetic: 0.01 us -> 5.19 us  [the longest x1 3.83 us: per_device(): neigh_count = lax.optimization_barrier(neigh_count.astype(BF16))]
    dot_general x2 -> x0, matrix products: 4.94 us -> none  [the longest x1 2.51 us: per_device(): jnp.dot(seg_t, sp_lo, preferred_element_type=F32)]
    reshape x5 -> x1, local copies, waits for them, and re-layouts: 4.39 us -> 0.29 us  [per_device(): feat_part.reshape(per, owner_count, feat_width)]
    all_to_all x1, waiting for transfers between devices: 28.1 us -> 24.3 us  [per_device(): lax.all_to_all(outgoing, 'nodes', split_axis=0, concat_axis=0, tiled=True)]
    transpose x0 -> x6, local copies, waits for them, and re-layouts: none -> 2.38 us  [per_device(): p[per, :, :per].T.reshape(per * owner_count)]
  transfers between devices with their start and end apart: 14 -> 13, of which waited for: 12 -> 12; matrix products, arithmetic and copies ran while one was open for 4% -> 6% of each run, Pallas kernels for 0% -> 0%
where the time goes in v4:
time: 168 us
  waiting for transfers between devices  67.8 us (40%)
  blocking collectives  41.2 us (25%)
  matrix products  20 us (12%)
  starting transfers between devices  18.1 us (11%)
  local copies, waits for them, and re-layouts  11.4 us (7%)
  other arithmetic  8.02 us (5%)
    all_to_all x1, blocking collectives, per_device(): lax.all_to_all(payload, 'nodes', split_axis=1, concat_axis=1, tiled=True)  41.2 us
    all_to_all x1, waiting for transfers between devices, per_device(): lax.all_to_all(outgoing, 'nodes', split_axis=0, concat_axis=0, tiled=True)  24.3 us
    ppermute x3, waiting for transfers between devices, per_device(): lax.ppermute(landed, 'mp', [(i, (i - t) % share_count) for i in range(sha...  21.4 us
    ppermute x6, waiting for transfers between devices, mp_reduce_scatter(): got = lax.ppermute(ahead[t], axis, [(i, (i + t) % n) for i in range(n)])  13.5 us
    ppermute x3, waiting for transfers between devices, mp_all_gather(): rel.append(lax.ppermute(piece, axis, [(i, (i - t) % n) for i in range(n)]))  8.58 us
    slice x4, local copies, waits for them, and re-layouts, per_device(): p[:per].reshape(per * owner_count, feat_width)  6.47 us
    all_to_all x1, starting transfers between devices, per_device(): lax.all_to_all(outgoing, 'nodes', split_axis=0, concat_axis=0, tiled=True)  6.22 us
    dot_general x1, matrix products, per_device(): hidden_sum = jnp.dot(seg, hidden_msg, preferred_element_type=F32)  5.39 us
  transfers between devices with their start and end apart: 13, of which 12 were waited for; matrix products, arithmetic and copies ran while one was open for 6% of the time, Pallas kernels for 0%

profile of v4, /device:TPU:1, one launch (start us, length us, event | category | flops | bytes accessed | tf_op | source)
XLA Modules:
  0.0 167.6 jit_solution(2003734352504844610)
XLA Ops:
  4.4 41.2 %all_to_all.10 = bf16[9,64,512]{2,0,1:T(8,128)(2,1)S(1)} all-to-all(bf16[9,64,512]{2,0,1:T(8,128)(2,1)S(1)} %pad_maximum_fusion), channel_id=1, replica_groups=mesh['nodes'=64,'mp'=4] {'nodes'}, dimensions={1} | all-to-all | bytes 1179648 | tf_op jit(solution)/shard_map/all_to_all | solution.py:97
  46.0 2.6 %collective-permute-start = (bf16[9,64,512]{2,1,0:T(8,128)(2,1)S(1)}, bf16[9,64,512]{2,1,0:T(8,128)(2,1)}, u32[]{:S(2)}, u32[]{:S(2)}) collective-permute-start(bf16[9,64,512]{2,1,0:T(8,128)(2,1)S(1)} %copy.67), channel_id=1, source_target_pairs={{0,3},{1,0},{2,1},{3,2},{4,7},{5,4},{6,5},{7,6},{8,11},{9,8},{10,9... | collective-permute-start | bytes 1769480 | tf_op jit(solution)/shard_map/ppermute | solution.py:101
  51.4 2.5 %subtract_convert_fusion.1 = (bf16[256,512]{1,0:T(8,128)(2,1)S(1)}, bf16[256,512]{1,0:T(8,128)(2,1)}) fusion(bf16[256,1024]{1,0:T(8,128)(2,1)} %param.22, bf16[1024,512]{1,0:T(8,128)(2,1)} %param.24), kind=kOutput, calls=%fused_computation.79 | convolution fusion | flops 268959744 | bytes 2097152 | tf_op jit(solution)/shard_map/dot_general | solution.py:119
  55.0 6.0 %collective-permute-done = bf16[9,64,512]{2,1,0:T(8,128)(2,1)} collective-permute-done((bf16[9,64,512]{2,1,0:T(8,128)(2,1)S(1)}, bf16[9,64,512]{2,1,0:T(8,128)(2,1)}, u32[]{:S(2)}, u32[]{:S(2)}) %collective-permute-start) | collective-permute-done | bytes 589856 | tf_op jit(solution)/shard_map/ppermute | solution.py:101
  61.8 1.9 %collective-permute-done.1 = bf16[9,64,512]{2,1,0:T(8,128)(2,1)} collective-permute-done((bf16[9,64,512]{2,1,0:T(8,128)(2,1)S(1)}, bf16[9,64,512]{2,1,0:T(8,128)(2,1)}, u32[]{:S(2)}, u32[]{:S(2)}) %collective-permute-start.1) | collective-permute-done | bytes 589856 | tf_op jit(solution)/shard_map/ppermute | solution.py:101
  64.6 13.5 %collective-permute-done.2 = bf16[9,64,512]{2,1,0:T(8,128)(2,1)} collective-permute-done((bf16[9,64,512]{2,1,0:T(8,128)(2,1)S(1)}, bf16[9,64,512]{2,1,0:T(8,128)(2,1)}, u32[]{:S(2)}, u32[]{:S(2)}) %collective-permute-start.2) | collective-permute-done | bytes 589856 | tf_op jit(solution)/shard_map/ppermute | solution.py:101
  80.7 1.9 %slice.139 = bf16[8,64,512]{2,1,0:T(8,128)(2,1)} slice(bf16[9,64,512]{2,1,0:T(8,128)(2,1)} %collective-permute-done), slice={[0:8], [0:64], [0:512]} | slice | bytes 1048576 | tf_op jit(solution)/shard_map/slice | solution.py:104
  82.5 1.9 %slice.140 = bf16[8,64,512]{2,1,0:T(8,128)(2,1)} slice(bf16[9,64,512]{2,1,0:T(8,128)(2,1)} %collective-permute-done.1), slice={[0:8], [0:64], [0:512]} | slice | bytes 1048576 | tf_op jit(solution)/shard_map/slice | solution.py:104
  84.4 1.9 %slice.141 = bf16[8,64,512]{2,1,0:T(8,128)(2,1)} slice(bf16[9,64,512]{2,1,0:T(8,128)(2,1)} %collective-permute-done.2), slice={[0:8], [0:64], [0:512]} | slice | bytes 1048576 | tf_op jit(solution)/shard_map/slice | solution.py:104
  86.3 5.4 %fusion.17 = f32[256,512]{1,0:T(8,128)S(1)} fusion(bf16[2048,256]{1,0:T(8,128)(2,1)} %fusion.19, bf16[512,512]{1,0:T(8,128)(2,1)} %bitcast.116, bf16[512,512]{1,0:T(8,128)(2,1)} %bitcast.115, bf16[512,512]{1,0:T(8,128)(2,1)} %bitcast.114, bf16[512,512]{1,0:T(8,128)(2,1)} %bitcast.113, f32[512]{0:T(512)S(1)} %copy-done.17, ...), kind=kOutput, calls=%fused_computation.34 | convolution fusion | flops 2716336128 | bytes 4728832 | tf_op jit(solution)/shard_map/dot_general | solution.py:126
  93.7 1.9 %collective-permute-start.5 = (bf16[64,1024]{1,0:T(8,128)(2,1)S(1)}, bf16[64,1024]{1,0:T(8,128)(2,1)S(1)}, u32[]{:S(2)}, u32[]{:S(2)}) collective-permute-start(bf16[64,1024]{1,0:T(8,128)(2,1)S(1)} %get-tuple-element.11), channel_id=1, source_target_pairs={{0,3},{1,0},{2,1},{3,2},{4,7},{5,4},{6,5},{7,6},{8,11},{9,8},{10,9... | collective-permute-start | bytes 393224 | tf_op jit(solution)/shard_map/ppermute | solution.py:31
  95.6 6.2 %collective-permute-done.3 = bf16[64,1024]{1,0:T(8,128)(2,1)S(1)} collective-permute-done((bf16[64,1024]{1,0:T(8,128)(2,1)S(1)}, bf16[64,1024]{1,0:T(8,128)(2,1)S(1)}, u32[]{:S(2)}, u32[]{:S(2)}) %collective-permute-start.3) | collective-permute-done | bytes 131104 | tf_op jit(solution)/shard_map/ppermute | solution.py:31
  102.0 2.9 %collective-permute-start.6 = (bf16[64,1024]{1,0:T(8,128)(2,1)S(1)}, bf16[64,1024]{1,0:T(8,128)(2,1)S(1)}, u32[]{:S(2)}, u32[]{:S(2)}) collective-permute-start(bf16[64,1024]{1,0:T(8,128)(2,1)S(1)} %get-tuple-element.3), channel_id=1, source_target_pairs={{0,3},{1,0},{2,1},{3,2},{4,7},{5,4},{6,5},{7,6},{8,11},{9,8},{10,9... | collective-permute-start | bytes 393224 | tf_op jit(solution)/shard_map/ppermute | solution.py:39
  105.6 2.9 %collective-permute-done.6 = bf16[64,1024]{1,0:T(8,128)(2,1)S(1)} collective-permute-done((bf16[64,1024]{1,0:T(8,128)(2,1)S(1)}, bf16[64,1024]{1,0:T(8,128)(2,1)S(1)}, u32[]{:S(2)}, u32[]{:S(2)}) %collective-permute-start.6) | collective-permute-done | bytes 131104 | tf_op jit(solution)/shard_map/ppermute | solution.py:39
  108.5 1.9 %collective-permute-done.7 = bf16[64,1024]{1,0:T(8,128)(2,1)S(1)} collective-permute-done((bf16[64,1024]{1,0:T(8,128)(2,1)S(1)}, bf16[64,1024]{1,0:T(8,128)(2,1)S(1)}, u32[]{:S(2)}, u32[]{:S(2)}) %collective-permute-start.7) | collective-permute-done | bytes 131104 | tf_op jit(solution)/shard_map/ppermute | solution.py:39
  110.4 3.9 %collective-permute-done.8 = bf16[64,1024]{1,0:T(8,128)(2,1)S(1)} collective-permute-done((bf16[64,1024]{1,0:T(8,128)(2,1)S(1)}, bf16[64,1024]{1,0:T(8,128)(2,1)S(1)}, u32[]{:S(2)}, u32[]{:S(2)}) %collective-permute-start.8) | collective-permute-done | bytes 131104 | tf_op jit(solution)/shard_map/ppermute | solution.py:39
  116.7 1.5 convolution_convert_fusion
  118.2 6.2 %all-to-all-start.1 = ((bf16[64,32,256]{2,1,0:T(8,128)(2,1)}), bf16[64,32,256]{2,1,0:T(8,128)(2,1)S(1)}, u32[]{:S(2)}, u32[]{:S(2)}) async-start(bf16[64,32,256]{2,1,0:T(8,128)(2,1)} %bitcast.112), calls=%async_computation.1 | async-start | bytes 2097152 | tf_op jit(solution)/shard_map/all_to_all | solution.py:151
  124.5 3.8 %add_convert_fusion = bf16[256,2048]{1,0:T(8,128)(2,1)} fusion(s32[256]{0:T(256)S(1)} %bitcast.131, s32[256]{0:T(256)S(1)} %bitcast.132, s32[256]{0:T(256)S(1)} %bitcast.124, s32[256]{0:T(256)S(1)} %bitcast.125, s32[256]{0:T(256)S(1)} %bitcast.126, s32[256]{0:T(256)S(1)} %bitcast.127, s32[256]{0:T(256)S(1)} %bitcast.128, s32[256]{0:T(256)S(1)} %bitcast.129, ...), kind=kLoop, calls=%fused_computation.17 | loop fusion | flops 15728640 | bytes 1058816 | tf_op jit(solution)/shard_map/convert_element_type | solution.py:118
  128.3 24.3 %all-to-all-done.1 = bf16[64,32,256]{2,1,0:T(8,128)(2,1)S(1)} async-done(((bf16[64,32,256]{2,1,0:T(8,128)(2,1)}), bf16[64,32,256]{2,1,0:T(8,128)(2,1)S(1)}, u32[]{:S(2)}, u32[]{:S(2)}) %all-to-all-start.1) | async-done | bytes 1048608 | tf_op jit(solution)/shard_map/all_to_all | solution.py:151
  152.6 3.1 %fusion.30 = f32[256,1024]{1,0:T(8,128)} fusion(bf16[256,1024]{1,0:T(8,128)(2,1)S(1)} %copy-done.4, bf16[256,2048]{1,0:T(8,128)(2,1)} %add_convert_fusion, bf16[2048,256]{1,0:T(8,128)(2,1)S(1)} %bitcast.109), kind=kOutput, calls=%fused_computation.51 | convolution fusion | flops 402784256 | bytes 3670016 | tf_op jit(solution)/shard_map/dot_general | solution.py:160
  155.7 1.8 %fusion.22 = bf16[256,1024]{1,0:T(8,128)(2,1)S(1)} fusion(f32[256,1024]{1,0:T(8,128)} %fusion.30, bf16[256,1024]{1,0:T(8,128)(2,1)} %param.36, bf16[256,256]{1,0:T(8,128)(2,1)S(1)} %fusion.58, s32[256]{0:T(256)S(1)} %copy-done.11), kind=kOutput, calls=%fused_computation.41 | convolution fusion | flops 168427520 | bytes 2229248 | tf_op jit(solution)/shard_map/dot_general | solution.py:161
  159.6 3.7 %collective-permute-done.10 = bf16[64,1024]{1,0:T(8,128)(2,1)S(1)} collective-permute-done((bf16[64,1024]{1,0:T(8,128)(2,1)S(1)}, bf16[64,1024]{1,0:T(8,128)(2,1)S(1)}, u32[]{:S(2)}, u32[]{:S(2)}) %collective-permute-start.10) | collective-permute-done | bytes 131104 | tf_op jit(solution)/shard_map/ppermute | solution.py:31
  164.3 2.6 %collective-permute-done.9 = bf16[64,1024]{1,0:T(8,128)(2,1)S(1)} collective-permute-done((bf16[64,1024]{1,0:T(8,128)(2,1)S(1)}, bf16[64,1024]{1,0:T(8,128)(2,1)S(1)}, u32[]{:S(2)}, u32[]{:S(2)}) %collective-permute-start.9) | collective-permute-done | bytes 131104 | tf_op jit(solution)/shard_map/ppermute | solution.py:31
  (101 shorter events, 21.2 us)
Async XLA Ops:
  0.6 48.5 %copy-start = (bf16[3,1024,256]{2,1,0:T(8,128)(2,1)S(1)}, bf16[3,1024,256]{2,1,0:T(8,128)(2,1)}, u32[]{:S(2)}) copy-start(bf16[3,1024,256]{2,1,0:T(8,128)(2,1)} %param.29) | copy-start | bytes 4718596
  4.4 44.7 %copy-start.2 = (bf16[256,1024]{1,0:T(8,128)(2,1)S(1)}, bf16[256,1024]{1,0:T(8,128)(2,1)}, u32[]{:S(2)}) copy-start(bf16[256,1024]{1,0:T(8,128)(2,1)} %param.22) | copy-start | bytes 1572868
  4.4 44.7 %copy-start.14 = (f32[3,256]{1,0:T(4,128)S(1)}, f32[3,256]{1,0:T(4,128)}, u32[]{:S(2)}) copy-start(f32[3,256]{1,0:T(4,128)} %param.31) | copy-start | bytes 9220
  46.0 14.9 %collective-permute-start = (bf16[9,64,512]{2,1,0:T(8,128)(2,1)S(1)}, bf16[9,64,512]{2,1,0:T(8,128)(2,1)}, u32[]{:S(2)}, u32[]{:S(2)}) collective-permute-start(bf16[9,64,512]{2,1,0:T(8,128)(2,1)S(1)} %copy.67), channel_id=1, source_target_pairs={{0,3},{1,0},{2,1},{3,2},{4,7},{5,4},{6,5},{7,6},{8,11},{9,8},{10,9... | collective-permute-start | bytes 1769480 | tf_op jit(solution)/shard_map/ppermute | solution.py:101
  48.6 15.1 %collective-permute-start.1 = (bf16[9,64,512]{2,1,0:T(8,128)(2,1)S(1)}, bf16[9,64,512]{2,1,0:T(8,128)(2,1)}, u32[]{:S(2)}, u32[]{:S(2)}) collective-permute-start(bf16[9,64,512]{2,1,0:T(8,128)(2,1)S(1)} %copy.67), channel_id=1, source_target_pairs={{0,2},{1,3},{2,0},{3,1},{4,6},{5,7},{6,4},{7,5},{8,10},{9,11},{10,... | collective-permute-start | bytes 1769480 | tf_op jit(solution)/shard_map/ppermute | solution.py:101
  50.8 27.3 %collective-permute-start.2 = (bf16[9,64,512]{2,1,0:T(8,128)(2,1)S(1)}, bf16[9,64,512]{2,1,0:T(8,128)(2,1)}, u32[]{:S(2)}, u32[]{:S(2)}) collective-permute-start(bf16[9,64,512]{2,1,0:T(8,128)(2,1)S(1)} %copy.67), channel_id=1, source_target_pairs={{0,1},{1,2},{2,3},{3,0},{4,5},{5,6},{6,7},{7,4},{8,9},{9,10},{10,1... | collective-permute-start | bytes 1769480 | tf_op jit(solution)/shard_map/ppermute | solution.py:101
  80.7 5.6 %copy-start.17 = (f32[512]{0:T(512)S(1)}, f32[512]{0:T(512)}, u32[]{:S(2)}) copy-start(f32[512]{0:T(512)} %param.25) | copy-start | bytes 6148
  92.8 8.9 %collective-permute-start.3 = (bf16[64,1024]{1,0:T(8,128)(2,1)S(1)}, bf16[64,1024]{1,0:T(8,128)(2,1)S(1)}, u32[]{:S(2)}, u32[]{:S(2)}) collective-permute-start(bf16[64,1024]{1,0:T(8,128)(2,1)S(1)} %get-tuple-element.9), channel_id=1, source_target_pairs={{0,1},{1,2},{2,3},{3,0},{4,5},{5,6},{6,7},{7,4},{8,9},{9,10},{10,1... | collective-permute-start | bytes 393224 | tf_op jit(solution)/shard_map/ppermute | solution.py:31
  92.9 8.9 %collective-permute-start.4 = (bf16[64,1024]{1,0:T(8,128)(2,1)S(1)}, bf16[64,1024]{1,0:T(8,128)(2,1)S(1)}, u32[]{:S(2)}, u32[]{:S(2)}) collective-permute-start(bf16[64,1024]{1,0:T(8,128)(2,1)S(1)} %get-tuple-element.10), channel_id=1, source_target_pairs={{0,2},{1,3},{2,0},{3,1},{4,6},{5,7},{6,4},{7,5},{8,10},{9,11},{10,... | collective-permute-start | bytes 393224 | tf_op jit(solution)/shard_map/ppermute | solution.py:31
  93.7 8.2 %collective-permute-start.5 = (bf16[64,1024]{1,0:T(8,128)(2,1)S(1)}, bf16[64,1024]{1,0:T(8,128)(2,1)S(1)}, u32[]{:S(2)}, u32[]{:S(2)}) collective-permute-start(bf16[64,1024]{1,0:T(8,128)(2,1)S(1)} %get-tuple-element.11), channel_id=1, source_target_pairs={{0,3},{1,0},{2,1},{3,2},{4,7},{5,4},{6,5},{7,6},{8,11},{9,8},{10,9... | collective-permute-start | bytes 393224 | tf_op jit(solution)/shard_map/ppermute | solution.py:31
  102.0 12.4 %copy-start.12 = (bf16[3,1024,256]{2,1,0:T(8,128)(2,1)S(1)}, bf16[3,1024,256]{2,1,0:T(8,128)(2,1)}, u32[]{:S(2)}) copy-start(bf16[3,1024,256]{2,1,0:T(8,128)(2,1)} %param.28) | copy-start | bytes 4718596
  102.0 12.4 %copy-start.15 = (f32[1024]{0:T(1024)S(1)}, f32[1024]{0:T(1024)}, u32[]{:S(2)}) copy-start(f32[1024]{0:T(1024)} %param.27) | copy-start | bytes 12292
  102.0 12.4 %copy-start.16 = (f32[3,256]{1,0:T(4,128)S(1)}, f32[3,256]{1,0:T(4,128)}, u32[]{:S(2)}) copy-start(f32[3,256]{1,0:T(4,128)} %param.30) | copy-start | bytes 9220
  102.0 6.5 %collective-permute-start.6 = (bf16[64,1024]{1,0:T(8,128)(2,1)S(1)}, bf16[64,1024]{1,0:T(8,128)(2,1)S(1)}, u32[]{:S(2)}, u32[]{:S(2)}) collective-permute-start(bf16[64,1024]{1,0:T(8,128)(2,1)S(1)} %get-tuple-element.3), channel_id=1, source_target_pairs={{0,3},{1,0},{2,1},{3,2},{4,7},{5,4},{6,5},{7,6},{8,11},{9,8},{10,9... | collective-permute-start | bytes 393224 | tf_op jit(solution)/shard_map/ppermute | solution.py:39
  104.9 5.4 %collective-permute-start.7 = (bf16[64,1024]{1,0:T(8,128)(2,1)S(1)}, bf16[64,1024]{1,0:T(8,128)(2,1)S(1)}, u32[]{:S(2)}, u32[]{:S(2)}) collective-permute-start(bf16[64,1024]{1,0:T(8,128)(2,1)S(1)} %get-tuple-element.3), channel_id=1, source_target_pairs={{0,2},{1,3},{2,0},{3,1},{4,6},{5,7},{6,4},{7,5},{8,10},{9,11},{10,... | collective-permute-start | bytes 393224 | tf_op jit(solution)/shard_map/ppermute | solution.py:39
  104.9 9.3 %collective-permute-start.8 = (bf16[64,1024]{1,0:T(8,128)(2,1)S(1)}, bf16[64,1024]{1,0:T(8,128)(2,1)S(1)}, u32[]{:S(2)}, u32[]{:S(2)}) collective-permute-start(bf16[64,1024]{1,0:T(8,128)(2,1)S(1)} %get-tuple-element.3), channel_id=1, source_target_pairs={{0,1},{1,2},{2,3},{3,0},{4,5},{5,6},{6,7},{7,4},{8,9},{9,10},{10,1... | collective-permute-start | bytes 393224 | tf_op jit(solution)/shard_map/ppermute | solution.py:39
  116.6 39.0 %copy-start.5 = (bf16[256,256]{1,0:T(8,128)(2,1)}, bf16[256,256]{1,0:T(8,128)(2,1)S(1)}, u32[]{:S(2)}) copy-start(bf16[256,256]{1,0:T(8,128)(2,1)S(1)} %fusion.58) | copy-start | bytes 393220
  116.7 7.8 %copy-start.7 = (s32[256,10]{0,1:T(8,128)S(1)}, s32[256,10]{0,1:T(8,128)}, u32[]{:S(2)}) copy-start(s32[256,10]{0,1:T(8,128)} %param.33) | copy-start | bytes 30724
  118.2 34.4 %copy-start.4 = (bf16[256,1024]{1,0:T(8,128)(2,1)S(1)}, bf16[256,1024]{1,0:T(8,128)(2,1)}, u32[]{:S(2)}) copy-start(bf16[256,1024]{1,0:T(8,128)(2,1)} %param.35) | copy-start | bytes 1572868
  118.2 34.4 %all-to-all-start.1 = ((bf16[64,32,256]{2,1,0:T(8,128)(2,1)}), bf16[64,32,256]{2,1,0:T(8,128)(2,1)S(1)}, u32[]{:S(2)}, u32[]{:S(2)}) async-start(bf16[64,32,256]{2,1,0:T(8,128)(2,1)} %bitcast.112), calls=%async_computation.1 | async-start | bytes 2097152 | tf_op jit(solution)/shard_map/all_to_all | solution.py:151
  155.7 11.1 %copy-start.8 = (f32[1024]{0:T(1024)S(1)}, f32[1024]{0:T(1024)}, u32[]{:S(2)}) copy-start(f32[1024]{0:T(1024)} %param.37) | copy-start | bytes 12292
  157.8 5.5 %collective-permute-start.10 = (bf16[64,1024]{1,0:T(8,128)(2,1)S(1)}, bf16[64,1024]{1,0:T(8,128)(2,1)S(1)}, u32[]{:S(2)}, u32[]{:S(2)}) collective-permute-start(bf16[64,1024]{1,0:T(8,128)(2,1)S(1)} %get-tuple-element.7), channel_id=1, source_target_pairs={{0,2},{1,3},{2,0},{3,1},{4,6},{5,7},{6,4},{7,5},{8,10},{9,11},{10,... | collective-permute-start | bytes 393224 | tf_op jit(solution)/shard_map/ppermute | solution.py:31
  158.1 6.2 %collective-permute-start.11 = (bf16[64,1024]{1,0:T(8,128)(2,1)S(1)}, bf16[64,1024]{1,0:T(8,128)(2,1)S(1)}, u32[]{:S(2)}, u32[]{:S(2)}) collective-permute-start(bf16[64,1024]{1,0:T(8,128)(2,1)S(1)} %get-tuple-element.8), channel_id=1, source_target_pairs={{0,3},{1,0},{2,1},{3,2},{4,7},{5,4},{6,5},{7,6},{8,11},{9,8},{10,9... | collective-permute-start | bytes 393224 | tf_op jit(solution)/shard_map/ppermute | solution.py:31
  159.0 7.8 %collective-permute-start.9 = (bf16[64,1024]{1,0:T(8,128)(2,1)S(1)}, bf16[64,1024]{1,0:T(8,128)(2,1)S(1)}, u32[]{:S(2)}, u32[]{:S(2)}) collective-permute-start(bf16[64,1024]{1,0:T(8,128)(2,1)S(1)} %get-tuple-element.6), channel_id=1, source_target_pairs={{0,1},{1,2},{2,3},{3,0},{4,5},{5,6},{6,7},{7,4},{8,9},{9,10},{10,1... | collective-permute-start | bytes 393224 | tf_op jit(solution)/shard_map/ppermute | solution.py:31
  (7 other events, 18.2 us)

commit v5 on v4

--- a/solution.py
+++ b/solution.py
@@ -84,32 +84,28 @@
     per = capacity // share_count
     low = mp_index * per
     in_range = (place >= low) & (place < low + per)
-    local = jnp.where(in_range, (place - low) * owner_count + owner, -1)
-    route = one_hot_t(local, per * owner_count)
+    local = jnp.where(in_range, owner * per + (place - low), -1)
+    route = one_hot_t(local, owner_count * per)
     feat_width = event_feats.shape[1]
     feat_part = jnp.dot(route, event_feats, preferred_element_type=F32).astype(BF16)
     slot_col = jnp.broadcast_to((event_slot + 1).astype(BF16)[:, None], (event_rows, 128))
     id_part = jnp.dot(route, slot_col, preferred_element_type=F32)[:, 0] - 1.0
-    id_plane = jnp.pad(id_part.reshape(per, owner_count).T, ((0, 0), (0, feat_width - per)))
+    id_block = jnp.pad(id_part.reshape(owner_count, per), ((0, 0), (0, 128 - per)))
     payload = jnp.concatenate(
-        [feat_part.reshape(per, owner_count, feat_width), id_plane.astype(BF16)[None]], axis=0
-    )
-    landed = lax.all_to_all(payload, "nodes", split_axis=1, concat_axis=1, tiled=True)
-    pieces = [landed]
+        [feat_part.reshape(owner_count, per * feat_width), id_block.astype(BF16)], axis=1
+    )
+    landed = lax.all_to_all(payload, "nodes", split_axis=0, concat_axis=0, tiled=True)
+    piece_rows = owner_count * per
+    id_row = landed[:, per * feat_width : per * feat_width + per].reshape(1, piece_rows)
+    id_rows = jnp.pad(id_row, ((0, 15), (0, feat_width - piece_rows)))
+    mine = jnp.concatenate(
+        [landed[:, : per * feat_width].reshape(piece_rows, feat_width), id_rows], axis=0
+    )
+    pieces = [mine]
     for t in range(1, share_count):
         pieces.append(
-            lax.ppermute(landed, "mp", [(i, (i - t) % share_count) for i in range(share_count)])
+            lax.ppermute(mine, "mp", [(i, (i - t) % share_count) for i in range(share_count)])
         )
-    arrived = jnp.concatenate(
-        [p[:per].reshape(per * owner_count, feat_width) for p in pieces], axis=0
-    )
-    arrived_ids = jnp.concatenate(
-        [p[per, :, :per].T.reshape(per * owner_count) for p in pieces], axis=0
-    ).astype(jnp.int32)
-
-    seg = one_hot_t(arrived_ids, mem_rows)
-    seg_t = one_hot(arrived_ids, mem_rows)
-    counts = jnp.sum(seg.astype(F32), axis=1)
 
     recv_rows = state_slots.shape[0] * state_slots.shape[1]
     neigh_count = one_hot(neighbours[:, 0], recv_rows, F32)
@@ -119,11 +115,21 @@
     state_proj = jnp.dot(memory, w_msg_state, preferred_element_type=F32)
     sp_hi = state_proj.astype(BF16)
     sp_lo = (state_proj - sp_hi.astype(F32)).astype(BF16)
-    lhs = jnp.concatenate([arrived, seg_t, seg_t], axis=1)
     rhs = jnp.concatenate([w_msg_event, sp_hi, sp_lo], axis=0)
-    pre = jnp.dot(lhs, rhs, preferred_element_type=F32) + b_msg
-    hidden_msg = jax.nn.relu(pre).astype(BF16)
-    hidden_sum = jnp.dot(seg, hidden_msg, preferred_element_type=F32)
+
+    hidden_sum = None
+    counts = None
+    for p in pieces:
+        ids_p = p[piece_rows, :piece_rows].astype(jnp.int32)
+        seg_t = one_hot(ids_p, mem_rows)
+        seg = one_hot_t(ids_p, mem_rows)
+        lhs = jnp.concatenate([p[:piece_rows], seg_t, seg_t], axis=1)
+        pre = jnp.dot(lhs, rhs, preferred_element_type=F32) + b_msg
+        hidden_msg = jax.nn.relu(pre).astype(BF16)
+        part = jnp.dot(seg, hidden_msg, preferred_element_type=F32)
+        cnt = jnp.sum(seg.astype(F32), axis=1)
+        hidden_sum = part if hidden_sum is None else hidden_sum + part
+        counts = cnt if counts is None else counts + cnt
     partial_total = split_dot(hidden_sum, w_msg_out)
 
     divisor = jnp.maximum(counts, 1.0)[:, None]

time: 168 us -> 159 us (0.946)
  blocking collectives: 41.2 us -> 0 us
  starting transfers between devices: 18.1 us -> 34.8 us
  waiting for transfers between devices: 67.8 us -> 77 us
  matrix products: 20 us -> 26.5 us
  local copies, waits for them, and re-layouts: 11.4 us -> 7.31 us
  other arithmetic: 8.02 us -> 11 us
    all_to_all x1 -> x0, blocking collectives: 41.2 us -> none  [per_device(): lax.all_to_all(payload, 'nodes', split_axis=1, concat_axis=1, tiled=True)]
    all_to_all x0 -> x1, waiting for transfers between devices: none -> 14.1 us  [per_device(): lax.all_to_all(payload, 'nodes', split_axis=0, concat_axis=0, tiled=True)]
    all_to_all x0 -> x1, starting transfers between devices: none -> 13.3 us  [per_device(): lax.all_to_all(payload, 'nodes', split_axis=0, concat_axis=0, tiled=True)]
    dot_general x1 -> x4, matrix products: 5.39 us -> 11.8 us  [per_device(): part = jnp.dot(seg, hidden_msg, preferred_element_type=F32)]
    ppermute x3, waiting for transfers between devices: 21.4 us -> 17.4 us  [per_device(): lax.ppermute(mine, 'mp', [(i, (i - t) % share_count) for i in range(share...]
    slice x5 -> x4, local copies, waits for them, and re-layouts: 6.51 us -> 3.03 us  [the longest x3 2.99 us: per_device(): lhs = jnp.concatenate([p[:piece_rows], seg_t, seg_t], axis=1)]
    transpose x6 -> x0, local copies, waits for them, and re-layouts: 2.38 us -> none  [per_device(): p[per, :, :per].T.reshape(per * owner_count)]
    ppermute x6, starting transfers between devices: 4.52 us -> 6.8 us  [mp_reduce_scatter(): got = lax.ppermute(ahead[t], axis, [(i, (i + t) % n) for i in range(n)])]
  transfers between devices with their start and end apart: 13 -> 14, of which waited for: 12 -> 12; matrix products, arithmetic and copies ran while one was open for 6% -> 9% of each run, Pallas kernels for 0% -> 0%
where the time goes in v5:
time: 159 us; the launch traced here: 158 us
  waiting for transfers between devices  77 us (48%)
  starting transfers between devices  34.8 us (22%)
  matrix products  26.5 us (17%)
  other arithmetic  11 us (7%)
  local copies, waits for them, and re-layouts  7.31 us (5%)
    all_to_all x1, waiting for transfers between devices, per_device(): lax.all_to_all(outgoing, 'nodes', split_axis=0, concat_axis=0, tiled=True)  24.3 us
    ppermute x3, waiting for transfers between devices, per_device(): lax.ppermute(mine, 'mp', [(i, (i - t) % share_count) for i in range(share...  17.4 us
    all_to_all x1, waiting for transfers between devices, per_device(): lax.all_to_all(payload, 'nodes', split_axis=0, concat_axis=0, tiled=True)  14.1 us
    all_to_all x1, starting transfers between devices, per_device(): lax.all_to_all(payload, 'nodes', split_axis=0, concat_axis=0, tiled=True)  13.3 us
    ppermute x6, waiting for transfers between devices, mp_reduce_scatter(): got = lax.ppermute(ahead[t], axis, [(i, (i + t) % n) for i in range(n)])  12.3 us
    dot_general x4, matrix products, per_device(): part = jnp.dot(seg, hidden_msg, preferred_element_type=F32)  11.8 us
    ppermute x3, waiting for transfers between devices, mp_all_gather(): rel.append(lax.ppermute(piece, axis, [(i, (i - t) % n) for i in range(n)]))  8.84 us
    ppermute x6, starting transfers between devices, mp_reduce_scatter(): got = lax.ppermute(ahead[t], axis, [(i, (i + t) % n) for i in range(n)])  6.8 us
  transfers between devices with their start and end apart: 14, of which 12 were waited for; matrix products, arithmetic and copies ran while one was open for 9% of the time, Pallas kernels for 0%

profile of v5, /device:TPU:1, one launch (start us, length us, event | category | flops | bytes accessed | tf_op | source)
XLA Modules:
  0.0 157.8 jit_solution(11400490836746788470)
XLA Ops:
  6.8 13.3 %all-to-all-start = ((bf16[64,2,2112]{2,1,0:T(2,128)(2,1)}), bf16[64,2,2112]{2,1,0:T(2,128)(2,1)S(1)}, u32[]{:S(2)}, u32[]{:S(2)}) async-start(bf16[64,2,2112]{2,1,0:T(2,128)(2,1)} %reshape.148), calls=%async_computation | async-start | bytes 1114112 | tf_op jit(solution)/shard_map/all_to_all | solution.py:97
  20.2 2.6 %fusion.152 = (bf16[256,512]{1,0:T(8,128)(2,1)}, bf16[256,512]{1,0:T(8,128)(2,1)}) fusion(bf16[256,1024]{1,0:T(8,128)(2,1)} %param.22, bf16[1024,512]{1,0:T(8,128)(2,1)} %param.24), kind=kOutput, calls=%fused_computation.210 | convolution fusion | flops 268959744 | bytes 2097152 | tf_op jit(solution)/shard_map/dot_general | solution.py:115
  24.3 14.1 %all-to-all-done = bf16[64,2,2112]{2,1,0:T(2,128)(2,1)S(1)} async-done(((bf16[64,2,2112]{2,1,0:T(2,128)(2,1)}), bf16[64,2,2112]{2,1,0:T(2,128)(2,1)S(1)}, u32[]{:S(2)}, u32[]{:S(2)}) %all-to-all-start) | async-done | bytes 540704 | tf_op jit(solution)/shard_map/all_to_all | solution.py:97
  39.5 2.8 %collective-permute-start.1 = (bf16[528,512]{1,0:T(8,128)(2,1)S(1)}, bf16[528,512]{1,0:T(8,128)(2,1)}, u32[]{:S(2)}, u32[]{:S(2)}) collective-permute-start(bf16[528,512]{1,0:T(8,128)(2,1)S(1)} %fusion.77), channel_id=1, source_target_pairs={{0,2},{1,3},{2,0},{3,1},{4,6},{5,7},{6,4},{7,5},{8,10},{9,11},{10,... | collective-permute-start | bytes 1622024 | tf_op jit(solution)/shard_map/ppermute | solution.py:107
  42.7 2.4 %collective-permute-start = (bf16[528,512]{1,0:T(8,128)(2,1)S(1)}, bf16[528,512]{1,0:T(8,128)(2,1)}, u32[]{:S(2)}, u32[]{:S(2)}) collective-permute-start(bf16[528,512]{1,0:T(8,128)(2,1)S(1)} %fusion.77), channel_id=1, source_target_pairs={{0,3},{1,0},{2,1},{3,2},{4,7},{5,4},{6,5},{7,6},{8,11},{9,8},{10,9... | collective-permute-start | bytes 1622024 | tf_op jit(solution)/shard_map/ppermute | solution.py:107
  45.3 2.9 %fusion.19 = f32[256,512]{1,0:T(8,128)} fusion(bf16[512,256]{1,0:T(8,128)(2,1)S(1)} %fusion.99, bf16[512,512]{1,0:T(8,128)(2,1)S(1)} %reshape.125, f32[512]{0:T(512)S(1)} %copy-done.19, s32[512]{0:T(512)S(1)} %reshape.130, bf16[256,512]{1,0:T(8,128)(2,1)} %get-tuple-element.15, bf16[256,512]{1,0:T(8,128)(2,1)} %get-tuple-element.14, bf16[512,512]{1,0:T(8,128)(2,1)} %param.23), kind=kOutput, calls=%fused_computation.42 | convolution fusion | flops 678297600 | bytes 2363392 | tf_op jit(solution)/shard_map/dot_general | solution.py:129
  48.2 6.5 %collective-permute-done.1 = bf16[528,512]{1,0:T(8,128)(2,1)} collective-permute-done((bf16[528,512]{1,0:T(8,128)(2,1)S(1)}, bf16[528,512]{1,0:T(8,128)(2,1)}, u32[]{:S(2)}, u32[]{:S(2)}) %collective-permute-start.1) | collective-permute-done | bytes 540704 | tf_op jit(solution)/shard_map/ppermute | solution.py:107
  55.4 11.0 %collective-permute-done = bf16[528,512]{1,0:T(8,128)(2,1)} collective-permute-done((bf16[528,512]{1,0:T(8,128)(2,1)S(1)}, bf16[528,512]{1,0:T(8,128)(2,1)}, u32[]{:S(2)}, u32[]{:S(2)}) %collective-permute-start) | collective-permute-done | bytes 540704 | tf_op jit(solution)/shard_map/ppermute | solution.py:107
  70.4 3.1 %fusion.17 = f32[256,512]{1,0:T(8,128)} fusion(bf16[512,256]{1,0:T(8,128)(2,1)} %fusion.101, bf16[512,512]{1,0:T(8,128)(2,1)S(1)} %slice.141, f32[512]{0:T(512)S(1)} %copy-done.19, s32[512]{0:T(512)S(1)} %bitcast.109, bf16[256,512]{1,0:T(8,128)(2,1)} %get-tuple-element.15, bf16[256,512]{1,0:T(8,128)(2,1)} %get-tuple-element.14, bf16[512,512]{1,0:T(8,128)(2,1)} %param.23), kind=kOutput, calls=%fused_computation.40 | convolution fusion | flops 678297600 | bytes 2363392 | tf_op jit(solution)/shard_map/dot_general | solution.py:129
  74.6 3.1 %fusion.22 = f32[256,512]{1,0:T(8,128)} fusion(f32[256,512]{1,0:T(8,128)} %fusion.17, f32[256,512]{1,0:T(8,128)} %fusion.19, bf16[512,256]{1,0:T(8,128)(2,1)S(1)} %fusion.100, bf16[512,512]{1,0:T(8,128)(2,1)S(1)} %slice.140, f32[512]{0:T(512)S(1)} %copy-done.19, s32[512]{0:T(512)S(1)} %bitcast.103, bf16[256,512]{1,0:T(8,128)(2,1)S(1)} %copy-done.7, ...), kind=kOutput, calls=%fused_computation.45 | convolution fusion | flops 678559744 | bytes 3411968 | tf_op jit(solution)/shard_map/dot_general | solution.py:129
  78.5 2.7 %fusion.21 = f32[256,512]{1,0:T(8,128)S(1)} fusion(f32[256,512]{1,0:T(8,128)} %fusion.22, bf16[512,256]{1,0:T(8,128)(2,1)} %fusion.102, bf16[512,512]{1,0:T(8,128)(2,1)} %slice.142, f32[512]{0:T(512)S(1)} %copy-done.19, s32[512]{0:T(512)S(1)} %bitcast.106, bf16[256,512]{1,0:T(8,128)(2,1)} %get-tuple-element.15, bf16[256,512]{1,0:T(8,128)(2,1)} %get-tuple-element.14, ...), kind=kOutput, calls=%fused_computation.44 | convolution fusion | flops 678428672 | bytes 2887680 | tf_op jit(solution)/shard_map/dot_general | solution.py:129
  82.3 2.0 %collective-permute-start.3 = (bf16[64,1024]{1,0:T(8,128)(2,1)S(1)}, bf16[64,1024]{1,0:T(8,128)(2,1)S(1)}, u32[]{:S(2)}, u32[]{:S(2)}) collective-permute-start(bf16[64,1024]{1,0:T(8,128)(2,1)S(1)} %get-tuple-element.11), channel_id=1, source_target_pairs={{0,1},{1,2},{2,3},{3,0},{4,5},{5,6},{6,7},{7,4},{8,9},{9,10},{10,1... | collective-permute-start | bytes 393224 | tf_op jit(solution)/shard_map/ppermute | solution.py:31
  84.3 2.4 %collective-permute-start.4 = (bf16[64,1024]{1,0:T(8,128)(2,1)S(1)}, bf16[64,1024]{1,0:T(8,128)(2,1)S(1)}, u32[]{:S(2)}, u32[]{:S(2)}) collective-permute-start(bf16[64,1024]{1,0:T(8,128)(2,1)S(1)} %get-tuple-element.12), channel_id=1, source_target_pairs={{0,2},{1,3},{2,0},{3,1},{4,6},{5,7},{6,4},{7,5},{8,10},{9,11},{10,... | collective-permute-start | bytes 393224 | tf_op jit(solution)/shard_map/ppermute | solution.py:31
  88.3 4.3 %collective-permute-done.4 = bf16[64,1024]{1,0:T(8,128)(2,1)S(1)} collective-permute-done((bf16[64,1024]{1,0:T(8,128)(2,1)S(1)}, bf16[64,1024]{1,0:T(8,128)(2,1)S(1)}, u32[]{:S(2)}, u32[]{:S(2)}) %collective-permute-start.4) | collective-permute-done | bytes 131104 | tf_op jit(solution)/shard_map/ppermute | solution.py:31
  92.8 2.8 %collective-permute-start.6 = (bf16[64,1024]{1,0:T(8,128)(2,1)S(1)}, bf16[64,1024]{1,0:T(8,128)(2,1)S(1)}, u32[]{:S(2)}, u32[]{:S(2)}) collective-permute-start(bf16[64,1024]{1,0:T(8,128)(2,1)S(1)} %get-tuple-element.5), channel_id=1, source_target_pairs={{0,3},{1,0},{2,1},{3,2},{4,7},{5,4},{6,5},{7,6},{8,11},{9,8},{10,9... | collective-permute-start | bytes 393224 | tf_op jit(solution)/shard_map/ppermute | solution.py:39
  96.2 3.0 %collective-permute-done.6 = bf16[64,1024]{1,0:T(8,128)(2,1)S(1)} collective-permute-done((bf16[64,1024]{1,0:T(8,128)(2,1)S(1)}, bf16[64,1024]{1,0:T(8,128)(2,1)S(1)}, u32[]{:S(2)}, u32[]{:S(2)}) %collective-permute-start.6) | collective-permute-done | bytes 131104 | tf_op jit(solution)/shard_map/ppermute | solution.py:39
  101.0 4.1 %collective-permute-done.8 = bf16[64,1024]{1,0:T(8,128)(2,1)S(1)} collective-permute-done((bf16[64,1024]{1,0:T(8,128)(2,1)S(1)}, bf16[64,1024]{1,0:T(8,128)(2,1)S(1)}, u32[]{:S(2)}, u32[]{:S(2)}) %collective-permute-start.8) | collective-permute-done | bytes 131104 | tf_op jit(solution)/shard_map/ppermute | solution.py:39
  109.1 5.8 %all-to-all-start.1 = ((bf16[64,32,256]{2,1,0:T(8,128)(2,1)}), bf16[64,32,256]{2,1,0:T(8,128)(2,1)S(1)}, u32[]{:S(2)}, u32[]{:S(2)}) async-start(bf16[64,32,256]{2,1,0:T(8,128)(2,1)} %bitcast.99), calls=%async_computation.1 | async-start | bytes 2097152 | tf_op jit(solution)/shard_map/all_to_all | solution.py:157
  114.9 3.8 %add_convert_fusion = bf16[256,2048]{1,0:T(8,128)(2,1)} fusion(s32[256]{0:T(256)S(1)} %bitcast.120, s32[256]{0:T(256)S(1)} %bitcast.121, s32[256]{0:T(256)S(1)} %bitcast.113, s32[256]{0:T(256)S(1)} %bitcast.114, s32[256]{0:T(256)S(1)} %bitcast.115, s32[256]{0:T(256)S(1)} %bitcast.116, s32[256]{0:T(256)S(1)} %bitcast.117, s32[256]{0:T(256)S(1)} %bitcast.118, ...), kind=kLoop, calls=%fused_computation.4 | loop fusion | flops 15728640 | bytes 1058816 | tf_op jit(solution)/shard_map/convert_element_type | solution.py:114
  118.7 24.3 %all-to-all-done.1 = bf16[64,32,256]{2,1,0:T(8,128)(2,1)S(1)} async-done(((bf16[64,32,256]{2,1,0:T(8,128)(2,1)}), bf16[64,32,256]{2,1,0:T(8,128)(2,1)S(1)}, u32[]{:S(2)}, u32[]{:S(2)}) %all-to-all-start.1) | async-done | bytes 1048608 | tf_op jit(solution)/shard_map/all_to_all | solution.py:157
  143.0 3.1 %fusion.26 = f32[256,1024]{1,0:T(8,128)} fusion(bf16[256,1024]{1,0:T(8,128)(2,1)S(1)} %copy-done.4, bf16[256,2048]{1,0:T(8,128)(2,1)} %add_convert_fusion, bf16[2048,256]{1,0:T(8,128)(2,1)S(1)} %bitcast.94), kind=kOutput, calls=%fused_computation.51 | convolution fusion | flops 402784256 | bytes 3670016 | tf_op jit(solution)/shard_map/dot_general | solution.py:166
  146.1 1.8 %fusion.13 = bf16[256,1024]{1,0:T(8,128)(2,1)S(1)} fusion(f32[256,1024]{1,0:T(8,128)} %fusion.26, bf16[256,1024]{1,0:T(8,128)(2,1)} %param.36, bf16[256,256]{1,0:T(8,128)(2,1)S(1)} %fusion.104, s32[256]{0:T(256)S(1)} %copy-done.13), kind=kOutput, calls=%fused_computation.34 | convolution fusion | flops 168427520 | bytes 2229248 | tf_op jit(solution)/shard_map/dot_general | solution.py:167
  150.4 3.3 %collective-permute-done.10 = bf16[64,1024]{1,0:T(8,128)(2,1)S(1)} collective-permute-done((bf16[64,1024]{1,0:T(8,128)(2,1)S(1)}, bf16[64,1024]{1,0:T(8,128)(2,1)S(1)}, u32[]{:S(2)}, u32[]{:S(2)}) %collective-permute-start.10) | collective-permute-done | bytes 131104 | tf_op jit(solution)/shard_map/ppermute | solution.py:31
  154.4 2.6 %collective-permute-done.9 = bf16[64,1024]{1,0:T(8,128)(2,1)S(1)} collective-permute-done((bf16[64,1024]{1,0:T(8,128)(2,1)S(1)}, bf16[64,1024]{1,0:T(8,128)(2,1)S(1)}, u32[]{:S(2)}, u32[]{:S(2)}) %collective-permute-start.9) | collective-permute-done | bytes 131104 | tf_op jit(solution)/shard_map/ppermute | solution.py:31
  (109 shorter events, 28.9 us)
Async XLA Ops:
  0.6 22.2 %copy-start = (bf16[3,1024,256]{2,1,0:T(8,128)(2,1)S(1)}, bf16[3,1024,256]{2,1,0:T(8,128)(2,1)}, u32[]{:S(2)}) copy-start(bf16[3,1024,256]{2,1,0:T(8,128)(2,1)} %param.29) | copy-start | bytes 4718596
  4.5 15.5 %copy-start.8 = (s32[64,32]{0,1:T(8,128)S(1)}, s32[64,32]{0,1:T(8,128)}, u32[]{:S(2)}) copy-start(s32[64,32]{0,1:T(8,128)} %param.32) | copy-start | bytes 24580
  6.8 16.1 %copy-start.2 = (bf16[256,1024]{1,0:T(8,128)(2,1)S(1)}, bf16[256,1024]{1,0:T(8,128)(2,1)}, u32[]{:S(2)}) copy-start(bf16[256,1024]{1,0:T(8,128)(2,1)} %param.22) | copy-start | bytes 1572868
  6.8 16.1 %copy-start.16 = (f32[3,256]{1,0:T(4,128)S(1)}, f32[3,256]{1,0:T(4,128)}, u32[]{:S(2)}) copy-start(f32[3,256]{1,0:T(4,128)} %param.31) | copy-start | bytes 9220
  6.8 31.6 %all-to-all-start = ((bf16[64,2,2112]{2,1,0:T(2,128)(2,1)}), bf16[64,2,2112]{2,1,0:T(2,128)(2,1)S(1)}, u32[]{:S(2)}, u32[]{:S(2)}) async-start(bf16[64,2,2112]{2,1,0:T(2,128)(2,1)} %reshape.148), calls=%async_computation | async-start | bytes 1114112 | tf_op jit(solution)/shard_map/all_to_all | solution.py:97
  39.5 15.1 %collective-permute-start.1 = (bf16[528,512]{1,0:T(8,128)(2,1)S(1)}, bf16[528,512]{1,0:T(8,128)(2,1)}, u32[]{:S(2)}, u32[]{:S(2)}) collective-permute-start(bf16[528,512]{1,0:T(8,128)(2,1)S(1)} %fusion.77), channel_id=1, source_target_pairs={{0,2},{1,3},{2,0},{3,1},{4,6},{5,7},{6,4},{7,5},{8,10},{9,11},{10,... | collective-permute-start | bytes 1622024 | tf_op jit(solution)/shard_map/ppermute | solution.py:107
  42.4 25.9 %collective-permute-start.2 = (bf16[528,512]{1,0:T(8,128)(2,1)S(1)}, bf16[528,512]{1,0:T(8,128)(2,1)S(1)}, u32[]{:S(2)}, u32[]{:S(2)}) collective-permute-start(bf16[528,512]{1,0:T(8,128)(2,1)S(1)} %fusion.77), channel_id=1, source_target_pairs={{0,1},{1,2},{2,3},{3,0},{4,5},{5,6},{6,7},{7,4},{8,9},{9,10},{10,1... | collective-permute-start | bytes 1622024 | tf_op jit(solution)/shard_map/ppermute | solution.py:107
  42.7 23.7 %collective-permute-start = (bf16[528,512]{1,0:T(8,128)(2,1)S(1)}, bf16[528,512]{1,0:T(8,128)(2,1)}, u32[]{:S(2)}, u32[]{:S(2)}) collective-permute-start(bf16[528,512]{1,0:T(8,128)(2,1)S(1)} %fusion.77), channel_id=1, source_target_pairs={{0,3},{1,0},{2,1},{3,2},{4,7},{5,4},{6,5},{7,6},{8,11},{9,8},{10,9... | collective-permute-start | bytes 1622024 | tf_op jit(solution)/shard_map/ppermute | solution.py:107
  82.3 6.0 %collective-permute-start.3 = (bf16[64,1024]{1,0:T(8,128)(2,1)S(1)}, bf16[64,1024]{1,0:T(8,128)(2,1)S(1)}, u32[]{:S(2)}, u32[]{:S(2)}) collective-permute-start(bf16[64,1024]{1,0:T(8,128)(2,1)S(1)} %get-tuple-element.11), channel_id=1, source_target_pairs={{0,1},{1,2},{2,3},{3,0},{4,5},{5,6},{6,7},{7,4},{8,9},{9,10},{10,1... | collective-permute-start | bytes 393224 | tf_op jit(solution)/shard_map/ppermute | solution.py:31
  84.3 8.4 %collective-permute-start.4 = (bf16[64,1024]{1,0:T(8,128)(2,1)S(1)}, bf16[64,1024]{1,0:T(8,128)(2,1)S(1)}, u32[]{:S(2)}, u32[]{:S(2)}) collective-permute-start(bf16[64,1024]{1,0:T(8,128)(2,1)S(1)} %get-tuple-element.12), channel_id=1, source_target_pairs={{0,2},{1,3},{2,0},{3,1},{4,6},{5,7},{6,4},{7,5},{8,10},{9,11},{10,... | collective-permute-start | bytes 393224 | tf_op jit(solution)/shard_map/ppermute | solution.py:31
  86.7 5.9 %collective-permute-start.5 = (bf16[64,1024]{1,0:T(8,128)(2,1)S(1)}, bf16[64,1024]{1,0:T(8,128)(2,1)S(1)}, u32[]{:S(2)}, u32[]{:S(2)}) collective-permute-start(bf16[64,1024]{1,0:T(8,128)(2,1)S(1)} %get-tuple-element.13), channel_id=1, source_target_pairs={{0,3},{1,0},{2,1},{3,2},{4,7},{5,4},{6,5},{7,6},{8,11},{9,8},{10,9... | collective-permute-start | bytes 393224 | tf_op jit(solution)/shard_map/ppermute | solution.py:31
  92.7 12.5 %copy-start.14 = (bf16[3,1024,256]{2,1,0:T(8,128)(2,1)S(1)}, bf16[3,1024,256]{2,1,0:T(8,128)(2,1)}, u32[]{:S(2)}) copy-start(bf16[3,1024,256]{2,1,0:T(8,128)(2,1)} %param.28) | copy-start | bytes 4718596
  92.7 12.5 %copy-start.17 = (f32[1024]{0:T(1024)S(1)}, f32[1024]{0:T(1024)}, u32[]{:S(2)}) copy-start(f32[1024]{0:T(1024)} %param.27) | copy-start | bytes 12292
  92.7 12.5 %copy-start.18 = (f32[3,256]{1,0:T(4,128)S(1)}, f32[3,256]{1,0:T(4,128)}, u32[]{:S(2)}) copy-start(f32[3,256]{1,0:T(4,128)} %param.30) | copy-start | bytes 9220
  92.8 6.5 %collective-permute-start.6 = (bf16[64,1024]{1,0:T(8,128)(2,1)S(1)}, bf16[64,1024]{1,0:T(8,128)(2,1)S(1)}, u32[]{:S(2)}, u32[]{:S(2)}) collective-permute-start(bf16[64,1024]{1,0:T(8,128)(2,1)S(1)} %get-tuple-element.5), channel_id=1, source_target_pairs={{0,3},{1,0},{2,1},{3,2},{4,7},{5,4},{6,5},{7,6},{8,11},{9,8},{10,9... | collective-permute-start | bytes 393224 | tf_op jit(solution)/shard_map/ppermute | solution.py:39
  95.6 5.4 %collective-permute-start.7 = (bf16[64,1024]{1,0:T(8,128)(2,1)S(1)}, bf16[64,1024]{1,0:T(8,128)(2,1)S(1)}, u32[]{:S(2)}, u32[]{:S(2)}) collective-permute-start(bf16[64,1024]{1,0:T(8,128)(2,1)S(1)} %get-tuple-element.5), channel_id=1, source_target_pairs={{0,2},{1,3},{2,0},{3,1},{4,6},{5,7},{6,4},{7,5},{8,10},{9,11},{10,... | collective-permute-start | bytes 393224 | tf_op jit(solution)/shard_map/ppermute | solution.py:39
  96.2 8.9 %collective-permute-start.8 = (bf16[64,1024]{1,0:T(8,128)(2,1)S(1)}, bf16[64,1024]{1,0:T(8,128)(2,1)S(1)}, u32[]{:S(2)}, u32[]{:S(2)}) collective-permute-start(bf16[64,1024]{1,0:T(8,128)(2,1)S(1)} %get-tuple-element.5), channel_id=1, source_target_pairs={{0,1},{1,2},{2,3},{3,0},{4,5},{5,6},{6,7},{7,4},{8,9},{9,10},{10,1... | collective-permute-start | bytes 393224 | tf_op jit(solution)/shard_map/ppermute | solution.py:39
  107.5 38.6 %copy-start.5 = (bf16[256,256]{1,0:T(8,128)(2,1)}, bf16[256,256]{1,0:T(8,128)(2,1)S(1)}, u32[]{:S(2)}) copy-start(bf16[256,256]{1,0:T(8,128)(2,1)S(1)} %fusion.104) | copy-start | bytes 393220
  109.1 33.9 %copy-start.4 = (bf16[256,1024]{1,0:T(8,128)(2,1)S(1)}, bf16[256,1024]{1,0:T(8,128)(2,1)}, u32[]{:S(2)}) copy-start(bf16[256,1024]{1,0:T(8,128)(2,1)} %param.35) | copy-start | bytes 1572868
  109.1 33.9 %all-to-all-start.1 = ((bf16[64,32,256]{2,1,0:T(8,128)(2,1)}), bf16[64,32,256]{2,1,0:T(8,128)(2,1)S(1)}, u32[]{:S(2)}, u32[]{:S(2)}) async-start(bf16[64,32,256]{2,1,0:T(8,128)(2,1)} %bitcast.99), calls=%async_computation.1 | async-start | bytes 2097152 | tf_op jit(solution)/shard_map/all_to_all | solution.py:157
  146.1 10.9 %copy-start.10 = (f32[1024]{0:T(1024)S(1)}, f32[1024]{0:T(1024)}, u32[]{:S(2)}) copy-start(f32[1024]{0:T(1024)} %param.37) | copy-start | bytes 12292
  148.2 5.4 %collective-permute-start.10 = (bf16[64,1024]{1,0:T(8,128)(2,1)S(1)}, bf16[64,1024]{1,0:T(8,128)(2,1)S(1)}, u32[]{:S(2)}, u32[]{:S(2)}) collective-permute-start(bf16[64,1024]{1,0:T(8,128)(2,1)S(1)} %get-tuple-element.9), channel_id=1, source_target_pairs={{0,2},{1,3},{2,0},{3,1},{4,6},{5,7},{6,4},{7,5},{8,10},{9,11},{10,... | collective-permute-start | bytes 393224 | tf_op jit(solution)/shard_map/ppermute | solution.py:31
  149.0 5.5 %collective-permute-start.11 = (bf16[64,1024]{1,0:T(8,128)(2,1)S(1)}, bf16[64,1024]{1,0:T(8,128)(2,1)S(1)}, u32[]{:S(2)}, u32[]{:S(2)}) collective-permute-start(bf16[64,1024]{1,0:T(8,128)(2,1)S(1)} %get-tuple-element.10), channel_id=1, source_target_pairs={{0,3},{1,0},{2,1},{3,2},{4,7},{5,4},{6,5},{7,6},{8,11},{9,8},{10,9... | collective-permute-start | bytes 393224 | tf_op jit(solution)/shard_map/ppermute | solution.py:31
  149.8 7.2 %collective-permute-start.9 = (bf16[64,1024]{1,0:T(8,128)(2,1)S(1)}, bf16[64,1024]{1,0:T(8,128)(2,1)S(1)}, u32[]{:S(2)}, u32[]{:S(2)}) collective-permute-start(bf16[64,1024]{1,0:T(8,128)(2,1)S(1)} %get-tuple-element.8), channel_id=1, source_target_pairs={{0,1},{1,2},{2,3},{3,0},{4,5},{5,6},{6,7},{7,4},{8,9},{9,10},{10,1... | collective-permute-start | bytes 393224 | tf_op jit(solution)/shard_map/ppermute | solution.py:31
  (10 other events, 32.9 us)

commit v6 on v5

--- a/solution.py
+++ b/solution.py
@@ -101,11 +101,22 @@
     mine = jnp.concatenate(
         [landed[:, : per * feat_width].reshape(piece_rows, feat_width), id_rows], axis=0
     )
-    pieces = [mine]
-    for t in range(1, share_count):
-        pieces.append(
-            lax.ppermute(mine, "mp", [(i, (i - t) % share_count) for i in range(share_count)])
-        )
+    if share_count == 4:
+        up = [(i, (i + 1) % 4) for i in range(4)]
+        down = [(i, (i - 1) % 4) for i in range(4)]
+        from_below = lax.ppermute(mine, "mp", up)
+        from_above = lax.ppermute(mine, "mp", down)
+        cut = piece_rows // 2
+        far_low = lax.ppermute(from_above[:cut], "mp", down)
+        far_high = lax.ppermute(from_below[cut:], "mp", up)
+        far = jnp.concatenate([far_low, far_high], axis=0)
+        pieces = [mine, from_below, from_above, far]
+    else:
+        pieces = [mine]
+        for t in range(1, share_count):
+            pieces.append(
+                lax.ppermute(mine, "mp", [(i, (i - t) % share_count) for i in range(share_count)])
+            )
 
     recv_rows = state_slots.shape[0] * state_slots.shape[1]
     neigh_count = one_hot(neighbours[:, 0], recv_rows, F32)

time: 159 us -> 145 us (0.912)
  waiting for transfers between devices: 77 us -> 64.7 us
  local copies, waits for them, and re-layouts: 7.31 us -> 5.1 us
    ppermute x3 -> x4, waiting for transfers between devices: 17.4 us -> 8.99 us  [the longest x1 8.98 us: per_device(): from_below = lax.ppermute(mine, 'mp', up)]
    all_to_all x1, starting transfers between devices: 5.76 us -> 9.55 us  [per_device(): lax.all_to_all(outgoing, 'nodes', split_axis=0, concat_axis=0, tiled=True)]
    ppermute x3, waiting for transfers between devices: 8.84 us -> 5.78 us  [mp_all_gather(): rel.append(lax.ppermute(piece, axis, [(i, (i - t) % n) for i in range(n)]))]
    slice x3 -> x2, local copies, waits for them, and re-layouts: 2.99 us -> 0.07 us  [per_device(): lhs = jnp.concatenate([p[:piece_rows], seg_t, seg_t], axis=1)]
    ppermute x3, starting transfers between devices: 3.49 us -> 1.89 us  [mp_all_gather(): rel.append(lax.ppermute(piece, axis, [(i, (i - t) % n) for i in range(n)]))]
    ppermute x3 -> x4, starting transfers between devices: 5.51 us -> 5.42 us  [the longest x1 2.66 us: per_device(): far_low = lax.ppermute(from_above[:cut], 'mp', down)]
  transfers between devices with their start and end apart: 14 -> 15, of which waited for: 12 -> 9; matrix products, arithmetic and copies ran while one was open for 9% -> 15% of each run, Pallas kernels for 0% -> 0%
where the time goes in v6:
time: 145 us; the launch traced here: 144 us
  waiting for transfers between devices  64.7 us (45%)
  starting transfers between devices  35.6 us (25%)
  matrix products  26.7 us (18%)
  other arithmetic  11.1 us (8%)
  local copies, waits for them, and re-layouts  5.1 us (4%)
    all_to_all x1, waiting for transfers between devices, per_device(): lax.all_to_all(outgoing, 'nodes', split_axis=0, concat_axis=0, tiled=True)  24.3 us
    all_to_all x1, waiting for transfers between devices, per_device(): lax.all_to_all(payload, 'nodes', split_axis=0, concat_axis=0, tiled=True)  14.1 us
    all_to_all x1, starting transfers between devices, per_device(): lax.all_to_all(payload, 'nodes', split_axis=0, concat_axis=0, tiled=True)  13.3 us
    dot_general x4, matrix products, per_device(): part = jnp.dot(seg, hidden_msg, preferred_element_type=F32)  12 us
    ppermute x6, waiting for transfers between devices, mp_reduce_scatter(): got = lax.ppermute(ahead[t], axis, [(i, (i + t) % n) for i in range(n)])  11.6 us
    all_to_all x1, starting transfers between devices, per_device(): lax.all_to_all(outgoing, 'nodes', split_axis=0, concat_axis=0, tiled=True)  9.55 us
    ppermute x1, waiting for transfers between devices, per_device(): from_below = lax.ppermute(mine, 'mp', up)  8.98 us
    ppermute x3, waiting for transfers between devices, mp_all_gather(): rel.append(lax.ppermute(piece, axis, [(i, (i - t) % n) for i in range(n)]))  5.78 us
  transfers between devices with their start and end apart: 15, of which 9 were waited for; matrix products, arithmetic and copies ran while one was open for 15% of the time, Pallas kernels for 0%

profile of v6, /device:TPU:1, one launch (start us, length us, event | category | flops | bytes accessed | tf_op | source)
XLA Modules:
  0.0 144.4 jit_solution(12625702290841805883)
XLA Ops:
  0.7 1.4 %fusion.25 = f32[1024]{0:T(1024)S(1)} fusion(s32[1024]{0:T(1024)} %bitcast.110), kind=kOutput, calls=%fused_computation.50 | convolution fusion | flops 135527424 | bytes 8192 | tf_op jit(solution)/shard_map/dot_general | solution.py:82
  6.7 13.3 %all-to-all-start = ((bf16[64,2,2112]{2,1,0:T(2,128)(2,1)}), bf16[64,2,2112]{2,1,0:T(2,128)(2,1)S(1)}, u32[]{:S(2)}, u32[]{:S(2)}) async-start(bf16[64,2,2112]{2,1,0:T(2,128)(2,1)} %reshape.148), calls=%async_computation | async-start | bytes 1114112 | tf_op jit(solution)/shard_map/all_to_all | solution.py:97
  20.2 2.6 %fusion.152 = (bf16[256,512]{1,0:T(8,128)(2,1)}, bf16[256,512]{1,0:T(8,128)(2,1)}) fusion(bf16[256,1024]{1,0:T(8,128)(2,1)} %param.22, bf16[1024,512]{1,0:T(8,128)(2,1)} %param.24), kind=kOutput, calls=%fused_computation.211 | convolution fusion | flops 268959744 | bytes 2097152 | tf_op jit(solution)/shard_map/dot_general | solution.py:126
  22.8 1.5 %fusion.14 = f32[3,256,256]{2,1,0:T(8,128)} fusion(bf16[3,1024,256]{2,1,0:T(8,128)(2,1)S(1)} %copy-done, bf16[256,1024]{1,0:T(8,128)(2,1)S(1)} %copy-done.2, f32[3,256]{1,0:T(4,128)S(1)} %copy-done.14), kind=kOutput, calls=%fused_computation.36 | convolution fusion | flops 402849792 | bytes 2886656 | tf_op jit(solution)/shard_map/nd,gdc->gnc/dot_general | solution.py:155
  24.3 14.1 %all-to-all-done = bf16[64,2,2112]{2,1,0:T(2,128)(2,1)S(1)} async-done(((bf16[64,2,2112]{2,1,0:T(2,128)(2,1)}), bf16[64,2,2112]{2,1,0:T(2,128)(2,1)S(1)}, u32[]{:S(2)}, u32[]{:S(2)}) %all-to-all-start) | async-done | bytes 540704 | tf_op jit(solution)/shard_map/all_to_all | solution.py:97
  41.5 1.5 %collective-permute-start.1 = (bf16[528,512]{1,0:T(8,128)(2,1)}, bf16[528,512]{1,0:T(8,128)(2,1)S(1)}, u32[]{:S(2)}, u32[]{:S(2)}) collective-permute-start(bf16[528,512]{1,0:T(8,128)(2,1)} %fusion.77), channel_id=1, source_target_pairs={{0,3},{1,0},{2,1},{3,2},{4,7},{5,4},{6,5},{7,6},{8,11},{9,8},{10,9... | collective-permute-start | bytes 1622024 | tf_op jit(solution)/shard_map/ppermute | solution.py:108
  43.3 2.9 %fusion.19 = f32[256,512]{1,0:T(8,128)} fusion(bf16[512,256]{1,0:T(8,128)(2,1)S(1)} %fusion.99, bf16[512,512]{1,0:T(8,128)(2,1)S(1)} %reshape.125, f32[512]{0:T(512)S(1)} %copy-done.17, s32[512]{0:T(512)S(1)} %reshape.130, bf16[256,512]{1,0:T(8,128)(2,1)} %get-tuple-element.15, bf16[256,512]{1,0:T(8,128)(2,1)} %get-tuple-element.14, bf16[512,512]{1,0:T(8,128)(2,1)} %param.23), kind=kOutput, calls=%fused_computation.42 | convolution fusion | flops 678297600 | bytes 2363392 | tf_op jit(solution)/shard_map/dot_general | solution.py:140
  46.2 9.0 %collective-permute-done = bf16[528,512]{1,0:T(8,128)(2,1)S(1)} collective-permute-done((bf16[528,512]{1,0:T(8,128)(2,1)}, bf16[528,512]{1,0:T(8,128)(2,1)S(1)}, u32[]{:S(2)}, u32[]{:S(2)}) %collective-permute-start) | collective-permute-done | bytes 540704 | tf_op jit(solution)/shard_map/ppermute | solution.py:107
  57.9 2.7 %collective-permute-start.3 = (bf16[256,512]{1,0:T(8,128)(2,1)}, bf16[256,512]{1,0:T(8,128)(2,1)}, u32[]{:S(2)}, u32[]{:S(2)}) collective-permute-start(bf16[256,512]{1,0:T(8,128)(2,1)} %slice.151), channel_id=1, source_target_pairs={{0,3},{1,0},{2,1},{3,2},{4,7},{5,4},{6,5},{7,6},{8,11},{9,8},{10,9... | collective-permute-start | bytes 786440 | tf_op jit(solution)/shard_map/ppermute | solution.py:110
  60.6 3.1 %fusion.17 = f32[256,512]{1,0:T(8,128)} fusion(bf16[512,256]{1,0:T(8,128)(2,1)} %fusion.101, bf16[512,512]{1,0:T(8,128)(2,1)S(1)} %slice.150, f32[512]{0:T(512)S(1)} %copy-done.17, s32[512]{0:T(512)S(1)} %bitcast.102, bf16[256,512]{1,0:T(8,128)(2,1)} %get-tuple-element.15, bf16[256,512]{1,0:T(8,128)(2,1)} %get-tuple-element.14, bf16[512,512]{1,0:T(8,128)(2,1)} %param.23), kind=kOutput, calls=%fused_computation.40 | convolution fusion | flops 678297600 | bytes 2363392 | tf_op jit(solution)/shard_map/dot_general | solution.py:140
  63.7 3.4 %fusion.22 = f32[256,512]{1,0:T(8,128)} fusion(f32[256,512]{1,0:T(8,128)} %fusion.17, f32[256,512]{1,0:T(8,128)} %fusion.19, bf16[512,256]{1,0:T(8,128)(2,1)} %fusion.100, bf16[512,512]{1,0:T(8,128)(2,1)S(1)} %slice.149, f32[512]{0:T(512)S(1)} %copy-done.17, s32[512]{0:T(512)S(1)} %bitcast.106, bf16[256,512]{1,0:T(8,128)(2,1)} %get-tuple-element.15, ...), kind=kOutput, calls=%fused_computation.45 | convolution fusion | flops 678559744 | bytes 3411968 | tf_op jit(solution)/shard_map/dot_general | solution.py:140
  68.2 2.5 %fusion.21 = f32[256,512]{1,0:T(8,128)S(1)} fusion(f32[256,512]{1,0:T(8,128)} %fusion.22, bf16[272,512]{1,0:T(8,128)(2,1)} %collective-permute-done.2, bf16[256,512]{1,0:T(8,128)(2,1)} %collective-permute-done.3, bf16[512,256]{1,0:T(8,128)(2,1)S(1)} %fusion.102, f32[512]{0:T(512)S(1)} %copy-done.17, s32[512]{0:T(512)S(1)} %bitcast.109, ...), kind=kOutput, calls=%fused_computation.44 | convolution fusion | flops 679477248 | bytes 2904064 | tf_op jit(solution)/shard_map/dot_general | solution.py:140
  73.3 1.3 collective-permute-start.6
  74.6 5.9 %collective-permute-done.4 = bf16[64,1024]{1,0:T(8,128)(2,1)S(1)} collective-permute-done((bf16[64,1024]{1,0:T(8,128)(2,1)S(1)}, bf16[64,1024]{1,0:T(8,128)(2,1)S(1)}, u32[]{:S(2)}, u32[]{:S(2)}) %collective-permute-start.4) | collective-permute-done | bytes 131104 | tf_op jit(solution)/shard_map/ppermute | solution.py:31
  82.6 2.0 %collective-permute-done.7 = bf16[64,1024]{1,0:T(8,128)(2,1)S(1)} collective-permute-done((bf16[64,1024]{1,0:T(8,128)(2,1)S(1)}, bf16[64,1024]{1,0:T(8,128)(2,1)S(1)}, u32[]{:S(2)}, u32[]{:S(2)}) %collective-permute-start.7) | collective-permute-done | bytes 131104 | tf_op jit(solution)/shard_map/ppermute | solution.py:39
  84.6 2.7 %collective-permute-done.8 = bf16[64,1024]{1,0:T(8,128)(2,1)S(1)} collective-permute-done((bf16[64,1024]{1,0:T(8,128)(2,1)S(1)}, bf16[64,1024]{1,0:T(8,128)(2,1)S(1)}, u32[]{:S(2)}, u32[]{:S(2)}) %collective-permute-start.8) | collective-permute-done | bytes 131104 | tf_op jit(solution)/shard_map/ppermute | solution.py:39
  90.8 1.6 %convolution_convert_fusion = bf16[2048,256]{1,0:T(8,128)(2,1)} fusion(bf16[256,256]{1,0:T(8,128)(2,1)S(1)} %fusion.104, s32[2048]{0:T(1024)S(1)} %eq.404), kind=kOutput, calls=%fused_computation.2 | convolution fusion | flops 269484032 | bytes 1187840 | tf_op jit(solution)/shard_map/dot_general | solution.py:166
  92.4 9.6 %all-to-all-start.1 = ((bf16[64,32,256]{2,1,0:T(8,128)(2,1)}), bf16[64,32,256]{2,1,0:T(8,128)(2,1)S(1)}, u32[]{:S(2)}, u32[]{:S(2)}) async-start(bf16[64,32,256]{2,1,0:T(8,128)(2,1)} %bitcast.99), calls=%async_computation.1 | async-start | bytes 2097152 | tf_op jit(solution)/shard_map/all_to_all | solution.py:168
  102.0 3.8 %add_convert_fusion = bf16[256,2048]{1,0:T(8,128)(2,1)} fusion(s32[256]{0:T(256)S(1)} %bitcast.120, s32[256]{0:T(256)S(1)} %bitcast.121, s32[256]{0:T(256)S(1)} %bitcast.113, s32[256]{0:T(256)S(1)} %bitcast.114, s32[256]{0:T(256)S(1)} %bitcast.115, s32[256]{0:T(256)S(1)} %bitcast.116, s32[256]{0:T(256)S(1)} %bitcast.117, s32[256]{0:T(256)S(1)} %bitcast.118, ...), kind=kLoop, calls=%fused_computation.4 | loop fusion | flops 15728640 | bytes 1058816 | tf_op jit(solution)/shard_map/convert_element_type | solution.py:125
  105.8 24.3 %all-to-all-done.1 = bf16[64,32,256]{2,1,0:T(8,128)(2,1)S(1)} async-done(((bf16[64,32,256]{2,1,0:T(8,128)(2,1)}), bf16[64,32,256]{2,1,0:T(8,128)(2,1)S(1)}, u32[]{:S(2)}, u32[]{:S(2)}) %all-to-all-start.1) | async-done | bytes 1048608 | tf_op jit(solution)/shard_map/all_to_all | solution.py:168
  130.1 3.1 %fusion.26 = f32[256,1024]{1,0:T(8,128)} fusion(bf16[256,1024]{1,0:T(8,128)(2,1)S(1)} %copy-done.4, bf16[256,2048]{1,0:T(8,128)(2,1)} %add_convert_fusion, bf16[2048,256]{1,0:T(8,128)(2,1)S(1)} %bitcast.94), kind=kOutput, calls=%fused_computation.51 | convolution fusion | flops 402784256 | bytes 3670016 | tf_op jit(solution)/shard_map/dot_general | solution.py:177
  133.2 1.8 %fusion.13 = bf16[256,1024]{1,0:T(8,128)(2,1)S(1)} fusion(f32[256,1024]{1,0:T(8,128)} %fusion.26, bf16[256,1024]{1,0:T(8,128)(2,1)} %param.36, bf16[256,256]{1,0:T(8,128)(2,1)S(1)} %fusion.104, s32[256]{0:T(256)S(1)} %copy-done.11), kind=kOutput, calls=%fused_computation.34 | convolution fusion | flops 168427520 | bytes 2229248 | tf_op jit(solution)/shard_map/dot_general | solution.py:178
  135.4 1.8 %collective-permute-start.11 = (bf16[64,1024]{1,0:T(8,128)(2,1)S(1)}, bf16[64,1024]{1,0:T(8,128)(2,1)S(1)}, u32[]{:S(2)}, u32[]{:S(2)}) collective-permute-start(bf16[64,1024]{1,0:T(8,128)(2,1)S(1)} %get-tuple-element.9), channel_id=1, source_target_pairs={{0,2},{1,3},{2,0},{3,1},{4,6},{5,7},{6,4},{7,5},{8,10},{9,11},{10,... | collective-permute-start | bytes 393224 | tf_op jit(solution)/shard_map/ppermute | solution.py:31
  138.1 4.5 %collective-permute-done.10 = bf16[64,1024]{1,0:T(8,128)(2,1)S(1)} collective-permute-done((bf16[64,1024]{1,0:T(8,128)(2,1)S(1)}, bf16[64,1024]{1,0:T(8,128)(2,1)S(1)}, u32[]{:S(2)}, u32[]{:S(2)}) %collective-permute-start.10) | collective-permute-done | bytes 131104 | tf_op jit(solution)/shard_map/ppermute | solution.py:31
  (108 shorter events, 22.9 us)
Async XLA Ops:
  0.6 22.2 %copy-start = (bf16[3,1024,256]{2,1,0:T(8,128)(2,1)S(1)}, bf16[3,1024,256]{2,1,0:T(8,128)(2,1)}, u32[]{:S(2)}) copy-start(bf16[3,1024,256]{2,1,0:T(8,128)(2,1)} %param.29) | copy-start | bytes 4718596
  4.5 15.5 %copy-start.6 = (s32[64,32]{0,1:T(8,128)S(1)}, s32[64,32]{0,1:T(8,128)}, u32[]{:S(2)}) copy-start(s32[64,32]{0,1:T(8,128)} %param.32) | copy-start | bytes 24580
  6.7 16.1 %copy-start.2 = (bf16[256,1024]{1,0:T(8,128)(2,1)S(1)}, bf16[256,1024]{1,0:T(8,128)(2,1)}, u32[]{:S(2)}) copy-start(bf16[256,1024]{1,0:T(8,128)(2,1)} %param.22) | copy-start | bytes 1572868
  6.7 16.1 %copy-start.14 = (f32[3,256]{1,0:T(4,128)S(1)}, f32[3,256]{1,0:T(4,128)}, u32[]{:S(2)}) copy-start(f32[3,256]{1,0:T(4,128)} %param.31) | copy-start | bytes 9220
  6.7 31.6 %all-to-all-start = ((bf16[64,2,2112]{2,1,0:T(2,128)(2,1)}), bf16[64,2,2112]{2,1,0:T(2,128)(2,1)S(1)}, u32[]{:S(2)}, u32[]{:S(2)}) async-start(bf16[64,2,2112]{2,1,0:T(2,128)(2,1)} %reshape.148), calls=%async_computation | async-start | bytes 1114112 | tf_op jit(solution)/shard_map/all_to_all | solution.py:97
  40.3 14.8 %collective-permute-start = (bf16[528,512]{1,0:T(8,128)(2,1)}, bf16[528,512]{1,0:T(8,128)(2,1)S(1)}, u32[]{:S(2)}, u32[]{:S(2)}) collective-permute-start(bf16[528,512]{1,0:T(8,128)(2,1)} %fusion.77), channel_id=1, source_target_pairs={{0,1},{1,2},{2,3},{3,0},{4,5},{5,6},{6,7},{7,4},{8,9},{9,10},{10,1... | collective-permute-start | bytes 1622024 | tf_op jit(solution)/shard_map/ppermute | solution.py:107
  41.5 14.8 %collective-permute-start.1 = (bf16[528,512]{1,0:T(8,128)(2,1)}, bf16[528,512]{1,0:T(8,128)(2,1)S(1)}, u32[]{:S(2)}, u32[]{:S(2)}) collective-permute-start(bf16[528,512]{1,0:T(8,128)(2,1)} %fusion.77), channel_id=1, source_target_pairs={{0,3},{1,0},{2,1},{3,2},{4,7},{5,4},{6,5},{7,6},{8,11},{9,8},{10,9... | collective-permute-start | bytes 1622024 | tf_op jit(solution)/shard_map/ppermute | solution.py:108
  55.2 11.9 %collective-permute-start.2 = (bf16[272,512]{1,0:T(8,128)(2,1)S(1)}, bf16[272,512]{1,0:T(8,128)(2,1)}, u32[]{:S(2)}, u32[]{:S(2)}) collective-permute-start(bf16[272,512]{1,0:T(8,128)(2,1)S(1)} %slice.147), channel_id=1, source_target_pairs={{0,1},{1,2},{2,3},{3,0},{4,5},{5,6},{6,7},{7,4},{8,9},{9,10},{10,1... | collective-permute-start | bytes 835592 | tf_op jit(solution)/shard_map/ppermute | solution.py:111
  57.9 10.3 %collective-permute-start.3 = (bf16[256,512]{1,0:T(8,128)(2,1)}, bf16[256,512]{1,0:T(8,128)(2,1)}, u32[]{:S(2)}, u32[]{:S(2)}) collective-permute-start(bf16[256,512]{1,0:T(8,128)(2,1)} %slice.151), channel_id=1, source_target_pairs={{0,3},{1,0},{2,1},{3,2},{4,7},{5,4},{6,5},{7,6},{8,11},{9,8},{10,9... | collective-permute-start | bytes 786440 | tf_op jit(solution)/shard_map/ppermute | solution.py:110
  71.9 8.7 %collective-permute-start.4 = (bf16[64,1024]{1,0:T(8,128)(2,1)S(1)}, bf16[64,1024]{1,0:T(8,128)(2,1)S(1)}, u32[]{:S(2)}, u32[]{:S(2)}) collective-permute-start(bf16[64,1024]{1,0:T(8,128)(2,1)S(1)} %get-tuple-element.11), channel_id=1, source_target_pairs={{0,1},{1,2},{2,3},{3,0},{4,5},{5,6},{6,7},{7,4},{8,9},{9,10},{10,1... | collective-permute-start | bytes 393224 | tf_op jit(solution)/shard_map/ppermute | solution.py:31
  71.9 8.6 %collective-permute-start.5 = (bf16[64,1024]{1,0:T(8,128)(2,1)S(1)}, bf16[64,1024]{1,0:T(8,128)(2,1)S(1)}, u32[]{:S(2)}, u32[]{:S(2)}) collective-permute-start(bf16[64,1024]{1,0:T(8,128)(2,1)S(1)} %get-tuple-element.12), channel_id=1, source_target_pairs={{0,2},{1,3},{2,0},{3,1},{4,6},{5,7},{6,4},{7,5},{8,10},{9,11},{10,... | collective-permute-start | bytes 393224 | tf_op jit(solution)/shard_map/ppermute | solution.py:31
  73.3 7.3 %collective-permute-start.6 = (bf16[64,1024]{1,0:T(8,128)(2,1)S(1)}, bf16[64,1024]{1,0:T(8,128)(2,1)S(1)}, u32[]{:S(2)}, u32[]{:S(2)}) collective-permute-start(bf16[64,1024]{1,0:T(8,128)(2,1)S(1)} %get-tuple-element.13), channel_id=1, source_target_pairs={{0,3},{1,0},{2,1},{3,2},{4,7},{5,4},{6,5},{7,6},{8,11},{9,8},{10,9... | collective-permute-start | bytes 393224 | tf_op jit(solution)/shard_map/ppermute | solution.py:31
  80.6 7.9 %copy-start.12 = (bf16[3,1024,256]{2,1,0:T(8,128)(2,1)S(1)}, bf16[3,1024,256]{2,1,0:T(8,128)(2,1)}, u32[]{:S(2)}) copy-start(bf16[3,1024,256]{2,1,0:T(8,128)(2,1)} %param.28) | copy-start | bytes 4718596
  80.7 3.9 %collective-permute-start.7 = (bf16[64,1024]{1,0:T(8,128)(2,1)S(1)}, bf16[64,1024]{1,0:T(8,128)(2,1)S(1)}, u32[]{:S(2)}, u32[]{:S(2)}) collective-permute-start(bf16[64,1024]{1,0:T(8,128)(2,1)S(1)} %get-tuple-element.5), channel_id=1, source_target_pairs={{0,3},{1,0},{2,1},{3,2},{4,7},{5,4},{6,5},{7,6},{8,11},{9,8},{10,9... | collective-permute-start | bytes 393224 | tf_op jit(solution)/shard_map/ppermute | solution.py:39
  81.9 5.4 %collective-permute-start.8 = (bf16[64,1024]{1,0:T(8,128)(2,1)S(1)}, bf16[64,1024]{1,0:T(8,128)(2,1)S(1)}, u32[]{:S(2)}, u32[]{:S(2)}) collective-permute-start(bf16[64,1024]{1,0:T(8,128)(2,1)S(1)} %get-tuple-element.5), channel_id=1, source_target_pairs={{0,2},{1,3},{2,0},{3,1},{4,6},{5,7},{6,4},{7,5},{8,10},{9,11},{10,... | collective-permute-start | bytes 393224 | tf_op jit(solution)/shard_map/ppermute | solution.py:39
  81.9 6.5 %collective-permute-start.9 = (bf16[64,1024]{1,0:T(8,128)(2,1)S(1)}, bf16[64,1024]{1,0:T(8,128)(2,1)S(1)}, u32[]{:S(2)}, u32[]{:S(2)}) collective-permute-start(bf16[64,1024]{1,0:T(8,128)(2,1)S(1)} %get-tuple-element.5), channel_id=1, source_target_pairs={{0,1},{1,2},{2,3},{3,0},{4,5},{5,6},{6,7},{7,4},{8,9},{9,10},{10,1... | collective-permute-start | bytes 393224 | tf_op jit(solution)/shard_map/ppermute | solution.py:39
  90.8 42.4 %copy-start.5 = (bf16[256,256]{1,0:T(8,128)(2,1)}, bf16[256,256]{1,0:T(8,128)(2,1)S(1)}, u32[]{:S(2)}) copy-start(bf16[256,256]{1,0:T(8,128)(2,1)S(1)} %fusion.104) | copy-start | bytes 393220
  90.8 11.1 %copy-start.7 = (s32[256,10]{0,1:T(8,128)S(1)}, s32[256,10]{0,1:T(8,128)}, u32[]{:S(2)}) copy-start(s32[256,10]{0,1:T(8,128)} %param.33) | copy-start | bytes 30724
  92.4 37.7 %copy-start.4 = (bf16[256,1024]{1,0:T(8,128)(2,1)S(1)}, bf16[256,1024]{1,0:T(8,128)(2,1)}, u32[]{:S(2)}) copy-start(bf16[256,1024]{1,0:T(8,128)(2,1)} %param.35) | copy-start | bytes 1572868
  92.4 37.7 %all-to-all-start.1 = ((bf16[64,32,256]{2,1,0:T(8,128)(2,1)}), bf16[64,32,256]{2,1,0:T(8,128)(2,1)S(1)}, u32[]{:S(2)}, u32[]{:S(2)}) async-start(bf16[64,32,256]{2,1,0:T(8,128)(2,1)} %bitcast.99), calls=%async_computation.1 | async-start | bytes 2097152 | tf_op jit(solution)/shard_map/all_to_all | solution.py:168
  133.2 10.5 %copy-start.8 = (f32[1024]{0:T(1024)S(1)}, f32[1024]{0:T(1024)}, u32[]{:S(2)}) copy-start(f32[1024]{0:T(1024)} %param.37) | copy-start | bytes 12292
  135.3 7.2 %collective-permute-start.10 = (bf16[64,1024]{1,0:T(8,128)(2,1)S(1)}, bf16[64,1024]{1,0:T(8,128)(2,1)S(1)}, u32[]{:S(2)}, u32[]{:S(2)}) collective-permute-start(bf16[64,1024]{1,0:T(8,128)(2,1)S(1)} %get-tuple-element.8), channel_id=1, source_target_pairs={{0,1},{1,2},{2,3},{3,0},{4,5},{5,6},{6,7},{7,4},{8,9},{9,10},{10,1... | collective-permute-start | bytes 393224 | tf_op jit(solution)/shard_map/ppermute | solution.py:31
  135.4 7.2 %collective-permute-start.11 = (bf16[64,1024]{1,0:T(8,128)(2,1)S(1)}, bf16[64,1024]{1,0:T(8,128)(2,1)S(1)}, u32[]{:S(2)}, u32[]{:S(2)}) collective-permute-start(bf16[64,1024]{1,0:T(8,128)(2,1)S(1)} %get-tuple-element.9), channel_id=1, source_target_pairs={{0,2},{1,3},{2,0},{3,1},{4,6},{5,7},{6,4},{7,5},{8,10},{9,11},{10,... | collective-permute-start | bytes 393224 | tf_op jit(solution)/shard_map/ppermute | solution.py:31
  137.2 6.5 %collective-permute-start.12 = (bf16[64,1024]{1,0:T(8,128)(2,1)S(1)}, bf16[64,1024]{1,0:T(8,128)(2,1)S(1)}, u32[]{:S(2)}, u32[]{:S(2)}) collective-permute-start(bf16[64,1024]{1,0:T(8,128)(2,1)S(1)} %get-tuple-element.10), channel_id=1, source_target_pairs={{0,3},{1,0},{2,1},{3,2},{4,7},{5,4},{6,5},{7,6},{8,11},{9,8},{10,9... | collective-permute-start | bytes 393224 | tf_op jit(solution)/shard_map/ppermute | solution.py:31
  (9 other events, 30.7 us)

commit v7 on v6

--- a/solution.py
+++ b/solution.py
@@ -37,6 +37,45 @@
     rel = [piece]
     for t in range(1, n):
         rel.append(lax.ppermute(piece, axis, [(i, (i - t) % n) for i in range(n)]))
+    rel = jnp.stack(rel + rel, axis=0)
+    full = lax.dynamic_slice_in_dim(rel, (n - me) % n, n, 0)
+    return full.reshape(n * piece.shape[0], piece.shape[1])
+
+
+def ring_moves(n):
+    return [(i, (i + 1) % n) for i in range(n)], [(i, (i - 1) % n) for i in range(n)]
+
+
+def mp_reduce_scatter4(x, axis, me):
+    n = 4
+    rows = x.shape[0] // n
+    half = rows // 2
+    chunks = x.reshape(n, rows, x.shape[1])
+    ahead = lax.dynamic_slice_in_dim(jnp.concatenate([chunks, chunks], axis=0), me, n, 0)
+    up, down = ring_moves(n)
+    up_a = lax.ppermute(jnp.concatenate([ahead[1], ahead[2][:half]], axis=0), axis, up)
+    down_a = lax.ppermute(jnp.concatenate([ahead[3], ahead[2][half:]], axis=0), axis, down)
+    up_b = lax.ppermute(up_a[rows:], axis, up)
+    down_b = lax.ppermute(down_a[rows:], axis, down)
+    far = jnp.concatenate([up_b, down_b], axis=0)
+    return (
+        ahead[0].astype(F32)
+        + up_a[:rows].astype(F32)
+        + down_a[:rows].astype(F32)
+        + far.astype(F32)
+    )
+
+
+def mp_all_gather4(piece, axis, me):
+    n = 4
+    half = piece.shape[0] // 2
+    up, down = ring_moves(n)
+    below = lax.ppermute(piece, axis, up)
+    above = lax.ppermute(piece, axis, down)
+    far = jnp.concatenate(
+        [lax.ppermute(above[:half], axis, down), lax.ppermute(below[half:], axis, up)], axis=0
+    )
+    rel = [piece, above, far, below]
     rel = jnp.stack(rel + rel, axis=0)
     full = lax.dynamic_slice_in_dim(rel, (n - me) % n, n, 0)
     return full.reshape(n * piece.shape[0], piece.shape[1])
@@ -144,8 +183,12 @@
     partial_total = split_dot(hidden_sum, w_msg_out)
 
     divisor = jnp.maximum(counts, 1.0)[:, None]
-    reduced = mp_reduce_scatter(partial_total.astype(BF16), "mp", share_count, mp_index)
-    msg_total = mp_all_gather(reduced.astype(BF16), "mp", share_count, mp_index).astype(F32)
+    if share_count == 4:
+        reduced = mp_reduce_scatter4(partial_total.astype(BF16), "mp", mp_index)
+        msg_total = mp_all_gather4(reduced.astype(BF16), "mp", mp_index).astype(F32)
+    else:
+        reduced = mp_reduce_scatter(partial_total.astype(BF16), "mp", share_count, mp_index)
+        msg_total = mp_all_gather(reduced.astype(BF16), "mp", share_count, mp_index).astype(F32)
     aggregate = (msg_total / divisor + b_out).astype(BF16)
     gates_in = (
         jnp.einsum("nd,gdc->gnc", aggregate, w_input, preferred_element_type=F32)
@@ -172,15 +215,14 @@
     self_state = jnp.dot(
         one_hot(query_slots, mem_rows), new_memory, preferred_element_type=F32
     ).astype(BF16)
-    summed = mp_reduce_scatter(
-        (
-            jnp.dot(neigh_mean, w_neigh, preferred_element_type=F32)
-            + jnp.dot(self_state, w_self, preferred_element_type=F32)
-        ).astype(BF16),
-        "mp",
-        share_count,
-        mp_index,
-    )
+    embed_partial = (
+        jnp.dot(neigh_mean, w_neigh, preferred_element_type=F32)
+        + jnp.dot(self_state, w_self, preferred_element_type=F32)
+    ).astype(BF16)
+    if share_count == 4:
+        summed = mp_reduce_scatter4(embed_partial, "mp", mp_index)
+    else:
+        summed = mp_reduce_scatter(embed_partial, "mp", share_count, mp_index)
     embedding = jax.nn.relu(summed + b_embed).astype(BF16)
     return (new_memory, embedding)
 

time: 145 us -> 159 us (1.097); the launches traced: 144 us -> 157 us
  starting transfers between devices: 35.6 us -> 47.9 us
    ppermute x9 -> x12, starting transfers between devices: 7.38 us -> 17.3 us  [the longest x2 5.85 us: mp_reduce_scatter4(): lax.ppermute(jnp.concatenate([ahead[3], ahead[2][half:]], axis=0), axis,...]
    all_to_all x1, starting transfers between devices: 9.55 us -> 11.9 us  [per_device(): lax.all_to_all(outgoing, 'nodes', split_axis=0, concat_axis=0, tiled=True)]
    ppermute x9 -> x12, waiting for transfers between devices: 17.4 us -> 17.1 us  [the longest x2 6.6 us: mp_reduce_scatter4(): lax.ppermute(jnp.concatenate([ahead[1], ahead[2][:half]], axis=0), axis, up)]
  transfers between devices with their start and end apart: 15 -> 18, of which waited for: 9 -> 9; matrix products, arithmetic and copies ran while one was open for 15% -> 14% of each run, Pallas kernels for 0% -> 0%
where the time goes in v7:
time: 159 us; the launch traced here: 157 us
  waiting for transfers between devices  64.4 us (41%)
  starting transfers between devices  47.9 us (30%)
  matrix products  26.7 us (17%)
  other arithmetic  11.2 us (7%)
  local copies, waits for them, and re-layouts  5.11 us (3%)
    all_to_all x1, waiting for transfers between devices, per_device(): lax.all_to_all(outgoing, 'nodes', split_axis=0, concat_axis=0, tiled=True)  24.3 us
    all_to_all x1, waiting for transfers between devices, per_device(): lax.all_to_all(payload, 'nodes', split_axis=0, concat_axis=0, tiled=True)  14 us
    all_to_all x1, starting transfers between devices, per_device(): lax.all_to_all(payload, 'nodes', split_axis=0, concat_axis=0, tiled=True)  13.3 us
    dot_general x4, matrix products, per_device(): part = jnp.dot(seg, hidden_msg, preferred_element_type=F32)  11.9 us
    all_to_all x1, starting transfers between devices, per_device(): lax.all_to_all(outgoing, 'nodes', split_axis=0, concat_axis=0, tiled=True)  11.9 us
    ppermute x1, waiting for transfers between devices, per_device(): from_below = lax.ppermute(mine, 'mp', up)  8.96 us
    ppermute x2, waiting for transfers between devices, mp_reduce_scatter4(): lax.ppermute(jnp.concatenate([ahead[1], ahead[2][:half]], axis=0), axis, up)  6.6 us
    ppermute x2, starting transfers between devices, mp_reduce_scatter4(): lax.ppermute(jnp.concatenate([ahead[3], ahead[2][half:]], axis=0), axis,...  5.85 us
  transfers between devices with their start and end apart: 18, of which 9 were waited for; matrix products, arithmetic and copies ran while one was open for 14% of the time, Pallas kernels for 0%

profile of v7, /device:TPU:1, one launch (start us, length us, event | category | flops | bytes accessed | tf_op | source)
XLA Modules:
  0.0 156.6 jit_solution(3379651545274200858)
XLA Ops:
  6.7 13.3 %all-to-all-start = ((bf16[64,2,2112]{2,1,0:T(2,128)(2,1)}), bf16[64,2,2112]{2,1,0:T(2,128)(2,1)S(1)}, u32[]{:S(2)}, u32[]{:S(2)}) async-start(bf16[64,2,2112]{2,1,0:T(2,128)(2,1)} %reshape.152), calls=%async_computation | async-start | bytes 1114112 | tf_op jit(solution)/shard_map/all_to_all | solution.py:136
  20.2 2.6 %fusion.154 = (bf16[256,512]{1,0:T(8,128)(2,1)}, bf16[256,512]{1,0:T(8,128)(2,1)}) fusion(bf16[256,1024]{1,0:T(8,128)(2,1)} %param.22, bf16[1024,512]{1,0:T(8,128)(2,1)} %param.24), kind=kOutput, calls=%fused_computation.218 | convolution fusion | flops 268959744 | bytes 2097152 | tf_op jit(solution)/shard_map/dot_general | solution.py:165
  24.3 14.0 %all-to-all-done = bf16[64,2,2112]{2,1,0:T(2,128)(2,1)S(1)} async-done(((bf16[64,2,2112]{2,1,0:T(2,128)(2,1)}), bf16[64,2,2112]{2,1,0:T(2,128)(2,1)S(1)}, u32[]{:S(2)}, u32[]{:S(2)}) %all-to-all-start) | async-done | bytes 540704 | tf_op jit(solution)/shard_map/all_to_all | solution.py:136
  43.2 2.9 %fusion.19 = f32[256,512]{1,0:T(8,128)} fusion(bf16[512,256]{1,0:T(8,128)(2,1)S(1)} %fusion.99, bf16[512,512]{1,0:T(8,128)(2,1)S(1)} %reshape.129, f32[512]{0:T(512)S(1)} %copy-done.17, s32[512]{0:T(512)S(1)} %reshape.134, bf16[256,512]{1,0:T(8,128)(2,1)} %get-tuple-element.17, bf16[256,512]{1,0:T(8,128)(2,1)} %get-tuple-element.16, bf16[512,512]{1,0:T(8,128)(2,1)} %param.23), kind=kOutput, calls=%fused_computation.42 | convolution fusion | flops 678297600 | bytes 2363392 | tf_op jit(solution)/shard_map/dot_general | solution.py:179
  46.2 9.0 %collective-permute-done = bf16[528,512]{1,0:T(8,128)(2,1)S(1)} collective-permute-done((bf16[528,512]{1,0:T(8,128)(2,1)}, bf16[528,512]{1,0:T(8,128)(2,1)S(1)}, u32[]{:S(2)}, u32[]{:S(2)}) %collective-permute-start) | collective-permute-done | bytes 540704 | tf_op jit(solution)/shard_map/ppermute | solution.py:146
  57.7 2.7 %collective-permute-start.3 = (bf16[256,512]{1,0:T(8,128)(2,1)}, bf16[256,512]{1,0:T(8,128)(2,1)}, u32[]{:S(2)}, u32[]{:S(2)}) collective-permute-start(bf16[256,512]{1,0:T(8,128)(2,1)} %slice.223), channel_id=1, source_target_pairs={{0,3},{1,0},{2,1},{3,2},{4,7},{5,4},{6,5},{7,6},{8,11},{9,8},{10,9... | collective-permute-start | bytes 786440 | tf_op jit(solution)/shard_map/ppermute | solution.py:149
  60.4 3.1 %fusion.17 = f32[256,512]{1,0:T(8,128)} fusion(bf16[512,256]{1,0:T(8,128)(2,1)} %fusion.101, bf16[512,512]{1,0:T(8,128)(2,1)S(1)} %slice.222, f32[512]{0:T(512)S(1)} %copy-done.17, s32[512]{0:T(512)S(1)} %bitcast.109, bf16[256,512]{1,0:T(8,128)(2,1)} %get-tuple-element.17, bf16[256,512]{1,0:T(8,128)(2,1)} %get-tuple-element.16, bf16[512,512]{1,0:T(8,128)(2,1)} %param.23), kind=kOutput, calls=%fused_computation.40 | convolution fusion | flops 678297600 | bytes 2363392 | tf_op jit(solution)/shard_map/dot_general | solution.py:179
  63.5 3.4 %fusion.22 = f32[256,512]{1,0:T(8,128)} fusion(f32[256,512]{1,0:T(8,128)} %fusion.17, f32[256,512]{1,0:T(8,128)} %fusion.19, bf16[512,256]{1,0:T(8,128)(2,1)} %fusion.100, bf16[512,512]{1,0:T(8,128)(2,1)S(1)} %slice.221, f32[512]{0:T(512)S(1)} %copy-done.17, s32[512]{0:T(512)S(1)} %bitcast.112, bf16[256,512]{1,0:T(8,128)(2,1)} %get-tuple-element.17, ...), kind=kOutput, calls=%fused_computation.45 | convolution fusion | flops 678559744 | bytes 3411968 | tf_op jit(solution)/shard_map/dot_general | solution.py:179
  67.8 2.5 %fusion.21 = f32[256,512]{1,0:T(8,128)S(1)} fusion(f32[256,512]{1,0:T(8,128)} %fusion.22, bf16[272,512]{1,0:T(8,128)(2,1)} %collective-permute-done.2, bf16[256,512]{1,0:T(8,128)(2,1)} %collective-permute-done.3, bf16[512,256]{1,0:T(8,128)(2,1)S(1)} %fusion.102, f32[512]{0:T(512)S(1)} %copy-done.17, s32[512]{0:T(512)S(1)} %bitcast.115, ...), kind=kOutput, calls=%fused_computation.44 | convolution fusion | flops 679477248 | bytes 2904064 | tf_op jit(solution)/shard_map/dot_general | solution.py:179
  71.8 2.7 %collective-permute-start.5 = (bf16[96,1024]{1,0:T(8,128)(2,1)S(1)}, bf16[96,1024]{1,0:T(8,128)(2,1)S(1)}, u32[]{:S(2)}, u32[]{:S(2)}) collective-permute-start(bf16[96,1024]{1,0:T(8,128)(2,1)S(1)} %pad_maximum_fusion.3), channel_id=1, source_target_pairs={{0,3},{1,0},{2,1},{3,2},{4,7},{5,4},{6,5},{7,6},{8,11},{9,8},{10,9... | collective-permute-start | bytes 589832 | tf_op jit(solution)/shard_map/ppermute | solution.py:57
  74.9 2.6 %collective-permute-done.4 = bf16[96,1024]{1,0:T(8,128)(2,1)S(1)} collective-permute-done((bf16[96,1024]{1,0:T(8,128)(2,1)S(1)}, bf16[96,1024]{1,0:T(8,128)(2,1)S(1)}, u32[]{:S(2)}, u32[]{:S(2)}) %collective-permute-start.4) | collective-permute-done | bytes 196640 | tf_op jit(solution)/shard_map/ppermute | solution.py:56
  77.5 2.7 %collective-permute-start.7 = (bf16[32,1024]{1,0:T(8,128)(2,1)S(1)}, bf16[32,1024]{1,0:T(8,128)(2,1)S(1)}, u32[]{:S(2)}, u32[]{:S(2)}) collective-permute-start(bf16[32,1024]{1,0:T(8,128)(2,1)S(1)} %slice.232), channel_id=1, source_target_pairs={{0,3},{1,0},{2,1},{3,2},{4,7},{5,4},{6,5},{7,6},{8,11},{9,8},{10,9... | collective-permute-start | bytes 196616 | tf_op jit(solution)/shard_map/ppermute | solution.py:59
  81.9 2.9 %collective-permute-start.8 = (bf16[64,1024]{1,0:T(8,128)(2,1)S(1)}, bf16[64,1024]{1,0:T(8,128)(2,1)S(1)}, u32[]{:S(2)}, u32[]{:S(2)}) collective-permute-start(bf16[64,1024]{1,0:T(8,128)(2,1)S(1)} %get-tuple-element.5), channel_id=1, source_target_pairs={{0,3},{1,0},{2,1},{3,2},{4,7},{5,4},{6,5},{7,6},{8,11},{9,8},{10,9... | collective-permute-start | bytes 393224 | tf_op jit(solution)/shard_map/ppermute | solution.py:74
  84.8 5.0 %collective-permute-done.10 = bf16[64,1024]{1,0:T(8,128)(2,1)S(1)} collective-permute-done((bf16[64,1024]{1,0:T(8,128)(2,1)S(1)}, bf16[64,1024]{1,0:T(8,128)(2,1)S(1)}, u32[]{:S(2)}, u32[]{:S(2)}) %collective-permute-start.10) | collective-permute-done | bytes 131104 | tf_op jit(solution)/shard_map/ppermute | solution.py:73
  89.8 2.7 %collective-permute-start.9 = (bf16[32,1024]{1,0:T(8,128)(2,1)S(1)}, bf16[32,1024]{1,0:T(8,128)(2,1)S(1)}, u32[]{:S(2)}, u32[]{:S(2)}) collective-permute-start(bf16[32,1024]{1,0:T(8,128)(2,1)S(1)} %slice.233), channel_id=1, source_target_pairs={{0,3},{1,0},{2,1},{3,2},{4,7},{5,4},{6,5},{7,6},{8,11},{9,8},{10,9... | collective-permute-start | bytes 196616 | tf_op jit(solution)/shard_map/ppermute | solution.py:76
  92.5 2.4 %collective-permute-done.11 = bf16[32,1024]{1,0:T(8,128)(2,1)S(1)} collective-permute-done((bf16[32,1024]{1,0:T(8,128)(2,1)S(1)}, bf16[32,1024]{1,0:T(8,128)(2,1)S(1)}, u32[]{:S(2)}, u32[]{:S(2)}) %collective-permute-start.11) | collective-permute-done | bytes 65568 | tf_op jit(solution)/shard_map/ppermute | solution.py:76
  98.9 11.9 %all-to-all-start.1 = ((bf16[64,32,256]{2,1,0:T(8,128)(2,1)}), bf16[64,32,256]{2,1,0:T(8,128)(2,1)S(1)}, u32[]{:S(2)}, u32[]{:S(2)}) async-start(bf16[64,32,256]{2,1,0:T(8,128)(2,1)} %bitcast.106), calls=%async_computation.1 | async-start | bytes 2097152 | tf_op jit(solution)/shard_map/all_to_all | solution.py:211
  110.9 3.8 %add_convert_fusion = bf16[256,2048]{1,0:T(8,128)(2,1)} fusion(s32[256]{0:T(256)S(1)} %bitcast.127, s32[256]{0:T(256)S(1)} %bitcast.128, s32[256]{0:T(256)S(1)} %bitcast.120, s32[256]{0:T(256)S(1)} %bitcast.121, s32[256]{0:T(256)S(1)} %bitcast.122, s32[256]{0:T(256)S(1)} %bitcast.123, s32[256]{0:T(256)S(1)} %bitcast.124, s32[256]{0:T(256)S(1)} %bitcast.125, ...), kind=kLoop, calls=%fused_computation.4 | loop fusion | flops 15728640 | bytes 1058816 | tf_op jit(solution)/shard_map/convert_element_type | solution.py:164
  114.7 24.3 %all-to-all-done.1 = bf16[64,32,256]{2,1,0:T(8,128)(2,1)S(1)} async-done(((bf16[64,32,256]{2,1,0:T(8,128)(2,1)}), bf16[64,32,256]{2,1,0:T(8,128)(2,1)S(1)}, u32[]{:S(2)}, u32[]{:S(2)}) %all-to-all-start.1) | async-done | bytes 1048608 | tf_op jit(solution)/shard_map/all_to_all | solution.py:211
  139.0 3.1 %fusion.26 = f32[256,1024]{1,0:T(8,128)} fusion(bf16[256,1024]{1,0:T(8,128)(2,1)S(1)} %copy-done.4, bf16[256,2048]{1,0:T(8,128)(2,1)} %add_convert_fusion, bf16[2048,256]{1,0:T(8,128)(2,1)S(1)} %bitcast.101), kind=kOutput, calls=%fused_computation.51 | convolution fusion | flops 402784256 | bytes 3670016 | tf_op jit(solution)/shard_map/dot_general | solution.py:219
  142.1 1.8 %fusion.13 = bf16[256,1024]{1,0:T(8,128)(2,1)S(1)} fusion(f32[256,1024]{1,0:T(8,128)} %fusion.26, bf16[256,1024]{1,0:T(8,128)(2,1)} %param.36, bf16[256,256]{1,0:T(8,128)(2,1)S(1)} %fusion.104, s32[256]{0:T(256)S(1)} %copy-done.11), kind=kOutput, calls=%fused_computation.34 | convolution fusion | flops 168427520 | bytes 2229248 | tf_op jit(solution)/shard_map/dot_general | solution.py:220
  144.3 3.1 %collective-permute-start.13 = (bf16[96,1024]{1,0:T(8,128)(2,1)S(1)}, bf16[96,1024]{1,0:T(8,128)(2,1)S(1)}, u32[]{:S(2)}, u32[]{:S(2)}) collective-permute-start(bf16[96,1024]{1,0:T(8,128)(2,1)S(1)} %pad_maximum_fusion.5), channel_id=1, source_target_pairs={{0,3},{1,0},{2,1},{3,2},{4,7},{5,4},{6,5},{7,6},{8,11},{9,8},{10,9... | collective-permute-start | bytes 589832 | tf_op jit(solution)/shard_map/ppermute | solution.py:57
  147.5 4.0 %collective-permute-done.12 = bf16[96,1024]{1,0:T(8,128)(2,1)S(1)} collective-permute-done((bf16[96,1024]{1,0:T(8,128)(2,1)S(1)}, bf16[96,1024]{1,0:T(8,128)(2,1)S(1)}, u32[]{:S(2)}, u32[]{:S(2)}) %collective-permute-start.12) | collective-permute-done | bytes 196640 | tf_op jit(solution)/shard_map/ppermute | solution.py:56
  151.5 2.7 %collective-permute-start.15 = (bf16[32,1024]{1,0:T(8,128)(2,1)S(1)}, bf16[32,1024]{1,0:T(8,128)(2,1)S(1)}, u32[]{:S(2)}, u32[]{:S(2)}) collective-permute-start(bf16[32,1024]{1,0:T(8,128)(2,1)S(1)} %slice.249), channel_id=1, source_target_pairs={{0,3},{1,0},{2,1},{3,2},{4,7},{5,4},{6,5},{7,6},{8,11},{9,8},{10,9... | collective-permute-start | bytes 196616 | tf_op jit(solution)/shard_map/ppermute | solution.py:59
  (126 shorter events, 25.9 us)
Async XLA Ops:
  0.6 22.2 %copy-start = (bf16[3,1024,256]{2,1,0:T(8,128)(2,1)S(1)}, bf16[3,1024,256]{2,1,0:T(8,128)(2,1)}, u32[]{:S(2)}) copy-start(bf16[3,1024,256]{2,1,0:T(8,128)(2,1)} %param.29) | copy-start | bytes 4718596
  4.5 15.5 %copy-start.6 = (s32[64,32]{0,1:T(8,128)S(1)}, s32[64,32]{0,1:T(8,128)}, u32[]{:S(2)}) copy-start(s32[64,32]{0,1:T(8,128)} %param.32) | copy-start | bytes 24580
  6.7 16.1 %copy-start.2 = (bf16[256,1024]{1,0:T(8,128)(2,1)S(1)}, bf16[256,1024]{1,0:T(8,128)(2,1)}, u32[]{:S(2)}) copy-start(bf16[256,1024]{1,0:T(8,128)(2,1)} %param.22) | copy-start | bytes 1572868
  6.7 16.1 %copy-start.14 = (f32[3,256]{1,0:T(4,128)S(1)}, f32[3,256]{1,0:T(4,128)}, u32[]{:S(2)}) copy-start(f32[3,256]{1,0:T(4,128)} %param.31) | copy-start | bytes 9220
  6.7 31.6 %all-to-all-start = ((bf16[64,2,2112]{2,1,0:T(2,128)(2,1)}), bf16[64,2,2112]{2,1,0:T(2,128)(2,1)S(1)}, u32[]{:S(2)}, u32[]{:S(2)}) async-start(bf16[64,2,2112]{2,1,0:T(2,128)(2,1)} %reshape.152), calls=%async_computation | async-start | bytes 1114112 | tf_op jit(solution)/shard_map/all_to_all | solution.py:136
  40.3 14.8 %collective-permute-start = (bf16[528,512]{1,0:T(8,128)(2,1)}, bf16[528,512]{1,0:T(8,128)(2,1)S(1)}, u32[]{:S(2)}, u32[]{:S(2)}) collective-permute-start(bf16[528,512]{1,0:T(8,128)(2,1)} %fusion.77), channel_id=1, source_target_pairs={{0,1},{1,2},{2,3},{3,0},{4,5},{5,6},{6,7},{7,4},{8,9},{9,10},{10,1... | collective-permute-start | bytes 1622024 | tf_op jit(solution)/shard_map/ppermute | solution.py:146
  41.5 13.7 %collective-permute-start.1 = (bf16[528,512]{1,0:T(8,128)(2,1)}, bf16[528,512]{1,0:T(8,128)(2,1)S(1)}, u32[]{:S(2)}, u32[]{:S(2)}) collective-permute-start(bf16[528,512]{1,0:T(8,128)(2,1)} %fusion.77), channel_id=1, source_target_pairs={{0,3},{1,0},{2,1},{3,2},{4,7},{5,4},{6,5},{7,6},{8,11},{9,8},{10,9... | collective-permute-start | bytes 1622024 | tf_op jit(solution)/shard_map/ppermute | solution.py:147
  55.1 11.7 %collective-permute-start.2 = (bf16[272,512]{1,0:T(8,128)(2,1)S(1)}, bf16[272,512]{1,0:T(8,128)(2,1)}, u32[]{:S(2)}, u32[]{:S(2)}) collective-permute-start(bf16[272,512]{1,0:T(8,128)(2,1)S(1)} %slice.219), channel_id=1, source_target_pairs={{0,1},{1,2},{2,3},{3,0},{4,5},{5,6},{6,7},{7,4},{8,9},{9,10},{10,1... | collective-permute-start | bytes 835592 | tf_op jit(solution)/shard_map/ppermute | solution.py:150
  57.7 10.1 %collective-permute-start.3 = (bf16[256,512]{1,0:T(8,128)(2,1)}, bf16[256,512]{1,0:T(8,128)(2,1)}, u32[]{:S(2)}, u32[]{:S(2)}) collective-permute-start(bf16[256,512]{1,0:T(8,128)(2,1)} %slice.223), channel_id=1, source_target_pairs={{0,3},{1,0},{2,1},{3,2},{4,7},{5,4},{6,5},{7,6},{8,11},{9,8},{10,9... | collective-permute-start | bytes 786440 | tf_op jit(solution)/shard_map/ppermute | solution.py:149
  71.5 6.0 %collective-permute-start.4 = (bf16[96,1024]{1,0:T(8,128)(2,1)S(1)}, bf16[96,1024]{1,0:T(8,128)(2,1)S(1)}, u32[]{:S(2)}, u32[]{:S(2)}) collective-permute-start(bf16[96,1024]{1,0:T(8,128)(2,1)S(1)} %pad_maximum_fusion.2), channel_id=1, source_target_pairs={{0,1},{1,2},{2,3},{3,0},{4,5},{5,6},{6,7},{7,4},{8,9},{9,10},{10,1... | collective-permute-start | bytes 589832 | tf_op jit(solution)/shard_map/ppermute | solution.py:56
  71.8 5.7 %collective-permute-start.5 = (bf16[96,1024]{1,0:T(8,128)(2,1)S(1)}, bf16[96,1024]{1,0:T(8,128)(2,1)S(1)}, u32[]{:S(2)}, u32[]{:S(2)}) collective-permute-start(bf16[96,1024]{1,0:T(8,128)(2,1)S(1)} %pad_maximum_fusion.3), channel_id=1, source_target_pairs={{0,3},{1,0},{2,1},{3,2},{4,7},{5,4},{6,5},{7,6},{8,11},{9,8},{10,9... | collective-permute-start | bytes 589832 | tf_op jit(solution)/shard_map/ppermute | solution.py:57
  77.5 4.3 %collective-permute-start.6 = (bf16[32,1024]{1,0:T(8,128)(2,1)S(1)}, bf16[32,1024]{1,0:T(8,128)(2,1)S(1)}, u32[]{:S(2)}, u32[]{:S(2)}) collective-permute-start(bf16[32,1024]{1,0:T(8,128)(2,1)S(1)} %slice.231), channel_id=1, source_target_pairs={{0,1},{1,2},{2,3},{3,0},{4,5},{5,6},{6,7},{7,4},{8,9},{9,10},{10,1... | collective-permute-start | bytes 196616 | tf_op jit(solution)/shard_map/ppermute | solution.py:58
  77.5 4.3 %collective-permute-start.7 = (bf16[32,1024]{1,0:T(8,128)(2,1)S(1)}, bf16[32,1024]{1,0:T(8,128)(2,1)S(1)}, u32[]{:S(2)}, u32[]{:S(2)}) collective-permute-start(bf16[32,1024]{1,0:T(8,128)(2,1)S(1)} %slice.232), channel_id=1, source_target_pairs={{0,3},{1,0},{2,1},{3,2},{4,7},{5,4},{6,5},{7,6},{8,11},{9,8},{10,9... | collective-permute-start | bytes 196616 | tf_op jit(solution)/shard_map/ppermute | solution.py:59
  81.9 7.9 %collective-permute-start.8 = (bf16[64,1024]{1,0:T(8,128)(2,1)S(1)}, bf16[64,1024]{1,0:T(8,128)(2,1)S(1)}, u32[]{:S(2)}, u32[]{:S(2)}) collective-permute-start(bf16[64,1024]{1,0:T(8,128)(2,1)S(1)} %get-tuple-element.5), channel_id=1, source_target_pairs={{0,3},{1,0},{2,1},{3,2},{4,7},{5,4},{6,5},{7,6},{8,11},{9,8},{10,9... | collective-permute-start | bytes 393224 | tf_op jit(solution)/shard_map/ppermute | solution.py:74
  84.7 5.0 %collective-permute-start.10 = (bf16[64,1024]{1,0:T(8,128)(2,1)S(1)}, bf16[64,1024]{1,0:T(8,128)(2,1)S(1)}, u32[]{:S(2)}, u32[]{:S(2)}) collective-permute-start(bf16[64,1024]{1,0:T(8,128)(2,1)S(1)} %get-tuple-element.5), channel_id=1, source_target_pairs={{0,1},{1,2},{2,3},{3,0},{4,5},{5,6},{6,7},{7,4},{8,9},{9,10},{10,1... | collective-permute-start | bytes 393224 | tf_op jit(solution)/shard_map/ppermute | solution.py:73
  89.8 5.2 %collective-permute-start.11 = (bf16[32,1024]{1,0:T(8,128)(2,1)S(1)}, bf16[32,1024]{1,0:T(8,128)(2,1)S(1)}, u32[]{:S(2)}, u32[]{:S(2)}) collective-permute-start(bf16[32,1024]{1,0:T(8,128)(2,1)S(1)} %slice.234), channel_id=1, source_target_pairs={{0,1},{1,2},{2,3},{3,0},{4,5},{5,6},{6,7},{7,4},{8,9},{9,10},{10,1... | collective-permute-start | bytes 196616 | tf_op jit(solution)/shard_map/ppermute | solution.py:76
  89.8 5.2 %collective-permute-start.9 = (bf16[32,1024]{1,0:T(8,128)(2,1)S(1)}, bf16[32,1024]{1,0:T(8,128)(2,1)S(1)}, u32[]{:S(2)}, u32[]{:S(2)}) collective-permute-start(bf16[32,1024]{1,0:T(8,128)(2,1)S(1)} %slice.233), channel_id=1, source_target_pairs={{0,3},{1,0},{2,1},{3,2},{4,7},{5,4},{6,5},{7,6},{8,11},{9,8},{10,9... | collective-permute-start | bytes 196616 | tf_op jit(solution)/shard_map/ppermute | solution.py:76
  97.4 44.7 %copy-start.5 = (bf16[256,256]{1,0:T(8,128)(2,1)}, bf16[256,256]{1,0:T(8,128)(2,1)S(1)}, u32[]{:S(2)}) copy-start(bf16[256,256]{1,0:T(8,128)(2,1)S(1)} %fusion.104) | copy-start | bytes 393220
  98.9 40.1 %copy-start.4 = (bf16[256,1024]{1,0:T(8,128)(2,1)S(1)}, bf16[256,1024]{1,0:T(8,128)(2,1)}, u32[]{:S(2)}) copy-start(bf16[256,1024]{1,0:T(8,128)(2,1)} %param.35) | copy-start | bytes 1572868
  98.9 40.1 %all-to-all-start.1 = ((bf16[64,32,256]{2,1,0:T(8,128)(2,1)}), bf16[64,32,256]{2,1,0:T(8,128)(2,1)S(1)}, u32[]{:S(2)}, u32[]{:S(2)}) async-start(bf16[64,32,256]{2,1,0:T(8,128)(2,1)} %bitcast.106), calls=%async_computation.1 | async-start | bytes 2097152 | tf_op jit(solution)/shard_map/all_to_all | solution.py:211
  144.2 7.2 %collective-permute-start.12 = (bf16[96,1024]{1,0:T(8,128)(2,1)S(1)}, bf16[96,1024]{1,0:T(8,128)(2,1)S(1)}, u32[]{:S(2)}, u32[]{:S(2)}) collective-permute-start(bf16[96,1024]{1,0:T(8,128)(2,1)S(1)} %pad_maximum_fusion.4), channel_id=1, source_target_pairs={{0,1},{1,2},{2,3},{3,0},{4,5},{5,6},{6,7},{7,4},{8,9},{9,10},{10,1... | collective-permute-start | bytes 589832 | tf_op jit(solution)/shard_map/ppermute | solution.py:56
  144.3 7.1 %collective-permute-start.13 = (bf16[96,1024]{1,0:T(8,128)(2,1)S(1)}, bf16[96,1024]{1,0:T(8,128)(2,1)S(1)}, u32[]{:S(2)}, u32[]{:S(2)}) collective-permute-start(bf16[96,1024]{1,0:T(8,128)(2,1)S(1)} %pad_maximum_fusion.5), channel_id=1, source_target_pairs={{0,3},{1,0},{2,1},{3,2},{4,7},{5,4},{6,5},{7,6},{8,11},{9,8},{10,9... | collective-permute-start | bytes 589832 | tf_op jit(solution)/shard_map/ppermute | solution.py:57
  151.5 4.3 %collective-permute-start.14 = (bf16[32,1024]{1,0:T(8,128)(2,1)S(1)}, bf16[32,1024]{1,0:T(8,128)(2,1)S(1)}, u32[]{:S(2)}, u32[]{:S(2)}) collective-permute-start(bf16[32,1024]{1,0:T(8,128)(2,1)S(1)} %slice.248), channel_id=1, source_target_pairs={{0,1},{1,2},{2,3},{3,0},{4,5},{5,6},{6,7},{7,4},{8,9},{9,10},{10,1... | collective-permute-start | bytes 196616 | tf_op jit(solution)/shard_map/ppermute | solution.py:58
  151.5 4.3 %collective-permute-start.15 = (bf16[32,1024]{1,0:T(8,128)(2,1)S(1)}, bf16[32,1024]{1,0:T(8,128)(2,1)S(1)}, u32[]{:S(2)}, u32[]{:S(2)}) collective-permute-start(bf16[32,1024]{1,0:T(8,128)(2,1)S(1)} %slice.249), channel_id=1, source_target_pairs={{0,3},{1,0},{2,1},{3,2},{4,7},{5,4},{6,5},{7,6},{8,11},{9,8},{10,9... | collective-permute-start | bytes 196616 | tf_op jit(solution)/shard_map/ppermute | solution.py:59
  (12 other events, 71.4 us)

commit v8 on v6

--- a/solution.py
+++ b/solution.py
@@ -71,7 +71,6 @@
     mem_width = memory.shape[1]
     col_share = mem_width // share_count
     capacity = 2 * event_rows // owner_count
-    send_rows = owner_count * capacity
 
     owner = event_owner[:, 0]
     match = owner[:, None] == lax.broadcasted_iota(jnp.int32, (1, owner_count), 1)
@@ -123,6 +122,7 @@
     for k in range(1, neighbours.shape[1]):
         neigh_count = neigh_count + one_hot(neighbours[:, k], recv_rows, F32)
     neigh_count = lax.optimization_barrier(neigh_count.astype(BF16))
+    pick = lax.optimization_barrier(one_hot(state_slots.reshape(-1), mem_rows))
     state_proj = jnp.dot(memory, w_msg_state, preferred_element_type=F32)
     sp_hi = state_proj.astype(BF16)
     sp_lo = (state_proj - sp_hi.astype(F32)).astype(BF16)
@@ -162,20 +162,20 @@
     updated = (1.0 - update_gate) * candidate + update_gate * old_state
     new_memory = jnp.where((counts > 0.0)[:, None], updated, old_state).astype(BF16)
 
-    pick = one_hot(state_slots.reshape(-1), mem_rows)
     outgoing = jnp.dot(pick, new_memory, preferred_element_type=F32).astype(BF16)
     outgoing = outgoing.reshape(state_slots.shape[0], state_slots.shape[1], col_share)
+    self_state = jnp.dot(
+        one_hot(query_slots, mem_rows), new_memory, preferred_element_type=F32
+    ).astype(BF16)
+    self_part = lax.optimization_barrier(jnp.dot(self_state, w_self, preferred_element_type=F32))
     relayed = lax.all_to_all(outgoing, "nodes", split_axis=0, concat_axis=0, tiled=True)
     relayed = relayed.reshape(relayed.shape[0] * relayed.shape[1], col_share)
     neigh_total = jnp.dot(neigh_count, relayed, preferred_element_type=F32)
     neigh_mean = (neigh_total / neighbours.shape[1]).astype(BF16)
-    self_state = jnp.dot(
-        one_hot(query_slots, mem_rows), new_memory, preferred_element_type=F32
-    ).astype(BF16)
     summed = mp_reduce_scatter(
         (
             jnp.dot(neigh_mean, w_neigh, preferred_element_type=F32)
-            + jnp.dot(self_state, w_self, preferred_element_type=F32)
+            + self_part
         ).astype(BF16),
         "mp",
         share_count,
@@ -208,6 +208,7 @@
         P(),
     )
     out_specs = (P("nodes", "mp"), P(("nodes", "mp"), None))
+
     return jax.shard_map(
         per_device, mesh=mesh, in_specs=in_specs, out_specs=out_specs, check_vma=False
     )

time: 145 us -> 143 us (0.986)
  waiting for transfers between devices: 64.7 us -> 61.1 us
    all_to_all x1, waiting for transfers between devices: 24.3 us -> 22.9 us  [per_device(): lax.all_to_all(outgoing, 'nodes', split_axis=0, concat_axis=0, tiled=True)]
    convert_element_type x4 -> x5, other arithmetic: 1.95 us -> 3.31 us  [one_hot(): (index[:, None] == lax.broadcasted_iota(jnp.int32, (1, size), 1)).astype(...]
  transfers between devices with their start and end apart: 15 -> 15, of which waited for: 9 -> 10; matrix products, arithmetic and copies ran while one was open for 15% -> 17% of each run, Pallas kernels for 0% -> 0%
where the time goes in v8:
time: 143 us; the launch traced here: 142 us
  waiting for transfers between devices  61.1 us (43%)
  starting transfers between devices  36.7 us (26%)
  matrix products  25.4 us (18%)
  other arithmetic  12.5 us (9%)
  local copies, waits for them, and re-layouts  5.09 us (4%)
    all_to_all x1, waiting for transfers between devices, per_device(): lax.all_to_all(outgoing, 'nodes', split_axis=0, concat_axis=0, tiled=True)  22.9 us
    all_to_all x1, starting transfers between devices, per_device(): lax.all_to_all(payload, 'nodes', split_axis=0, concat_axis=0, tiled=True)  13.3 us
    all_to_all x1, waiting for transfers between devices, per_device(): lax.all_to_all(payload, 'nodes', split_axis=0, concat_axis=0, tiled=True)  13 us
    dot_general x4, matrix products, per_device(): part = jnp.dot(seg, hidden_msg, preferred_element_type=F32)  11.9 us
    ppermute x6, waiting for transfers between devices, mp_reduce_scatter(): got = lax.ppermute(ahead[t], axis, [(i, (i + t) % n) for i in range(n)])  10.5 us
    all_to_all x1, starting transfers between devices, per_device(): lax.all_to_all(outgoing, 'nodes', split_axis=0, concat_axis=0, tiled=True)  9.62 us
    ppermute x1, waiting for transfers between devices, per_device(): from_below = lax.ppermute(mine, 'mp', up)  8.97 us
    ppermute x3, waiting for transfers between devices, mp_all_gather(): rel.append(lax.ppermute(piece, axis, [(i, (i - t) % n) for i in range(n)]))  5.72 us
  transfers between devices with their start and end apart: 15, of which 10 were waited for; matrix products, arithmetic and copies ran while one was open for 17% of the time, Pallas kernels for 0%

profile of v8, /device:TPU:1, one launch (start us, length us, event | category | flops | bytes accessed | tf_op | source)
XLA Modules:
  0.0 141.9 jit_solution(8662442344841061480)
XLA Ops:
  0.7 1.4 %fusion.26 = f32[1024]{0:T(1024)S(1)} fusion(s32[1024]{0:T(1024)} %bitcast.110), kind=kOutput, calls=%fused_computation.51 | convolution fusion | flops 135527424 | bytes 8192 | tf_op jit(solution)/shard_map/dot_general | solution.py:81
  6.7 13.3 %all-to-all-start = ((bf16[64,2,2112]{2,1,0:T(2,128)(2,1)}), bf16[64,2,2112]{2,1,0:T(2,128)(2,1)S(1)}, u32[]{:S(2)}, u32[]{:S(2)}) async-start(bf16[64,2,2112]{2,1,0:T(2,128)(2,1)} %reshape.148), calls=%async_computation | async-start | bytes 1114112 | tf_op jit(solution)/shard_map/all_to_all | solution.py:96
  21.5 2.3 %fusion.152 = (bf16[256,512]{1,0:T(8,128)(2,1)}, bf16[256,512]{1,0:T(8,128)(2,1)}) fusion(bf16[256,1024]{1,0:T(8,128)(2,1)} %param.22, bf16[1024,512]{1,0:T(8,128)(2,1)S(1)} %copy-done.4), kind=kOutput, calls=%fused_computation.211 | convolution fusion | flops 268959744 | bytes 2097152 | tf_op jit(solution)/shard_map/dot_general | solution.py:126
  23.9 1.5 %fusion.15 = f32[3,256,256]{2,1,0:T(8,128)} fusion(bf16[3,1024,256]{2,1,0:T(8,128)(2,1)S(1)} %copy-done, bf16[256,1024]{1,0:T(8,128)(2,1)S(1)} %copy-done.5, f32[3,256]{1,0:T(4,128)S(1)} %copy-done.16), kind=kOutput, calls=%fused_computation.37 | convolution fusion | flops 402849792 | bytes 2886656 | tf_op jit(solution)/shard_map/nd,gdc->gnc/dot_general | solution.py:155
  25.4 13.0 %all-to-all-done = bf16[64,2,2112]{2,1,0:T(2,128)(2,1)S(1)} async-done(((bf16[64,2,2112]{2,1,0:T(2,128)(2,1)}), bf16[64,2,2112]{2,1,0:T(2,128)(2,1)S(1)}, u32[]{:S(2)}, u32[]{:S(2)}) %all-to-all-start) | async-done | bytes 540704 | tf_op jit(solution)/shard_map/all_to_all | solution.py:96
  41.5 1.5 %collective-permute-start.1 = (bf16[528,512]{1,0:T(8,128)(2,1)}, bf16[528,512]{1,0:T(8,128)(2,1)S(1)}, u32[]{:S(2)}, u32[]{:S(2)}) collective-permute-start(bf16[528,512]{1,0:T(8,128)(2,1)} %fusion.77), channel_id=1, source_target_pairs={{0,3},{1,0},{2,1},{3,2},{4,7},{5,4},{6,5},{7,6},{8,11},{9,8},{10,9... | collective-permute-start | bytes 1622024 | tf_op jit(solution)/shard_map/ppermute | solution.py:107
  43.2 2.9 %fusion.20 = f32[256,512]{1,0:T(8,128)} fusion(bf16[512,256]{1,0:T(8,128)(2,1)S(1)} %fusion.99, bf16[512,512]{1,0:T(8,128)(2,1)S(1)} %reshape.125, f32[512]{0:T(512)S(1)} %copy-done.19, s32[512]{0:T(512)S(1)} %reshape.130, bf16[256,512]{1,0:T(8,128)(2,1)} %get-tuple-element.15, bf16[256,512]{1,0:T(8,128)(2,1)} %get-tuple-element.14, bf16[512,512]{1,0:T(8,128)(2,1)} %param.23), kind=kOutput, calls=%fused_computation.43 | convolution fusion | flops 678297600 | bytes 2363392 | tf_op jit(solution)/shard_map/dot_general | solution.py:140
  46.2 9.0 %collective-permute-done = bf16[528,512]{1,0:T(8,128)(2,1)S(1)} collective-permute-done((bf16[528,512]{1,0:T(8,128)(2,1)}, bf16[528,512]{1,0:T(8,128)(2,1)S(1)}, u32[]{:S(2)}, u32[]{:S(2)}) %collective-permute-start) | collective-permute-done | bytes 540704 | tf_op jit(solution)/shard_map/ppermute | solution.py:106
  57.9 2.7 %collective-permute-start.3 = (bf16[256,512]{1,0:T(8,128)(2,1)}, bf16[256,512]{1,0:T(8,128)(2,1)}, u32[]{:S(2)}, u32[]{:S(2)}) collective-permute-start(bf16[256,512]{1,0:T(8,128)(2,1)} %slice.151), channel_id=1, source_target_pairs={{0,3},{1,0},{2,1},{3,2},{4,7},{5,4},{6,5},{7,6},{8,11},{9,8},{10,9... | collective-permute-start | bytes 786440 | tf_op jit(solution)/shard_map/ppermute | solution.py:109
  60.6 3.1 %fusion.18 = f32[256,512]{1,0:T(8,128)} fusion(bf16[512,256]{1,0:T(8,128)(2,1)} %fusion.101, bf16[512,512]{1,0:T(8,128)(2,1)S(1)} %slice.150, f32[512]{0:T(512)S(1)} %copy-done.19, s32[512]{0:T(512)S(1)} %bitcast.102, bf16[256,512]{1,0:T(8,128)(2,1)} %get-tuple-element.15, bf16[256,512]{1,0:T(8,128)(2,1)} %get-tuple-element.14, bf16[512,512]{1,0:T(8,128)(2,1)} %param.23), kind=kOutput, calls=%fused_computation.41 | convolution fusion | flops 678297600 | bytes 2363392 | tf_op jit(solution)/shard_map/dot_general | solution.py:140
  63.7 3.4 %fusion.23 = f32[256,512]{1,0:T(8,128)} fusion(f32[256,512]{1,0:T(8,128)} %fusion.18, f32[256,512]{1,0:T(8,128)} %fusion.20, bf16[512,256]{1,0:T(8,128)(2,1)} %fusion.100, bf16[512,512]{1,0:T(8,128)(2,1)S(1)} %slice.149, f32[512]{0:T(512)S(1)} %copy-done.19, s32[512]{0:T(512)S(1)} %bitcast.106, bf16[256,512]{1,0:T(8,128)(2,1)} %get-tuple-element.15, ...), kind=kOutput, calls=%fused_computation.46 | convolution fusion | flops 678559744 | bytes 3411968 | tf_op jit(solution)/shard_map/dot_general | solution.py:140
  68.1 2.5 %fusion.22 = f32[256,512]{1,0:T(8,128)S(1)} fusion(f32[256,512]{1,0:T(8,128)} %fusion.23, bf16[272,512]{1,0:T(8,128)(2,1)} %collective-permute-done.2, bf16[256,512]{1,0:T(8,128)(2,1)} %collective-permute-done.3, bf16[512,256]{1,0:T(8,128)(2,1)S(1)} %fusion.102, f32[512]{0:T(512)S(1)} %copy-done.19, s32[512]{0:T(512)S(1)} %bitcast.109, ...), kind=kOutput, calls=%fused_computation.45 | convolution fusion | flops 679477248 | bytes 2904064 | tf_op jit(solution)/shard_map/dot_general | solution.py:140
  74.6 4.5 %collective-permute-done.4 = bf16[64,1024]{1,0:T(8,128)(2,1)S(1)} collective-permute-done((bf16[64,1024]{1,0:T(8,128)(2,1)S(1)}, bf16[64,1024]{1,0:T(8,128)(2,1)S(1)}, u32[]{:S(2)}, u32[]{:S(2)}) %collective-permute-start.4) | collective-permute-done | bytes 131104 | tf_op jit(solution)/shard_map/ppermute | solution.py:31
  79.6 2.2 %collective-permute-start.7 = (bf16[64,1024]{1,0:T(8,128)(2,1)S(1)}, bf16[64,1024]{1,0:T(8,128)(2,1)S(1)}, u32[]{:S(2)}, u32[]{:S(2)}) collective-permute-start(bf16[64,1024]{1,0:T(8,128)(2,1)S(1)} %get-tuple-element.5), channel_id=1, source_target_pairs={{0,3},{1,0},{2,1},{3,2},{4,7},{5,4},{6,5},{7,6},{8,11},{9,8},{10,9... | collective-permute-start | bytes 393224 | tf_op jit(solution)/shard_map/ppermute | solution.py:39
  82.5 2.6 %collective-permute-done.7 = bf16[64,1024]{1,0:T(8,128)(2,1)S(1)} collective-permute-done((bf16[64,1024]{1,0:T(8,128)(2,1)S(1)}, bf16[64,1024]{1,0:T(8,128)(2,1)S(1)}, u32[]{:S(2)}, u32[]{:S(2)}) %collective-permute-start.7) | collective-permute-done | bytes 131104 | tf_op jit(solution)/shard_map/ppermute | solution.py:39
  85.2 2.1 %collective-permute-done.8 = bf16[64,1024]{1,0:T(8,128)(2,1)S(1)} collective-permute-done((bf16[64,1024]{1,0:T(8,128)(2,1)S(1)}, bf16[64,1024]{1,0:T(8,128)(2,1)S(1)}, u32[]{:S(2)}, u32[]{:S(2)}) %collective-permute-start.8) | collective-permute-done | bytes 131104 | tf_op jit(solution)/shard_map/ppermute | solution.py:39
  90.7 1.4 %convolution_convert_fusion = bf16[2048,256]{1,0:T(8,128)(2,1)} fusion(bf16[2048,256]{1,0:T(8,128)(2,1)S(1)} %copy-done.2, bf16[256,256]{1,0:T(8,128)(2,1)S(1)} %fusion.104), kind=kOutput, calls=%fused_computation.2 | convolution fusion | flops 268959744 | bytes 2228224 | tf_op jit(solution)/shard_map/dot_general | solution.py:165
  92.2 9.6 %all-to-all-start.1 = ((bf16[64,32,256]{2,1,0:T(8,128)(2,1)}), bf16[64,32,256]{2,1,0:T(8,128)(2,1)S(1)}, u32[]{:S(2)}, u32[]{:S(2)}) async-start(bf16[64,32,256]{2,1,0:T(8,128)(2,1)} %bitcast.31), calls=%async_computation.1 | async-start | bytes 2097152 | tf_op jit(solution)/shard_map/all_to_all | solution.py:171
  101.8 3.8 %add_convert_fusion = bf16[256,2048]{1,0:T(8,128)(2,1)} fusion(s32[256]{0:T(256)S(1)} %bitcast.120, s32[256]{0:T(256)S(1)} %bitcast.121, s32[256]{0:T(256)S(1)} %bitcast.113, s32[256]{0:T(256)S(1)} %bitcast.114, s32[256]{0:T(256)S(1)} %bitcast.115, s32[256]{0:T(256)S(1)} %bitcast.116, s32[256]{0:T(256)S(1)} %bitcast.117, s32[256]{0:T(256)S(1)} %bitcast.118, ...), kind=kLoop, calls=%fused_computation.4 | loop fusion | flops 15728640 | bytes 1058816 | tf_op jit(solution)/shard_map/convert_element_type | solution.py:124
  105.6 1.5 %fusion.27 = f32[256,1024]{1,0:T(8,128)} fusion(bf16[256,1024]{1,0:T(8,128)(2,1)S(1)} %copy-done.7, bf16[256,256]{1,0:T(8,128)(2,1)S(1)} %fusion.104, s32[256]{0:T(256)S(1)} %copy-done.13), kind=kOutput, calls=%fused_computation.52 | convolution fusion | flops 167903232 | bytes 1704960 | tf_op jit(solution)/shard_map/dot_general | solution.py:170
  107.1 22.9 %all-to-all-done.1 = bf16[64,32,256]{2,1,0:T(8,128)(2,1)S(1)} async-done(((bf16[64,32,256]{2,1,0:T(8,128)(2,1)}), bf16[64,32,256]{2,1,0:T(8,128)(2,1)S(1)}, u32[]{:S(2)}, u32[]{:S(2)}) %all-to-all-start.1) | async-done | bytes 1048608 | tf_op jit(solution)/shard_map/all_to_all | solution.py:171
  130.0 2.6 %fusion.14 = bf16[256,1024]{1,0:T(8,128)(2,1)S(1)} fusion(f32[256,1024]{1,0:T(8,128)} %fusion.27, bf16[256,1024]{1,0:T(8,128)(2,1)} %param.35, bf16[256,2048]{1,0:T(8,128)(2,1)} %add_convert_fusion, bf16[2048,256]{1,0:T(8,128)(2,1)S(1)} %bitcast.95), kind=kOutput, calls=%fused_computation.35 | convolution fusion | flops 403308544 | bytes 4194304 | tf_op jit(solution)/shard_map/dot_general | solution.py:177
  132.9 1.8 %collective-permute-start.11 = (bf16[64,1024]{1,0:T(8,128)(2,1)S(1)}, bf16[64,1024]{1,0:T(8,128)(2,1)S(1)}, u32[]{:S(2)}, u32[]{:S(2)}) collective-permute-start(bf16[64,1024]{1,0:T(8,128)(2,1)S(1)} %get-tuple-element.9), channel_id=1, source_target_pairs={{0,2},{1,3},{2,0},{3,1},{4,6},{5,7},{6,4},{7,5},{8,10},{9,11},{10,... | collective-permute-start | bytes 393224 | tf_op jit(solution)/shard_map/ppermute | solution.py:31
  135.6 4.5 %collective-permute-done.10 = bf16[64,1024]{1,0:T(8,128)(2,1)S(1)} collective-permute-done((bf16[64,1024]{1,0:T(8,128)(2,1)S(1)}, bf16[64,1024]{1,0:T(8,128)(2,1)S(1)}, u32[]{:S(2)}, u32[]{:S(2)}) %collective-permute-start.10) | collective-permute-done | bytes 131104 | tf_op jit(solution)/shard_map/ppermute | solution.py:31
  (113 shorter events, 24.7 us)
Async XLA Ops:
  0.6 23.3 %copy-start = (bf16[3,1024,256]{2,1,0:T(8,128)(2,1)S(1)}, bf16[3,1024,256]{2,1,0:T(8,128)(2,1)}, u32[]{:S(2)}) copy-start(bf16[3,1024,256]{2,1,0:T(8,128)(2,1)} %param.29) | copy-start | bytes 4718596
  4.5 15.5 %copy-start.8 = (s32[64,32]{0,1:T(8,128)S(1)}, s32[64,32]{0,1:T(8,128)}, u32[]{:S(2)}) copy-start(s32[64,32]{0,1:T(8,128)} %param.32) | copy-start | bytes 24580
  6.7 14.8 %copy-start.4 = (bf16[1024,512]{1,0:T(8,128)(2,1)S(1)}, bf16[1024,512]{1,0:T(8,128)(2,1)}, u32[]{:S(2)}) copy-start(bf16[1024,512]{1,0:T(8,128)(2,1)} %param.24) | copy-start | bytes 3145732
  6.7 31.6 %all-to-all-start = ((bf16[64,2,2112]{2,1,0:T(2,128)(2,1)}), bf16[64,2,2112]{2,1,0:T(2,128)(2,1)S(1)}, u32[]{:S(2)}, u32[]{:S(2)}) async-start(bf16[64,2,2112]{2,1,0:T(2,128)(2,1)} %reshape.148), calls=%async_computation | async-start | bytes 1114112 | tf_op jit(solution)/shard_map/all_to_all | solution.py:96
  40.3 14.8 %collective-permute-start = (bf16[528,512]{1,0:T(8,128)(2,1)}, bf16[528,512]{1,0:T(8,128)(2,1)S(1)}, u32[]{:S(2)}, u32[]{:S(2)}) collective-permute-start(bf16[528,512]{1,0:T(8,128)(2,1)} %fusion.77), channel_id=1, source_target_pairs={{0,1},{1,2},{2,3},{3,0},{4,5},{5,6},{6,7},{7,4},{8,9},{9,10},{10,1... | collective-permute-start | bytes 1622024 | tf_op jit(solution)/shard_map/ppermute | solution.py:106
  41.5 14.8 %collective-permute-start.1 = (bf16[528,512]{1,0:T(8,128)(2,1)}, bf16[528,512]{1,0:T(8,128)(2,1)S(1)}, u32[]{:S(2)}, u32[]{:S(2)}) collective-permute-start(bf16[528,512]{1,0:T(8,128)(2,1)} %fusion.77), channel_id=1, source_target_pairs={{0,3},{1,0},{2,1},{3,2},{4,7},{5,4},{6,5},{7,6},{8,11},{9,8},{10,9... | collective-permute-start | bytes 1622024 | tf_op jit(solution)/shard_map/ppermute | solution.py:107
  55.1 11.9 %collective-permute-start.2 = (bf16[272,512]{1,0:T(8,128)(2,1)S(1)}, bf16[272,512]{1,0:T(8,128)(2,1)}, u32[]{:S(2)}, u32[]{:S(2)}) collective-permute-start(bf16[272,512]{1,0:T(8,128)(2,1)S(1)} %slice.147), channel_id=1, source_target_pairs={{0,1},{1,2},{2,3},{3,0},{4,5},{5,6},{6,7},{7,4},{8,9},{9,10},{10,1... | collective-permute-start | bytes 835592 | tf_op jit(solution)/shard_map/ppermute | solution.py:110
  57.9 10.3 %collective-permute-start.3 = (bf16[256,512]{1,0:T(8,128)(2,1)}, bf16[256,512]{1,0:T(8,128)(2,1)}, u32[]{:S(2)}, u32[]{:S(2)}) collective-permute-start(bf16[256,512]{1,0:T(8,128)(2,1)} %slice.151), channel_id=1, source_target_pairs={{0,3},{1,0},{2,1},{3,2},{4,7},{5,4},{6,5},{7,6},{8,11},{9,8},{10,9... | collective-permute-start | bytes 786440 | tf_op jit(solution)/shard_map/ppermute | solution.py:109
  71.8 7.3 %collective-permute-start.4 = (bf16[64,1024]{1,0:T(8,128)(2,1)S(1)}, bf16[64,1024]{1,0:T(8,128)(2,1)S(1)}, u32[]{:S(2)}, u32[]{:S(2)}) collective-permute-start(bf16[64,1024]{1,0:T(8,128)(2,1)S(1)} %get-tuple-element.11), channel_id=1, source_target_pairs={{0,1},{1,2},{2,3},{3,0},{4,5},{5,6},{6,7},{7,4},{8,9},{9,10},{10,1... | collective-permute-start | bytes 393224 | tf_op jit(solution)/shard_map/ppermute | solution.py:31
  71.9 7.2 %collective-permute-start.5 = (bf16[64,1024]{1,0:T(8,128)(2,1)S(1)}, bf16[64,1024]{1,0:T(8,128)(2,1)S(1)}, u32[]{:S(2)}, u32[]{:S(2)}) collective-permute-start(bf16[64,1024]{1,0:T(8,128)(2,1)S(1)} %get-tuple-element.12), channel_id=1, source_target_pairs={{0,2},{1,3},{2,0},{3,1},{4,6},{5,7},{6,4},{7,5},{8,10},{9,11},{10,... | collective-permute-start | bytes 393224 | tf_op jit(solution)/shard_map/ppermute | solution.py:31
  73.3 6.2 %collective-permute-start.6 = (bf16[64,1024]{1,0:T(8,128)(2,1)S(1)}, bf16[64,1024]{1,0:T(8,128)(2,1)S(1)}, u32[]{:S(2)}, u32[]{:S(2)}) collective-permute-start(bf16[64,1024]{1,0:T(8,128)(2,1)S(1)} %get-tuple-element.13), channel_id=1, source_target_pairs={{0,3},{1,0},{2,1},{3,2},{4,7},{5,4},{6,5},{7,6},{8,11},{9,8},{10,9... | collective-permute-start | bytes 393224 | tf_op jit(solution)/shard_map/ppermute | solution.py:31
  79.6 8.8 %copy-start.14 = (bf16[3,1024,256]{2,1,0:T(8,128)(2,1)S(1)}, bf16[3,1024,256]{2,1,0:T(8,128)(2,1)}, u32[]{:S(2)}) copy-start(bf16[3,1024,256]{2,1,0:T(8,128)(2,1)} %param.28) | copy-start | bytes 4718596
  79.6 8.8 %copy-start.17 = (f32[1024]{0:T(1024)S(1)}, f32[1024]{0:T(1024)}, u32[]{:S(2)}) copy-start(f32[1024]{0:T(1024)} %param.27) | copy-start | bytes 12292
  79.6 5.5 %collective-permute-start.7 = (bf16[64,1024]{1,0:T(8,128)(2,1)S(1)}, bf16[64,1024]{1,0:T(8,128)(2,1)S(1)}, u32[]{:S(2)}, u32[]{:S(2)}) collective-permute-start(bf16[64,1024]{1,0:T(8,128)(2,1)S(1)} %get-tuple-element.5), channel_id=1, source_target_pairs={{0,3},{1,0},{2,1},{3,2},{4,7},{5,4},{6,5},{7,6},{8,11},{9,8},{10,9... | collective-permute-start | bytes 393224 | tf_op jit(solution)/shard_map/ppermute | solution.py:39
  81.9 5.4 %collective-permute-start.8 = (bf16[64,1024]{1,0:T(8,128)(2,1)S(1)}, bf16[64,1024]{1,0:T(8,128)(2,1)S(1)}, u32[]{:S(2)}, u32[]{:S(2)}) collective-permute-start(bf16[64,1024]{1,0:T(8,128)(2,1)S(1)} %get-tuple-element.5), channel_id=1, source_target_pairs={{0,2},{1,3},{2,0},{3,1},{4,6},{5,7},{6,4},{7,5},{8,10},{9,11},{10,... | collective-permute-start | bytes 393224 | tf_op jit(solution)/shard_map/ppermute | solution.py:39
  81.9 6.4 %collective-permute-start.9 = (bf16[64,1024]{1,0:T(8,128)(2,1)S(1)}, bf16[64,1024]{1,0:T(8,128)(2,1)S(1)}, u32[]{:S(2)}, u32[]{:S(2)}) collective-permute-start(bf16[64,1024]{1,0:T(8,128)(2,1)S(1)} %get-tuple-element.5), channel_id=1, source_target_pairs={{0,1},{1,2},{2,3},{3,0},{4,5},{5,6},{6,7},{7,4},{8,9},{9,10},{10,1... | collective-permute-start | bytes 393224 | tf_op jit(solution)/shard_map/ppermute | solution.py:39
  90.7 14.9 %copy-start.3 = (bf16[256,256]{1,0:T(8,128)(2,1)}, bf16[256,256]{1,0:T(8,128)(2,1)S(1)}, u32[]{:S(2)}) copy-start(bf16[256,256]{1,0:T(8,128)(2,1)S(1)} %fusion.104) | copy-start | bytes 393220
  92.2 9.6 %copy-start.9 = (s32[256,10]{0,1:T(8,128)S(1)}, s32[256,10]{0,1:T(8,128)}, u32[]{:S(2)}) copy-start(s32[256,10]{0,1:T(8,128)} %param.33) | copy-start | bytes 30724
  92.2 13.5 %copy-start.7 = (bf16[256,1024]{1,0:T(8,128)(2,1)S(1)}, bf16[256,1024]{1,0:T(8,128)(2,1)}, u32[]{:S(2)}) copy-start(bf16[256,1024]{1,0:T(8,128)(2,1)} %param.36) | copy-start | bytes 1572868
  92.2 13.5 %copy-start.13 = (s32[256]{0:T(256)S(1)}, s32[256]{0:T(256)}, u32[]{:S(2)}) copy-start(s32[256]{0:T(256)} %param.34) | copy-start | bytes 3076
  92.2 37.8 %all-to-all-start.1 = ((bf16[64,32,256]{2,1,0:T(8,128)(2,1)}), bf16[64,32,256]{2,1,0:T(8,128)(2,1)S(1)}, u32[]{:S(2)}, u32[]{:S(2)}) async-start(bf16[64,32,256]{2,1,0:T(8,128)(2,1)} %bitcast.31), calls=%async_computation.1 | async-start | bytes 2097152 | tf_op jit(solution)/shard_map/all_to_all | solution.py:171
  132.8 7.2 %collective-permute-start.10 = (bf16[64,1024]{1,0:T(8,128)(2,1)S(1)}, bf16[64,1024]{1,0:T(8,128)(2,1)S(1)}, u32[]{:S(2)}, u32[]{:S(2)}) collective-permute-start(bf16[64,1024]{1,0:T(8,128)(2,1)S(1)} %get-tuple-element.8), channel_id=1, source_target_pairs={{0,1},{1,2},{2,3},{3,0},{4,5},{5,6},{6,7},{7,4},{8,9},{9,10},{10,1... | collective-permute-start | bytes 393224 | tf_op jit(solution)/shard_map/ppermute | solution.py:31
  132.9 7.2 %collective-permute-start.11 = (bf16[64,1024]{1,0:T(8,128)(2,1)S(1)}, bf16[64,1024]{1,0:T(8,128)(2,1)S(1)}, u32[]{:S(2)}, u32[]{:S(2)}) collective-permute-start(bf16[64,1024]{1,0:T(8,128)(2,1)S(1)} %get-tuple-element.9), channel_id=1, source_target_pairs={{0,2},{1,3},{2,0},{3,1},{4,6},{5,7},{6,4},{7,5},{8,10},{9,11},{10,... | collective-permute-start | bytes 393224 | tf_op jit(solution)/shard_map/ppermute | solution.py:31
  134.7 6.5 %collective-permute-start.12 = (bf16[64,1024]{1,0:T(8,128)(2,1)S(1)}, bf16[64,1024]{1,0:T(8,128)(2,1)S(1)}, u32[]{:S(2)}, u32[]{:S(2)}) collective-permute-start(bf16[64,1024]{1,0:T(8,128)(2,1)S(1)} %get-tuple-element.10), channel_id=1, source_target_pairs={{0,3},{1,0},{2,1},{3,2},{4,7},{5,4},{6,5},{7,6},{8,11},{9,8},{10,9... | collective-permute-start | bytes 393224 | tf_op jit(solution)/shard_map/ppermute | solution.py:31
  (11 other events, 37.0 us)

commit v9 on v8

--- a/solution.py
+++ b/solution.py
@@ -90,10 +90,12 @@
     slot_col = jnp.broadcast_to((event_slot + 1).astype(BF16)[:, None], (event_rows, 128))
     id_part = jnp.dot(route, slot_col, preferred_element_type=F32)[:, 0] - 1.0
     id_block = jnp.pad(id_part.reshape(owner_count, per), ((0, 0), (0, 128 - per)))
+    width = per * feat_width + 128
     payload = jnp.concatenate(
         [feat_part.reshape(owner_count, per * feat_width), id_block.astype(BF16)], axis=1
-    )
+    ).reshape(owner_count, 2, width // 2)
     landed = lax.all_to_all(payload, "nodes", split_axis=0, concat_axis=0, tiled=True)
+    landed = landed.reshape(owner_count, width)
     piece_rows = owner_count * per
     id_row = landed[:, per * feat_width : per * feat_width + per].reshape(1, piece_rows)
     id_rows = jnp.pad(id_row, ((0, 15), (0, feat_width - piece_rows)))
@@ -122,7 +124,6 @@
     for k in range(1, neighbours.shape[1]):
         neigh_count = neigh_count + one_hot(neighbours[:, k], recv_rows, F32)
     neigh_count = lax.optimization_barrier(neigh_count.astype(BF16))
-    pick = lax.optimization_barrier(one_hot(state_slots.reshape(-1), mem_rows))
     state_proj = jnp.dot(memory, w_msg_state, preferred_element_type=F32)
     sp_hi = state_proj.astype(BF16)
     sp_lo = (state_proj - sp_hi.astype(F32)).astype(BF16)
@@ -162,6 +163,7 @@
     updated = (1.0 - update_gate) * candidate + update_gate * old_state
     new_memory = jnp.where((counts > 0.0)[:, None], updated, old_state).astype(BF16)
 
+    pick = one_hot(state_slots.reshape(-1), mem_rows)
     outgoing = jnp.dot(pick, new_memory, preferred_element_type=F32).astype(BF16)
     outgoing = outgoing.reshape(state_slots.shape[0], state_slots.shape[1], col_share)
     self_state = jnp.dot(

time: 143 us -> 141 us (0.986)
  other arithmetic: 12.5 us -> 10.1 us
  waiting for transfers between devices: 61.1 us -> 63.5 us
    unnamed x50 -> x45, local copies, waits for them, and re-layouts: 2.57 us -> 0.74 us
    reshape x0 -> x2, local copies, waits for them, and re-layouts: none -> 1.59 us  [the longest x1 1.22 us: per_device(): payload = jnp.concatenate([feat_part.reshape(owner_count, per * feat_widt...]
    convert_element_type x5 -> x4, other arithmetic: 3.31 us -> 1.97 us  [one_hot(): (index[:, None] == lax.broadcasted_iota(jnp.int32, (1, size), 1)).astype(...]
  transfers between devices with their start and end apart: 15 -> 15, of which waited for: 10 -> 9; matrix products, arithmetic and copies ran while one was open for 17% -> 16% of each run, Pallas kernels for 0% -> 0%
where the time goes in v9:
time: 141 us
  waiting for transfers between devices  63.5 us (45%)
  starting transfers between devices  35.8 us (25%)
  matrix products  25.6 us (18%)
  other arithmetic  10.1 us (7%)
  local copies, waits for them, and re-layouts  4.33 us (3%)
    all_to_all x1, waiting for transfers between devices, per_device(): lax.all_to_all(outgoing, 'nodes', split_axis=0, concat_axis=0, tiled=True)  22.9 us
    all_to_all x1, waiting for transfers between devices, per_device(): lax.all_to_all(payload, 'nodes', split_axis=0, concat_axis=0, tiled=True)  14.3 us
    all_to_all x1, starting transfers between devices, per_device(): lax.all_to_all(payload, 'nodes', split_axis=0, concat_axis=0, tiled=True)  13.3 us
    dot_general x4, matrix products, per_device(): part = jnp.dot(seg, hidden_msg, preferred_element_type=F32)  12 us
    ppermute x6, waiting for transfers between devices, mp_reduce_scatter(): got = lax.ppermute(ahead[t], axis, [(i, (i + t) % n) for i in range(n)])  11.6 us
    all_to_all x1, starting transfers between devices, per_device(): lax.all_to_all(outgoing, 'nodes', split_axis=0, concat_axis=0, tiled=True)  9.53 us
    ppermute x1, waiting for transfers between devices, per_device(): from_below = lax.ppermute(mine, 'mp', up)  8.96 us
    ppermute x3, waiting for transfers between devices, mp_all_gather(): rel.append(lax.ppermute(piece, axis, [(i, (i - t) % n) for i in range(n)]))  5.73 us
  transfers between devices with their start and end apart: 15, of which 9 were waited for; matrix products, arithmetic and copies ran while one was open for 16% of the time, Pallas kernels for 0%

profile of v9, /device:TPU:1, one launch (start us, length us, event | category | flops | bytes accessed | tf_op | source)
XLA Modules:
  0.0 140.5 jit_solution(3649695804045694321)
XLA Ops:
  0.7 1.4 %fusion.25 = f32[1024]{0:T(1024)S(1)} fusion(s32[1024]{0:T(1024)} %bitcast.103), kind=kOutput, calls=%fused_computation.50 | convolution fusion | flops 135527424 | bytes 8192 | tf_op jit(solution)/shard_map/dot_general | solution.py:81
  5.3 13.3 %all-to-all-start = ((bf16[64,2,2112]{2,1,0:T(2,128)(2,1)}), bf16[64,2,2112]{2,1,0:T(2,128)(2,1)S(1)}, u32[]{:S(2)}, u32[]{:S(2)}) async-start(bf16[64,2,2112]{2,1,0:T(2,128)(2,1)} %reshape.129), calls=%async_computation | async-start | bytes 1114112 | tf_op jit(solution)/shard_map/all_to_all | solution.py:97
  18.7 2.4 %fusion.151 = (bf16[256,512]{1,0:T(8,128)(2,1)}, bf16[256,512]{1,0:T(8,128)(2,1)}) fusion(bf16[256,1024]{1,0:T(8,128)(2,1)} %param.22, bf16[1024,512]{1,0:T(8,128)(2,1)S(1)} %copy-done.2), kind=kOutput, calls=%fused_computation.209 | convolution fusion | flops 268959744 | bytes 2097152 | tf_op jit(solution)/shard_map/dot_general | solution.py:127
  21.1 1.5 %fusion.14 = f32[3,256,256]{2,1,0:T(8,128)} fusion(bf16[3,1024,256]{2,1,0:T(8,128)(2,1)S(1)} %copy-done, bf16[256,1024]{1,0:T(8,128)(2,1)S(1)} %copy-done.3, f32[3,256]{1,0:T(4,128)S(1)} %copy-done.15), kind=kOutput, calls=%fused_computation.36 | convolution fusion | flops 402849792 | bytes 2886656 | tf_op jit(solution)/shard_map/nd,gdc->gnc/dot_general | solution.py:156
  22.6 14.3 %all-to-all-done = bf16[64,2,2112]{2,1,0:T(2,128)(2,1)S(1)} async-done(((bf16[64,2,2112]{2,1,0:T(2,128)(2,1)}), bf16[64,2,2112]{2,1,0:T(2,128)(2,1)S(1)}, u32[]{:S(2)}, u32[]{:S(2)}) %all-to-all-start) | async-done | bytes 540704 | tf_op jit(solution)/shard_map/all_to_all | solution.py:97
  39.8 1.5 %collective-permute-start.1 = (bf16[528,512]{1,0:T(8,128)(2,1)}, bf16[528,512]{1,0:T(8,128)(2,1)S(1)}, u32[]{:S(2)}, u32[]{:S(2)}) collective-permute-start(bf16[528,512]{1,0:T(8,128)(2,1)} %fusion.77), channel_id=1, source_target_pairs={{0,3},{1,0},{2,1},{3,2},{4,7},{5,4},{6,5},{7,6},{8,11},{9,8},{10,9... | collective-permute-start | bytes 1622024 | tf_op jit(solution)/shard_map/ppermute | solution.py:109
  41.5 2.9 %fusion.19 = f32[256,512]{1,0:T(8,128)} fusion(bf16[512,256]{1,0:T(8,128)(2,1)S(1)} %fusion.98, bf16[512,512]{1,0:T(8,128)(2,1)S(1)} %reshape.131, f32[512]{0:T(512)S(1)} %copy-done.18, s32[512]{0:T(512)S(1)} %reshape.136, bf16[256,512]{1,0:T(8,128)(2,1)} %get-tuple-element.15, bf16[256,512]{1,0:T(8,128)(2,1)} %get-tuple-element.14, bf16[512,512]{1,0:T(8,128)(2,1)} %param.23), kind=kOutput, calls=%fused_computation.42 | convolution fusion | flops 678297600 | bytes 2363392 | tf_op jit(solution)/shard_map/dot_general | solution.py:141
  44.4 9.0 %collective-permute-done = bf16[528,512]{1,0:T(8,128)(2,1)S(1)} collective-permute-done((bf16[528,512]{1,0:T(8,128)(2,1)}, bf16[528,512]{1,0:T(8,128)(2,1)S(1)}, u32[]{:S(2)}, u32[]{:S(2)}) %collective-permute-start) | collective-permute-done | bytes 540704 | tf_op jit(solution)/shard_map/ppermute | solution.py:108
  56.1 2.7 %collective-permute-start.3 = (bf16[256,512]{1,0:T(8,128)(2,1)}, bf16[256,512]{1,0:T(8,128)(2,1)}, u32[]{:S(2)}, u32[]{:S(2)}) collective-permute-start(bf16[256,512]{1,0:T(8,128)(2,1)} %slice.151), channel_id=1, source_target_pairs={{0,3},{1,0},{2,1},{3,2},{4,7},{5,4},{6,5},{7,6},{8,11},{9,8},{10,9... | collective-permute-start | bytes 786440 | tf_op jit(solution)/shard_map/ppermute | solution.py:111
  58.8 3.1 %fusion.17 = f32[256,512]{1,0:T(8,128)} fusion(bf16[512,256]{1,0:T(8,128)(2,1)} %fusion.100, bf16[512,512]{1,0:T(8,128)(2,1)S(1)} %slice.150, f32[512]{0:T(512)S(1)} %copy-done.18, s32[512]{0:T(512)S(1)} %bitcast.95, bf16[256,512]{1,0:T(8,128)(2,1)} %get-tuple-element.15, bf16[256,512]{1,0:T(8,128)(2,1)} %get-tuple-element.14, bf16[512,512]{1,0:T(8,128)(2,1)} %param.23), kind=kOutput, calls=%fused_computation.40 | convolution fusion | flops 678297600 | bytes 2363392 | tf_op jit(solution)/shard_map/dot_general | solution.py:141
  62.0 3.4 %fusion.22 = f32[256,512]{1,0:T(8,128)} fusion(f32[256,512]{1,0:T(8,128)} %fusion.17, f32[256,512]{1,0:T(8,128)} %fusion.19, bf16[512,256]{1,0:T(8,128)(2,1)} %fusion.99, bf16[512,512]{1,0:T(8,128)(2,1)S(1)} %slice.149, f32[512]{0:T(512)S(1)} %copy-done.18, s32[512]{0:T(512)S(1)} %bitcast.99, bf16[256,512]{1,0:T(8,128)(2,1)} %get-tuple-element.15, ...), kind=kOutput, calls=%fused_computation.45 | convolution fusion | flops 678559744 | bytes 3411968 | tf_op jit(solution)/shard_map/dot_general | solution.py:141
  66.4 2.5 %fusion.21 = f32[256,512]{1,0:T(8,128)S(1)} fusion(f32[256,512]{1,0:T(8,128)} %fusion.22, bf16[272,512]{1,0:T(8,128)(2,1)} %collective-permute-done.2, bf16[256,512]{1,0:T(8,128)(2,1)} %collective-permute-done.3, bf16[512,256]{1,0:T(8,128)(2,1)S(1)} %fusion.101, f32[512]{0:T(512)S(1)} %copy-done.18, s32[512]{0:T(512)S(1)} %bitcast.102, ...), kind=kOutput, calls=%fused_computation.44 | convolution fusion | flops 679477248 | bytes 2904064 | tf_op jit(solution)/shard_map/dot_general | solution.py:141
  71.7 1.4 collective-permute-start.6
  73.1 6.0 %collective-permute-done.4 = bf16[64,1024]{1,0:T(8,128)(2,1)S(1)} collective-permute-done((bf16[64,1024]{1,0:T(8,128)(2,1)S(1)}, bf16[64,1024]{1,0:T(8,128)(2,1)S(1)}, u32[]{:S(2)}, u32[]{:S(2)}) %collective-permute-start.4) | collective-permute-done | bytes 131104 | tf_op jit(solution)/shard_map/ppermute | solution.py:31
  81.1 1.9 %collective-permute-done.7 = bf16[64,1024]{1,0:T(8,128)(2,1)S(1)} collective-permute-done((bf16[64,1024]{1,0:T(8,128)(2,1)S(1)}, bf16[64,1024]{1,0:T(8,128)(2,1)S(1)}, u32[]{:S(2)}, u32[]{:S(2)}) %collective-permute-start.7) | collective-permute-done | bytes 131104 | tf_op jit(solution)/shard_map/ppermute | solution.py:39
  83.1 2.8 %collective-permute-done.8 = bf16[64,1024]{1,0:T(8,128)(2,1)S(1)} collective-permute-done((bf16[64,1024]{1,0:T(8,128)(2,1)S(1)}, bf16[64,1024]{1,0:T(8,128)(2,1)S(1)}, u32[]{:S(2)}, u32[]{:S(2)}) %collective-permute-start.8) | collective-permute-done | bytes 131104 | tf_op jit(solution)/shard_map/ppermute | solution.py:39
  89.3 1.5 %convolution_convert_fusion = bf16[2048,256]{1,0:T(8,128)(2,1)} fusion(bf16[256,256]{1,0:T(8,128)(2,1)S(1)} %fusion.103, s32[2048]{0:T(1024)S(1)} %eq.404), kind=kOutput, calls=%fused_computation.2 | convolution fusion | flops 269484032 | bytes 1187840 | tf_op jit(solution)/shard_map/dot_general | solution.py:167
  90.8 9.5 %all-to-all-start.1 = ((bf16[64,32,256]{2,1,0:T(8,128)(2,1)}), bf16[64,32,256]{2,1,0:T(8,128)(2,1)S(1)}, u32[]{:S(2)}, u32[]{:S(2)}) async-start(bf16[64,32,256]{2,1,0:T(8,128)(2,1)} %bitcast.92), calls=%async_computation.1 | async-start | bytes 2097152 | tf_op jit(solution)/shard_map/all_to_all | solution.py:173
  100.4 3.8 %add_convert_fusion = bf16[256,2048]{1,0:T(8,128)(2,1)} fusion(s32[256]{0:T(256)S(1)} %bitcast.113, s32[256]{0:T(256)S(1)} %bitcast.114, s32[256]{0:T(256)S(1)} %bitcast.106, s32[256]{0:T(256)S(1)} %bitcast.107, s32[256]{0:T(256)S(1)} %bitcast.108, s32[256]{0:T(256)S(1)} %bitcast.109, s32[256]{0:T(256)S(1)} %bitcast.110, s32[256]{0:T(256)S(1)} %bitcast.111, ...), kind=kLoop, calls=%fused_computation.4 | loop fusion | flops 15728640 | bytes 1058816 | tf_op jit(solution)/shard_map/convert_element_type | solution.py:126
  104.2 1.5 %fusion.26 = f32[256,1024]{1,0:T(8,128)} fusion(bf16[256,1024]{1,0:T(8,128)(2,1)S(1)} %copy-done.5, bf16[256,256]{1,0:T(8,128)(2,1)S(1)} %fusion.103, s32[256]{0:T(256)S(1)} %copy-done.12), kind=kOutput, calls=%fused_computation.51 | convolution fusion | flops 167903232 | bytes 1704960 | tf_op jit(solution)/shard_map/dot_general | solution.py:172
  105.7 22.9 %all-to-all-done.1 = bf16[64,32,256]{2,1,0:T(8,128)(2,1)S(1)} async-done(((bf16[64,32,256]{2,1,0:T(8,128)(2,1)}), bf16[64,32,256]{2,1,0:T(8,128)(2,1)S(1)}, u32[]{:S(2)}, u32[]{:S(2)}) %all-to-all-start.1) | async-done | bytes 1048608 | tf_op jit(solution)/shard_map/all_to_all | solution.py:173
  128.5 2.6 %fusion.13 = bf16[256,1024]{1,0:T(8,128)(2,1)S(1)} fusion(f32[256,1024]{1,0:T(8,128)} %fusion.26, bf16[256,1024]{1,0:T(8,128)(2,1)} %param.35, bf16[256,2048]{1,0:T(8,128)(2,1)} %add_convert_fusion, bf16[2048,256]{1,0:T(8,128)(2,1)S(1)} %bitcast.89), kind=kOutput, calls=%fused_computation.34 | convolution fusion | flops 403308544 | bytes 4194304 | tf_op jit(solution)/shard_map/dot_general | solution.py:179
  131.5 1.8 %collective-permute-start.11 = (bf16[64,1024]{1,0:T(8,128)(2,1)S(1)}, bf16[64,1024]{1,0:T(8,128)(2,1)S(1)}, u32[]{:S(2)}, u32[]{:S(2)}) collective-permute-start(bf16[64,1024]{1,0:T(8,128)(2,1)S(1)} %get-tuple-element.9), channel_id=1, source_target_pairs={{0,2},{1,3},{2,0},{3,1},{4,6},{5,7},{6,4},{7,5},{8,10},{9,11},{10,... | collective-permute-start | bytes 393224 | tf_op jit(solution)/shard_map/ppermute | solution.py:31
  134.1 4.5 %collective-permute-done.10 = bf16[64,1024]{1,0:T(8,128)(2,1)S(1)} collective-permute-done((bf16[64,1024]{1,0:T(8,128)(2,1)S(1)}, bf16[64,1024]{1,0:T(8,128)(2,1)S(1)}, u32[]{:S(2)}, u32[]{:S(2)}) %collective-permute-start.10) | collective-permute-done | bytes 131104 | tf_op jit(solution)/shard_map/ppermute | solution.py:31
  (107 shorter events, 21.3 us)
Async XLA Ops:
  0.6 20.5 %copy-start = (bf16[3,1024,256]{2,1,0:T(8,128)(2,1)S(1)}, bf16[3,1024,256]{2,1,0:T(8,128)(2,1)}, u32[]{:S(2)}) copy-start(bf16[3,1024,256]{2,1,0:T(8,128)(2,1)} %param.29) | copy-start | bytes 4718596
  4.0 14.6 %copy-start.7 = (s32[64,32]{0,1:T(8,128)S(1)}, s32[64,32]{0,1:T(8,128)}, u32[]{:S(2)}) copy-start(s32[64,32]{0,1:T(8,128)} %param.32) | copy-start | bytes 24580
  4.0 14.7 %copy-start.2 = (bf16[1024,512]{1,0:T(8,128)(2,1)S(1)}, bf16[1024,512]{1,0:T(8,128)(2,1)}, u32[]{:S(2)}) copy-start(bf16[1024,512]{1,0:T(8,128)(2,1)} %param.24) | copy-start | bytes 3145732
  5.3 15.8 %copy-start.15 = (f32[3,256]{1,0:T(4,128)S(1)}, f32[3,256]{1,0:T(4,128)}, u32[]{:S(2)}) copy-start(f32[3,256]{1,0:T(4,128)} %param.31) | copy-start | bytes 9220
  5.3 31.6 %all-to-all-start = ((bf16[64,2,2112]{2,1,0:T(2,128)(2,1)}), bf16[64,2,2112]{2,1,0:T(2,128)(2,1)S(1)}, u32[]{:S(2)}, u32[]{:S(2)}) async-start(bf16[64,2,2112]{2,1,0:T(2,128)(2,1)} %reshape.129), calls=%async_computation | async-start | bytes 1114112 | tf_op jit(solution)/shard_map/all_to_all | solution.py:97
  38.6 14.8 %collective-permute-start = (bf16[528,512]{1,0:T(8,128)(2,1)}, bf16[528,512]{1,0:T(8,128)(2,1)S(1)}, u32[]{:S(2)}, u32[]{:S(2)}) collective-permute-start(bf16[528,512]{1,0:T(8,128)(2,1)} %fusion.77), channel_id=1, source_target_pairs={{0,1},{1,2},{2,3},{3,0},{4,5},{5,6},{6,7},{7,4},{8,9},{9,10},{10,1... | collective-permute-start | bytes 1622024 | tf_op jit(solution)/shard_map/ppermute | solution.py:108
  39.8 14.8 %collective-permute-start.1 = (bf16[528,512]{1,0:T(8,128)(2,1)}, bf16[528,512]{1,0:T(8,128)(2,1)S(1)}, u32[]{:S(2)}, u32[]{:S(2)}) collective-permute-start(bf16[528,512]{1,0:T(8,128)(2,1)} %fusion.77), channel_id=1, source_target_pairs={{0,3},{1,0},{2,1},{3,2},{4,7},{5,4},{6,5},{7,6},{8,11},{9,8},{10,9... | collective-permute-start | bytes 1622024 | tf_op jit(solution)/shard_map/ppermute | solution.py:109
  53.4 12.0 %collective-permute-start.2 = (bf16[272,512]{1,0:T(8,128)(2,1)S(1)}, bf16[272,512]{1,0:T(8,128)(2,1)}, u32[]{:S(2)}, u32[]{:S(2)}) collective-permute-start(bf16[272,512]{1,0:T(8,128)(2,1)S(1)} %slice.147), channel_id=1, source_target_pairs={{0,1},{1,2},{2,3},{3,0},{4,5},{5,6},{6,7},{7,4},{8,9},{9,10},{10,1... | collective-permute-start | bytes 835592 | tf_op jit(solution)/shard_map/ppermute | solution.py:112
  56.1 10.3 %collective-permute-start.3 = (bf16[256,512]{1,0:T(8,128)(2,1)}, bf16[256,512]{1,0:T(8,128)(2,1)}, u32[]{:S(2)}, u32[]{:S(2)}) collective-permute-start(bf16[256,512]{1,0:T(8,128)(2,1)} %slice.151), channel_id=1, source_target_pairs={{0,3},{1,0},{2,1},{3,2},{4,7},{5,4},{6,5},{7,6},{8,11},{9,8},{10,9... | collective-permute-start | bytes 786440 | tf_op jit(solution)/shard_map/ppermute | solution.py:111
  70.1 8.9 %collective-permute-start.4 = (bf16[64,1024]{1,0:T(8,128)(2,1)S(1)}, bf16[64,1024]{1,0:T(8,128)(2,1)S(1)}, u32[]{:S(2)}, u32[]{:S(2)}) collective-permute-start(bf16[64,1024]{1,0:T(8,128)(2,1)S(1)} %get-tuple-element.11), channel_id=1, source_target_pairs={{0,1},{1,2},{2,3},{3,0},{4,5},{5,6},{6,7},{7,4},{8,9},{9,10},{10,1... | collective-permute-start | bytes 393224 | tf_op jit(solution)/shard_map/ppermute | solution.py:31
  70.4 8.6 %collective-permute-start.5 = (bf16[64,1024]{1,0:T(8,128)(2,1)S(1)}, bf16[64,1024]{1,0:T(8,128)(2,1)S(1)}, u32[]{:S(2)}, u32[]{:S(2)}) collective-permute-start(bf16[64,1024]{1,0:T(8,128)(2,1)S(1)} %get-tuple-element.12), channel_id=1, source_target_pairs={{0,2},{1,3},{2,0},{3,1},{4,6},{5,7},{6,4},{7,5},{8,10},{9,11},{10,... | collective-permute-start | bytes 393224 | tf_op jit(solution)/shard_map/ppermute | solution.py:31
  71.7 7.3 %collective-permute-start.6 = (bf16[64,1024]{1,0:T(8,128)(2,1)S(1)}, bf16[64,1024]{1,0:T(8,128)(2,1)S(1)}, u32[]{:S(2)}, u32[]{:S(2)}) collective-permute-start(bf16[64,1024]{1,0:T(8,128)(2,1)S(1)} %get-tuple-element.13), channel_id=1, source_target_pairs={{0,3},{1,0},{2,1},{3,2},{4,7},{5,4},{6,5},{7,6},{8,11},{9,8},{10,9... | collective-permute-start | bytes 393224 | tf_op jit(solution)/shard_map/ppermute | solution.py:31
  79.2 3.9 %collective-permute-start.7 = (bf16[64,1024]{1,0:T(8,128)(2,1)S(1)}, bf16[64,1024]{1,0:T(8,128)(2,1)S(1)}, u32[]{:S(2)}, u32[]{:S(2)}) collective-permute-start(bf16[64,1024]{1,0:T(8,128)(2,1)S(1)} %get-tuple-element.5), channel_id=1, source_target_pairs={{0,3},{1,0},{2,1},{3,2},{4,7},{5,4},{6,5},{7,6},{8,11},{9,8},{10,9... | collective-permute-start | bytes 393224 | tf_op jit(solution)/shard_map/ppermute | solution.py:39
  80.4 5.4 %collective-permute-start.8 = (bf16[64,1024]{1,0:T(8,128)(2,1)S(1)}, bf16[64,1024]{1,0:T(8,128)(2,1)S(1)}, u32[]{:S(2)}, u32[]{:S(2)}) collective-permute-start(bf16[64,1024]{1,0:T(8,128)(2,1)S(1)} %get-tuple-element.5), channel_id=1, source_target_pairs={{0,2},{1,3},{2,0},{3,1},{4,6},{5,7},{6,4},{7,5},{8,10},{9,11},{10,... | collective-permute-start | bytes 393224 | tf_op jit(solution)/shard_map/ppermute | solution.py:39
  80.4 6.4 %collective-permute-start.9 = (bf16[64,1024]{1,0:T(8,128)(2,1)S(1)}, bf16[64,1024]{1,0:T(8,128)(2,1)S(1)}, u32[]{:S(2)}, u32[]{:S(2)}) collective-permute-start(bf16[64,1024]{1,0:T(8,128)(2,1)S(1)} %get-tuple-element.5), channel_id=1, source_target_pairs={{0,1},{1,2},{2,3},{3,0},{4,5},{5,6},{6,7},{7,4},{8,9},{9,10},{10,1... | collective-permute-start | bytes 393224 | tf_op jit(solution)/shard_map/ppermute | solution.py:39
  89.3 14.9 %copy-start.6 = (bf16[256,256]{1,0:T(8,128)(2,1)}, bf16[256,256]{1,0:T(8,128)(2,1)S(1)}, u32[]{:S(2)}) copy-start(bf16[256,256]{1,0:T(8,128)(2,1)S(1)} %fusion.103) | copy-start | bytes 393220
  89.3 11.1 %copy-start.8 = (s32[256,10]{0,1:T(8,128)S(1)}, s32[256,10]{0,1:T(8,128)}, u32[]{:S(2)}) copy-start(s32[256,10]{0,1:T(8,128)} %param.33) | copy-start | bytes 30724
  90.8 13.4 %copy-start.5 = (bf16[256,1024]{1,0:T(8,128)(2,1)S(1)}, bf16[256,1024]{1,0:T(8,128)(2,1)}, u32[]{:S(2)}) copy-start(bf16[256,1024]{1,0:T(8,128)(2,1)} %param.36) | copy-start | bytes 1572868
  90.8 13.4 %copy-start.12 = (s32[256]{0:T(256)S(1)}, s32[256]{0:T(256)}, u32[]{:S(2)}) copy-start(s32[256]{0:T(256)} %param.34) | copy-start | bytes 3076
  90.8 37.7 %all-to-all-start.1 = ((bf16[64,32,256]{2,1,0:T(8,128)(2,1)}), bf16[64,32,256]{2,1,0:T(8,128)(2,1)S(1)}, u32[]{:S(2)}, u32[]{:S(2)}) async-start(bf16[64,32,256]{2,1,0:T(8,128)(2,1)} %bitcast.92), calls=%async_computation.1 | async-start | bytes 2097152 | tf_op jit(solution)/shard_map/all_to_all | solution.py:173
  131.1 8.7 %copy-start.9 = (f32[1024]{0:T(1024)S(1)}, f32[1024]{0:T(1024)}, u32[]{:S(2)}) copy-start(f32[1024]{0:T(1024)} %param.37) | copy-start | bytes 12292
  131.4 7.2 %collective-permute-start.10 = (bf16[64,1024]{1,0:T(8,128)(2,1)S(1)}, bf16[64,1024]{1,0:T(8,128)(2,1)S(1)}, u32[]{:S(2)}, u32[]{:S(2)}) collective-permute-start(bf16[64,1024]{1,0:T(8,128)(2,1)S(1)} %get-tuple-element.8), channel_id=1, source_target_pairs={{0,1},{1,2},{2,3},{3,0},{4,5},{5,6},{6,7},{7,4},{8,9},{9,10},{10,1... | collective-permute-start | bytes 393224 | tf_op jit(solution)/shard_map/ppermute | solution.py:31
  131.5 7.2 %collective-permute-start.11 = (bf16[64,1024]{1,0:T(8,128)(2,1)S(1)}, bf16[64,1024]{1,0:T(8,128)(2,1)S(1)}, u32[]{:S(2)}, u32[]{:S(2)}) collective-permute-start(bf16[64,1024]{1,0:T(8,128)(2,1)S(1)} %get-tuple-element.9), channel_id=1, source_target_pairs={{0,2},{1,3},{2,0},{3,1},{4,6},{5,7},{6,4},{7,5},{8,10},{9,11},{10,... | collective-permute-start | bytes 393224 | tf_op jit(solution)/shard_map/ppermute | solution.py:31
  133.3 6.5 %collective-permute-start.12 = (bf16[64,1024]{1,0:T(8,128)(2,1)S(1)}, bf16[64,1024]{1,0:T(8,128)(2,1)S(1)}, u32[]{:S(2)}, u32[]{:S(2)}) collective-permute-start(bf16[64,1024]{1,0:T(8,128)(2,1)S(1)} %get-tuple-element.10), channel_id=1, source_target_pairs={{0,3},{1,0},{2,1},{3,2},{4,7},{5,4},{6,5},{7,6},{8,11},{9,8},{10,9... | collective-permute-start | bytes 393224 | tf_op jit(solution)/shard_map/ppermute | solution.py:31
  (10 other events, 37.9 us)

commit v10 on v9

--- a/solution.py
+++ b/solution.py
@@ -74,11 +74,19 @@
 
     owner = event_owner[:, 0]
     match = owner[:, None] == lax.broadcasted_iota(jnp.int32, (1, owner_count), 1)
-    earlier = (
-        lax.broadcasted_iota(jnp.int32, (event_rows, event_rows), 1)
-        < lax.broadcasted_iota(jnp.int32, (event_rows, event_rows), 0)
+    blk = 128
+    nblk = event_rows // blk
+    m_blk = match.astype(BF16).reshape(nblk, blk, owner_count)
+    tri = (
+        lax.broadcasted_iota(jnp.int32, (blk, blk), 1) < lax.broadcasted_iota(jnp.int32, (blk, blk), 0)
     ).astype(BF16)
-    before = jnp.dot(earlier, match.astype(BF16), preferred_element_type=F32)
+    inblock = jnp.einsum("rs,bso->bro", tri, m_blk, preferred_element_type=F32)
+    block_sum = jnp.sum(m_blk.astype(F32), axis=1)
+    tri_b = (
+        lax.broadcasted_iota(jnp.int32, (nblk, nblk), 1) < lax.broadcasted_iota(jnp.int32, (nblk, nblk), 0)
+    ).astype(F32)
+    offset = jnp.dot(tri_b, block_sum, precision=lax.Precision.HIGHEST)
+    before = (inblock + offset[:, None, :]).reshape(event_rows, owner_count)
     place = jnp.sum(jnp.where(match, before, 0.0), axis=1).astype(jnp.int32)
     per = capacity // share_count
     low = mp_index * per

time: 141 us -> 144 us (1.021)
  other arithmetic: 10.1 us -> 11.8 us
  transfers between devices with their start and end apart: 15 -> 15, of which waited for: 9 -> 10; matrix products, arithmetic and copies ran while one was open for 16% -> 16% of each run, Pallas kernels for 0% -> 0%
where the time goes in v10:
time: 144 us; the launch traced here: 143 us
  waiting for transfers between devices  62.5 us (43%)
  starting transfers between devices  36.8 us (26%)
  matrix products  26.4 us (18%)
  other arithmetic  11.8 us (8%)
  local copies, waits for them, and re-layouts  4.31 us (3%)
    all_to_all x1, waiting for transfers between devices, per_device(): lax.all_to_all(outgoing, 'nodes', split_axis=0, concat_axis=0, tiled=True)  22.8 us
    all_to_all x1, waiting for transfers between devices, per_device(): lax.all_to_all(payload, 'nodes', split_axis=0, concat_axis=0, tiled=True)  14.3 us
    all_to_all x1, starting transfers between devices, per_device(): lax.all_to_all(payload, 'nodes', split_axis=0, concat_axis=0, tiled=True)  13.3 us
    dot_general x4, matrix products, per_device(): part = jnp.dot(seg, hidden_msg, preferred_element_type=F32)  11.9 us
    ppermute x6, waiting for transfers between devices, mp_reduce_scatter(): got = lax.ppermute(ahead[t], axis, [(i, (i + t) % n) for i in range(n)])  10.6 us
    all_to_all x1, starting transfers between devices, per_device(): lax.all_to_all(outgoing, 'nodes', split_axis=0, concat_axis=0, tiled=True)  9.56 us
    ppermute x1, waiting for transfers between devices, per_device(): from_below = lax.ppermute(mine, 'mp', up)  8.98 us
    ppermute x3, waiting for transfers between devices, mp_all_gather(): rel.append(lax.ppermute(piece, axis, [(i, (i - t) % n) for i in range(n)]))  5.72 us
  transfers between devices with their start and end apart: 15, of which 10 were waited for; matrix products, arithmetic and copies ran while one was open for 16% of the time, Pallas kernels for 0%

profile of v10, /device:TPU:1, one launch (start us, length us, event | category | flops | bytes accessed | tf_op | source)
XLA Modules:
  0.0 142.9 jit_solution(10846389657904180411)
XLA Ops:
  3.4 1.9 %fusion.6 = bf16[512,512]{1,0:T(8,128)(2,1)S(1)} fusion(bf16[1024,512]{1,0:T(8,128)(2,1)} %param.19, s32[1024]{0:T(1024)S(1)} %fusion.139), kind=kOutput, calls=%fused_computation.26 | convolution fusion | flops 537657344 | bytes 1576960 | tf_op jit(solution)/shard_map/dot_general | solution.py:97
  7.7 13.3 %all-to-all-start = ((bf16[64,2,2112]{2,1,0:T(2,128)(2,1)}), bf16[64,2,2112]{2,1,0:T(2,128)(2,1)S(1)}, u32[]{:S(2)}, u32[]{:S(2)}) async-start(bf16[64,2,2112]{2,1,0:T(2,128)(2,1)} %reshape.170), calls=%async_computation | async-start | bytes 1114112 | tf_op jit(solution)/shard_map/all_to_all | solution.py:105
  21.2 2.4 %fusion.157 = (bf16[256,512]{1,0:T(8,128)(2,1)}, bf16[256,512]{1,0:T(8,128)(2,1)}) fusion(bf16[256,1024]{1,0:T(8,128)(2,1)} %param.22, bf16[1024,512]{1,0:T(8,128)(2,1)S(1)} %copy-done.2), kind=kOutput, calls=%fused_computation.218 | convolution fusion | flops 268959744 | bytes 2097152 | tf_op jit(solution)/shard_map/dot_general | solution.py:135
  23.6 1.5 %fusion.13 = f32[3,256,256]{2,1,0:T(8,128)} fusion(bf16[3,1024,256]{2,1,0:T(8,128)(2,1)S(1)} %copy-done, bf16[256,1024]{1,0:T(8,128)(2,1)S(1)} %copy-done.3, f32[3,256]{1,0:T(4,128)S(1)} %copy-done.13), kind=kOutput, calls=%fused_computation.34 | convolution fusion | flops 402849792 | bytes 2886656 | tf_op jit(solution)/shard_map/nd,gdc->gnc/dot_general | solution.py:164
  25.0 14.3 %all-to-all-done = bf16[64,2,2112]{2,1,0:T(2,128)(2,1)S(1)} async-done(((bf16[64,2,2112]{2,1,0:T(2,128)(2,1)}), bf16[64,2,2112]{2,1,0:T(2,128)(2,1)S(1)}, u32[]{:S(2)}, u32[]{:S(2)}) %all-to-all-start) | async-done | bytes 540704 | tf_op jit(solution)/shard_map/all_to_all | solution.py:105
  42.2 1.5 %collective-permute-start.1 = (bf16[528,512]{1,0:T(8,128)(2,1)}, bf16[528,512]{1,0:T(8,128)(2,1)S(1)}, u32[]{:S(2)}, u32[]{:S(2)}) collective-permute-start(bf16[528,512]{1,0:T(8,128)(2,1)} %fusion.77), channel_id=1, source_target_pairs={{0,3},{1,0},{2,1},{3,2},{4,7},{5,4},{6,5},{7,6},{8,11},{9,8},{10,9... | collective-permute-start | bytes 1622024 | tf_op jit(solution)/shard_map/ppermute | solution.py:117
  44.0 2.9 %fusion.18 = f32[256,512]{1,0:T(8,128)} fusion(bf16[512,256]{1,0:T(8,128)(2,1)S(1)} %fusion.98, bf16[512,512]{1,0:T(8,128)(2,1)S(1)} %reshape.172, f32[512]{0:T(512)S(1)} %copy-done.16, s32[512]{0:T(512)S(1)} %reshape.177, bf16[256,512]{1,0:T(8,128)(2,1)} %get-tuple-element.15, bf16[256,512]{1,0:T(8,128)(2,1)} %get-tuple-element.14, bf16[512,512]{1,0:T(8,128)(2,1)} %param.23), kind=kOutput, calls=%fused_computation.40 | convolution fusion | flops 678297600 | bytes 2363392 | tf_op jit(solution)/shard_map/dot_general | solution.py:149
  46.9 9.0 %collective-permute-done = bf16[528,512]{1,0:T(8,128)(2,1)S(1)} collective-permute-done((bf16[528,512]{1,0:T(8,128)(2,1)}, bf16[528,512]{1,0:T(8,128)(2,1)S(1)}, u32[]{:S(2)}, u32[]{:S(2)}) %collective-permute-start) | collective-permute-done | bytes 540704 | tf_op jit(solution)/shard_map/ppermute | solution.py:116
  58.6 2.7 %collective-permute-start.3 = (bf16[256,512]{1,0:T(8,128)(2,1)}, bf16[256,512]{1,0:T(8,128)(2,1)}, u32[]{:S(2)}, u32[]{:S(2)}) collective-permute-start(bf16[256,512]{1,0:T(8,128)(2,1)} %slice.151), channel_id=1, source_target_pairs={{0,3},{1,0},{2,1},{3,2},{4,7},{5,4},{6,5},{7,6},{8,11},{9,8},{10,9... | collective-permute-start | bytes 786440 | tf_op jit(solution)/shard_map/ppermute | solution.py:119
  61.3 3.1 %fusion.16 = f32[256,512]{1,0:T(8,128)} fusion(bf16[512,256]{1,0:T(8,128)(2,1)} %fusion.100, bf16[512,512]{1,0:T(8,128)(2,1)S(1)} %slice.150, f32[512]{0:T(512)S(1)} %copy-done.16, s32[512]{0:T(512)S(1)} %bitcast.114, bf16[256,512]{1,0:T(8,128)(2,1)} %get-tuple-element.15, bf16[256,512]{1,0:T(8,128)(2,1)} %get-tuple-element.14, bf16[512,512]{1,0:T(8,128)(2,1)} %param.23), kind=kOutput, calls=%fused_computation.38 | convolution fusion | flops 678297600 | bytes 2363392 | tf_op jit(solution)/shard_map/dot_general | solution.py:149
  64.4 3.4 %fusion.21 = f32[256,512]{1,0:T(8,128)} fusion(f32[256,512]{1,0:T(8,128)} %fusion.16, f32[256,512]{1,0:T(8,128)} %fusion.18, bf16[512,256]{1,0:T(8,128)(2,1)} %fusion.99, bf16[512,512]{1,0:T(8,128)(2,1)S(1)} %slice.149, f32[512]{0:T(512)S(1)} %copy-done.16, s32[512]{0:T(512)S(1)} %bitcast.118, bf16[256,512]{1,0:T(8,128)(2,1)} %get-tuple-element.15, ...), kind=kOutput, calls=%fused_computation.43 | convolution fusion | flops 678559744 | bytes 3411968 | tf_op jit(solution)/shard_map/dot_general | solution.py:149
  68.9 2.5 %fusion.20 = f32[256,512]{1,0:T(8,128)S(1)} fusion(f32[256,512]{1,0:T(8,128)} %fusion.21, bf16[272,512]{1,0:T(8,128)(2,1)} %collective-permute-done.2, bf16[256,512]{1,0:T(8,128)(2,1)} %collective-permute-done.3, bf16[512,256]{1,0:T(8,128)(2,1)S(1)} %fusion.101, f32[512]{0:T(512)S(1)} %copy-done.16, s32[512]{0:T(512)S(1)} %bitcast.121, ...), kind=kOutput, calls=%fused_computation.42 | convolution fusion | flops 679477248 | bytes 2904064 | tf_op jit(solution)/shard_map/dot_general | solution.py:149
  75.5 4.6 %collective-permute-done.4 = bf16[64,1024]{1,0:T(8,128)(2,1)S(1)} collective-permute-done((bf16[64,1024]{1,0:T(8,128)(2,1)S(1)}, bf16[64,1024]{1,0:T(8,128)(2,1)S(1)}, u32[]{:S(2)}, u32[]{:S(2)}) %collective-permute-start.4) | collective-permute-done | bytes 131104 | tf_op jit(solution)/shard_map/ppermute | solution.py:31
  80.5 2.2 %collective-permute-start.7 = (bf16[64,1024]{1,0:T(8,128)(2,1)S(1)}, bf16[64,1024]{1,0:T(8,128)(2,1)S(1)}, u32[]{:S(2)}, u32[]{:S(2)}) collective-permute-start(bf16[64,1024]{1,0:T(8,128)(2,1)S(1)} %get-tuple-element.5), channel_id=1, source_target_pairs={{0,3},{1,0},{2,1},{3,2},{4,7},{5,4},{6,5},{7,6},{8,11},{9,8},{10,9... | collective-permute-start | bytes 393224 | tf_op jit(solution)/shard_map/ppermute | solution.py:39
  83.5 2.6 %collective-permute-done.7 = bf16[64,1024]{1,0:T(8,128)(2,1)S(1)} collective-permute-done((bf16[64,1024]{1,0:T(8,128)(2,1)S(1)}, bf16[64,1024]{1,0:T(8,128)(2,1)S(1)}, u32[]{:S(2)}, u32[]{:S(2)}) %collective-permute-start.7) | collective-permute-done | bytes 131104 | tf_op jit(solution)/shard_map/ppermute | solution.py:39
  86.1 2.1 %collective-permute-done.8 = bf16[64,1024]{1,0:T(8,128)(2,1)S(1)} collective-permute-done((bf16[64,1024]{1,0:T(8,128)(2,1)S(1)}, bf16[64,1024]{1,0:T(8,128)(2,1)S(1)}, u32[]{:S(2)}, u32[]{:S(2)}) %collective-permute-start.8) | collective-permute-done | bytes 131104 | tf_op jit(solution)/shard_map/ppermute | solution.py:39
  91.6 1.5 %convolution_convert_fusion = bf16[2048,256]{1,0:T(8,128)(2,1)} fusion(bf16[256,256]{1,0:T(8,128)(2,1)S(1)} %fusion.103, s32[2048]{0:T(1024)S(1)} %eq.407), kind=kOutput, calls=%fused_computation | convolution fusion | flops 269484032 | bytes 1187840 | tf_op jit(solution)/shard_map/dot_general | solution.py:175
  93.2 9.6 %all-to-all-start.1 = ((bf16[64,32,256]{2,1,0:T(8,128)(2,1)}), bf16[64,32,256]{2,1,0:T(8,128)(2,1)S(1)}, u32[]{:S(2)}, u32[]{:S(2)}) async-start(bf16[64,32,256]{2,1,0:T(8,128)(2,1)} %bitcast.111), calls=%async_computation.1 | async-start | bytes 2097152 | tf_op jit(solution)/shard_map/all_to_all | solution.py:181
  102.8 3.8 %add_convert_fusion = bf16[256,2048]{1,0:T(8,128)(2,1)} fusion(s32[256]{0:T(256)S(1)} %bitcast.133, s32[256]{0:T(256)S(1)} %bitcast.134, s32[256]{0:T(256)S(1)} %bitcast.126, s32[256]{0:T(256)S(1)} %bitcast.127, s32[256]{0:T(256)S(1)} %bitcast.128, s32[256]{0:T(256)S(1)} %bitcast.129, s32[256]{0:T(256)S(1)} %bitcast.130, s32[256]{0:T(256)S(1)} %bitcast.131, ...), kind=kLoop, calls=%fused_computation.2 | loop fusion | flops 15728640 | bytes 1058816 | tf_op jit(solution)/shard_map/convert_element_type | solution.py:134
  106.6 1.5 %fusion.26 = f32[256,1024]{1,0:T(8,128)} fusion(bf16[256,1024]{1,0:T(8,128)(2,1)S(1)} %copy-done.5, bf16[256,256]{1,0:T(8,128)(2,1)S(1)} %fusion.103, s32[256]{0:T(256)S(1)} %copy-done.11), kind=kOutput, calls=%fused_computation.51 | convolution fusion | flops 167903232 | bytes 1704960 | tf_op jit(solution)/shard_map/dot_general | solution.py:180
  108.1 22.8 %all-to-all-done.1 = bf16[64,32,256]{2,1,0:T(8,128)(2,1)S(1)} async-done(((bf16[64,32,256]{2,1,0:T(8,128)(2,1)}), bf16[64,32,256]{2,1,0:T(8,128)(2,1)S(1)}, u32[]{:S(2)}, u32[]{:S(2)}) %all-to-all-start.1) | async-done | bytes 1048608 | tf_op jit(solution)/shard_map/all_to_all | solution.py:181
  130.9 2.6 %fusion.12 = bf16[256,1024]{1,0:T(8,128)(2,1)S(1)} fusion(f32[256,1024]{1,0:T(8,128)} %fusion.26, bf16[256,1024]{1,0:T(8,128)(2,1)} %param.35, bf16[256,2048]{1,0:T(8,128)(2,1)} %add_convert_fusion, bf16[2048,256]{1,0:T(8,128)(2,1)S(1)} %bitcast.108), kind=kOutput, calls=%fused_computation.32 | convolution fusion | flops 403308544 | bytes 4194304 | tf_op jit(solution)/shard_map/dot_general | solution.py:187
  133.9 1.8 %collective-permute-start.11 = (bf16[64,1024]{1,0:T(8,128)(2,1)S(1)}, bf16[64,1024]{1,0:T(8,128)(2,1)S(1)}, u32[]{:S(2)}, u32[]{:S(2)}) collective-permute-start(bf16[64,1024]{1,0:T(8,128)(2,1)S(1)} %get-tuple-element.9), channel_id=1, source_target_pairs={{0,2},{1,3},{2,0},{3,1},{4,6},{5,7},{6,4},{7,5},{8,10},{9,11},{10,... | collective-permute-start | bytes 393224 | tf_op jit(solution)/shard_map/ppermute | solution.py:31
  136.5 4.5 %collective-permute-done.10 = bf16[64,1024]{1,0:T(8,128)(2,1)S(1)} collective-permute-done((bf16[64,1024]{1,0:T(8,128)(2,1)S(1)}, bf16[64,1024]{1,0:T(8,128)(2,1)S(1)}, u32[]{:S(2)}, u32[]{:S(2)}) %collective-permute-start.10) | collective-permute-done | bytes 131104 | tf_op jit(solution)/shard_map/ppermute | solution.py:31
  (106 shorter events, 23.8 us)
Async XLA Ops:
  0.6 22.9 %copy-start = (bf16[3,1024,256]{2,1,0:T(8,128)(2,1)S(1)}, bf16[3,1024,256]{2,1,0:T(8,128)(2,1)}, u32[]{:S(2)}) copy-start(bf16[3,1024,256]{2,1,0:T(8,128)(2,1)} %param.29) | copy-start | bytes 4718596
  6.5 14.6 %copy-start.7 = (s32[64,32]{0,1:T(8,128)S(1)}, s32[64,32]{0,1:T(8,128)}, u32[]{:S(2)}) copy-start(s32[64,32]{0,1:T(8,128)} %param.32) | copy-start | bytes 24580
  6.5 14.7 %copy-start.2 = (bf16[1024,512]{1,0:T(8,128)(2,1)S(1)}, bf16[1024,512]{1,0:T(8,128)(2,1)}, u32[]{:S(2)}) copy-start(bf16[1024,512]{1,0:T(8,128)(2,1)} %param.24) | copy-start | bytes 3145732
  7.7 15.8 %copy-start.13 = (f32[3,256]{1,0:T(4,128)S(1)}, f32[3,256]{1,0:T(4,128)}, u32[]{:S(2)}) copy-start(f32[3,256]{1,0:T(4,128)} %param.31) | copy-start | bytes 9220
  7.7 31.6 %all-to-all-start = ((bf16[64,2,2112]{2,1,0:T(2,128)(2,1)}), bf16[64,2,2112]{2,1,0:T(2,128)(2,1)S(1)}, u32[]{:S(2)}, u32[]{:S(2)}) async-start(bf16[64,2,2112]{2,1,0:T(2,128)(2,1)} %reshape.170), calls=%async_computation | async-start | bytes 1114112 | tf_op jit(solution)/shard_map/all_to_all | solution.py:105
  41.0 14.8 %collective-permute-start = (bf16[528,512]{1,0:T(8,128)(2,1)}, bf16[528,512]{1,0:T(8,128)(2,1)S(1)}, u32[]{:S(2)}, u32[]{:S(2)}) collective-permute-start(bf16[528,512]{1,0:T(8,128)(2,1)} %fusion.77), channel_id=1, source_target_pairs={{0,1},{1,2},{2,3},{3,0},{4,5},{5,6},{6,7},{7,4},{8,9},{9,10},{10,1... | collective-permute-start | bytes 1622024 | tf_op jit(solution)/shard_map/ppermute | solution.py:116
  42.2 14.8 %collective-permute-start.1 = (bf16[528,512]{1,0:T(8,128)(2,1)}, bf16[528,512]{1,0:T(8,128)(2,1)S(1)}, u32[]{:S(2)}, u32[]{:S(2)}) collective-permute-start(bf16[528,512]{1,0:T(8,128)(2,1)} %fusion.77), channel_id=1, source_target_pairs={{0,3},{1,0},{2,1},{3,2},{4,7},{5,4},{6,5},{7,6},{8,11},{9,8},{10,9... | collective-permute-start | bytes 1622024 | tf_op jit(solution)/shard_map/ppermute | solution.py:117
  55.9 11.9 %collective-permute-start.2 = (bf16[272,512]{1,0:T(8,128)(2,1)S(1)}, bf16[272,512]{1,0:T(8,128)(2,1)}, u32[]{:S(2)}, u32[]{:S(2)}) collective-permute-start(bf16[272,512]{1,0:T(8,128)(2,1)S(1)} %slice.147), channel_id=1, source_target_pairs={{0,1},{1,2},{2,3},{3,0},{4,5},{5,6},{6,7},{7,4},{8,9},{9,10},{10,1... | collective-permute-start | bytes 835592 | tf_op jit(solution)/shard_map/ppermute | solution.py:120
  58.6 10.3 %collective-permute-start.3 = (bf16[256,512]{1,0:T(8,128)(2,1)}, bf16[256,512]{1,0:T(8,128)(2,1)}, u32[]{:S(2)}, u32[]{:S(2)}) collective-permute-start(bf16[256,512]{1,0:T(8,128)(2,1)} %slice.151), channel_id=1, source_target_pairs={{0,3},{1,0},{2,1},{3,2},{4,7},{5,4},{6,5},{7,6},{8,11},{9,8},{10,9... | collective-permute-start | bytes 786440 | tf_op jit(solution)/shard_map/ppermute | solution.py:119
  72.5 7.5 %collective-permute-start.4 = (bf16[64,1024]{1,0:T(8,128)(2,1)S(1)}, bf16[64,1024]{1,0:T(8,128)(2,1)S(1)}, u32[]{:S(2)}, u32[]{:S(2)}) collective-permute-start(bf16[64,1024]{1,0:T(8,128)(2,1)S(1)} %get-tuple-element.11), channel_id=1, source_target_pairs={{0,1},{1,2},{2,3},{3,0},{4,5},{5,6},{6,7},{7,4},{8,9},{9,10},{10,1... | collective-permute-start | bytes 393224 | tf_op jit(solution)/shard_map/ppermute | solution.py:31
  72.8 7.2 %collective-permute-start.5 = (bf16[64,1024]{1,0:T(8,128)(2,1)S(1)}, bf16[64,1024]{1,0:T(8,128)(2,1)S(1)}, u32[]{:S(2)}, u32[]{:S(2)}) collective-permute-start(bf16[64,1024]{1,0:T(8,128)(2,1)S(1)} %get-tuple-element.12), channel_id=1, source_target_pairs={{0,2},{1,3},{2,0},{3,1},{4,6},{5,7},{6,4},{7,5},{8,10},{9,11},{10,... | collective-permute-start | bytes 393224 | tf_op jit(solution)/shard_map/ppermute | solution.py:31
  74.2 6.2 %collective-permute-start.6 = (bf16[64,1024]{1,0:T(8,128)(2,1)S(1)}, bf16[64,1024]{1,0:T(8,128)(2,1)S(1)}, u32[]{:S(2)}, u32[]{:S(2)}) collective-permute-start(bf16[64,1024]{1,0:T(8,128)(2,1)S(1)} %get-tuple-element.13), channel_id=1, source_target_pairs={{0,3},{1,0},{2,1},{3,2},{4,7},{5,4},{6,5},{7,6},{8,11},{9,8},{10,9... | collective-permute-start | bytes 393224 | tf_op jit(solution)/shard_map/ppermute | solution.py:31
  80.5 8.8 %copy-start.12 = (bf16[3,1024,256]{2,1,0:T(8,128)(2,1)S(1)}, bf16[3,1024,256]{2,1,0:T(8,128)(2,1)}, u32[]{:S(2)}) copy-start(bf16[3,1024,256]{2,1,0:T(8,128)(2,1)} %param.28) | copy-start | bytes 4718596
  80.5 5.5 %collective-permute-start.7 = (bf16[64,1024]{1,0:T(8,128)(2,1)S(1)}, bf16[64,1024]{1,0:T(8,128)(2,1)S(1)}, u32[]{:S(2)}, u32[]{:S(2)}) collective-permute-start(bf16[64,1024]{1,0:T(8,128)(2,1)S(1)} %get-tuple-element.5), channel_id=1, source_target_pairs={{0,3},{1,0},{2,1},{3,2},{4,7},{5,4},{6,5},{7,6},{8,11},{9,8},{10,9... | collective-permute-start | bytes 393224 | tf_op jit(solution)/shard_map/ppermute | solution.py:39
  82.8 5.4 %collective-permute-start.8 = (bf16[64,1024]{1,0:T(8,128)(2,1)S(1)}, bf16[64,1024]{1,0:T(8,128)(2,1)S(1)}, u32[]{:S(2)}, u32[]{:S(2)}) collective-permute-start(bf16[64,1024]{1,0:T(8,128)(2,1)S(1)} %get-tuple-element.5), channel_id=1, source_target_pairs={{0,2},{1,3},{2,0},{3,1},{4,6},{5,7},{6,4},{7,5},{8,10},{9,11},{10,... | collective-permute-start | bytes 393224 | tf_op jit(solution)/shard_map/ppermute | solution.py:39
  82.8 6.4 %collective-permute-start.9 = (bf16[64,1024]{1,0:T(8,128)(2,1)S(1)}, bf16[64,1024]{1,0:T(8,128)(2,1)S(1)}, u32[]{:S(2)}, u32[]{:S(2)}) collective-permute-start(bf16[64,1024]{1,0:T(8,128)(2,1)S(1)} %get-tuple-element.5), channel_id=1, source_target_pairs={{0,1},{1,2},{2,3},{3,0},{4,5},{5,6},{6,7},{7,4},{8,9},{9,10},{10,1... | collective-permute-start | bytes 393224 | tf_op jit(solution)/shard_map/ppermute | solution.py:39
  91.6 15.0 %copy-start.6 = (bf16[256,256]{1,0:T(8,128)(2,1)}, bf16[256,256]{1,0:T(8,128)(2,1)S(1)}, u32[]{:S(2)}) copy-start(bf16[256,256]{1,0:T(8,128)(2,1)S(1)} %fusion.103) | copy-start | bytes 393220
  91.6 11.1 %copy-start.8 = (s32[256,10]{0,1:T(8,128)S(1)}, s32[256,10]{0,1:T(8,128)}, u32[]{:S(2)}) copy-start(s32[256,10]{0,1:T(8,128)} %param.33) | copy-start | bytes 30724
  93.2 13.4 %copy-start.5 = (bf16[256,1024]{1,0:T(8,128)(2,1)S(1)}, bf16[256,1024]{1,0:T(8,128)(2,1)}, u32[]{:S(2)}) copy-start(bf16[256,1024]{1,0:T(8,128)(2,1)} %param.36) | copy-start | bytes 1572868
  93.2 13.4 %copy-start.11 = (s32[256]{0:T(256)S(1)}, s32[256]{0:T(256)}, u32[]{:S(2)}) copy-start(s32[256]{0:T(256)} %param.34) | copy-start | bytes 3076
  93.2 37.7 %all-to-all-start.1 = ((bf16[64,32,256]{2,1,0:T(8,128)(2,1)}), bf16[64,32,256]{2,1,0:T(8,128)(2,1)S(1)}, u32[]{:S(2)}, u32[]{:S(2)}) async-start(bf16[64,32,256]{2,1,0:T(8,128)(2,1)} %bitcast.111), calls=%async_computation.1 | async-start | bytes 2097152 | tf_op jit(solution)/shard_map/all_to_all | solution.py:181
  133.8 7.2 %collective-permute-start.10 = (bf16[64,1024]{1,0:T(8,128)(2,1)S(1)}, bf16[64,1024]{1,0:T(8,128)(2,1)S(1)}, u32[]{:S(2)}, u32[]{:S(2)}) collective-permute-start(bf16[64,1024]{1,0:T(8,128)(2,1)S(1)} %get-tuple-element.8), channel_id=1, source_target_pairs={{0,1},{1,2},{2,3},{3,0},{4,5},{5,6},{6,7},{7,4},{8,9},{9,10},{10,1... | collective-permute-start | bytes 393224 | tf_op jit(solution)/shard_map/ppermute | solution.py:31
  133.9 7.2 %collective-permute-start.11 = (bf16[64,1024]{1,0:T(8,128)(2,1)S(1)}, bf16[64,1024]{1,0:T(8,128)(2,1)S(1)}, u32[]{:S(2)}, u32[]{:S(2)}) collective-permute-start(bf16[64,1024]{1,0:T(8,128)(2,1)S(1)} %get-tuple-element.9), channel_id=1, source_target_pairs={{0,2},{1,3},{2,0},{3,1},{4,6},{5,7},{6,4},{7,5},{8,10},{9,11},{10,... | collective-permute-start | bytes 393224 | tf_op jit(solution)/shard_map/ppermute | solution.py:31
  135.7 6.5 %collective-permute-start.12 = (bf16[64,1024]{1,0:T(8,128)(2,1)S(1)}, bf16[64,1024]{1,0:T(8,128)(2,1)S(1)}, u32[]{:S(2)}, u32[]{:S(2)}) collective-permute-start(bf16[64,1024]{1,0:T(8,128)(2,1)S(1)} %get-tuple-element.10), channel_id=1, source_target_pairs={{0,3},{1,0},{2,1},{3,2},{4,7},{5,4},{6,5},{7,6},{8,11},{9,8},{10,9... | collective-permute-start | bytes 393224 | tf_op jit(solution)/shard_map/ppermute | solution.py:31
  (8 other events, 38.8 us)
